TPU v7x, 256 devices: a whole 4x4x8 slice. The times are simulated.
256 devices in a mesh: svc: 32 (over y_lo, z, core), tm: 8 (over y_hi, x).
Axes of the slice: x: 4, y: 4 (y_hi: 2, y_lo: 2; y = y_hi * 2 + y_lo), z: 8, core: 2. Of those that a mesh axis runs over, the one named last changes fastest.
Arguments:
- metrics: bfloat16 [8192, 4096], P('svc', 'tm'), may hold values from -15 to 15
- band_starts: int32 [4], replicated, may hold values from 1 to 2015
Outputs:
- cross: bfloat16 [4, 2, 8192, 8192], P(None, None, 'svc', 'tm')
- coherence: float32 [4, 8192, 8192], P(None, 'svc', 'tm')
Inputs may be any that keep to these rules, and one draw needn't show every extreme that they name: `band_starts`: each band covers 32 consecutive bins starting at its entry.
All inputs are finite; a program needn't handle non-finite values.
Results may differ from a plain program's by a relative error of at most 0.0066.
Values may be sent and summed in bfloat16 or wider, within the bound.
No kernel may reach another device: no remote copies, remote signals or barrier semaphores. Data moves between devices by JAX's collectives and lax.ppermute only.
A program may use at most 64 MiB of HBM per device.

v0:
```python
import jax
import jax.numpy as jnp
from jax import lax
from jax.sharding import PartitionSpec as P

TLEN = 4096
BANDS = 4
BINS = 32


epsilon = 1e-06


def make_table(minutes, band_starts):
    offsets = jnp.arange(BINS, dtype=jnp.int32)
    freqs = band_starts[:, None] + offsets[None, :]
    phase_index = minutes[:, None, None] * freqs[None, :, :] % TLEN
    phases = 2.0 * jnp.pi / TLEN * phase_index.astype(jnp.float32)
    norm = 1.0 / jnp.sqrt(jnp.float32(TLEN))
    stacked = jnp.stack([jnp.cos(phases) * norm, -jnp.sin(phases) * norm], axis=2)
    return stacked.reshape(minutes.shape[0], BANDS * 2 * BINS).astype(jnp.bfloat16)


def band_products(row_spec, col_spec):
    swapped = jnp.concatenate([row_spec[:, BINS:], -row_spec[:, :BINS]], axis=1)
    dims = (((1,), (1,)), ((), ()))
    real_part = lax.dot_general(row_spec, col_spec, dims, preferred_element_type=jnp.float32) / BINS
    imag_part = lax.dot_general(swapped, col_spec, dims, preferred_element_type=jnp.float32) / BINS
    row_power = jnp.sum(jnp.square(row_spec.astype(jnp.float32)), axis=1) / BINS
    col_power = jnp.sum(jnp.square(col_spec.astype(jnp.float32)), axis=1) / BINS
    coherence = (real_part * real_part + imag_part * imag_part) / (
        (row_power[:, None] + epsilon) * (col_power[None, :] + epsilon)
    )
    cross = jnp.stack([real_part, imag_part], axis=0).astype(jnp.bfloat16)
    return (cross, coherence)


def body(metrics, band_starts):
    row_count = metrics.shape[0]
    local_minutes = metrics.shape[1]
    time_index = lax.axis_index("tm")
    minutes = time_index * local_minutes + jnp.arange(local_minutes, dtype=jnp.int32)
    dft_table = make_table(minutes, band_starts)
    partial_value = jnp.dot(metrics, dft_table, preferred_element_type=jnp.float32)
    spectra = lax.psum(partial_value, "tm").astype(jnp.bfloat16)
    owners = lax.axis_size("svc") // lax.axis_size("tm")
    col_count = row_count * owners
    gathered = lax.all_gather(spectra, "svc", axis=0, tiled=True)
    columns_panel = lax.dynamic_slice_in_dim(gathered, time_index * col_count, col_count, 0)
    cross_list = []
    coherence_list = []
    for band in range(BANDS):
        offset = band * 2 * BINS
        row_spec = spectra[:, offset : offset + 2 * BINS]
        col_spec = columns_panel[:, offset : offset + 2 * BINS]
        cross, coherence = band_products(row_spec, col_spec)
        cross_list.append(cross)
        coherence_list.append(coherence)
    return (jnp.stack(cross_list, axis=0), jnp.stack(coherence_list, axis=0))


def solution(mesh):
    return jax.shard_map(
        body,
        mesh=mesh,
        in_specs=(P("svc", "tm"), P()),
        out_specs=(P(None, None, "svc", "tm"), P(None, "svc", "tm")),
        check_vma=False,
    )
```

profile of v0, /device:TPU:1, one launch (start us, length us, event | category | flops | bytes accessed | tf_op | source)
XLA Modules:
  0.0 150.9 jit_solution(4337779228758525286)
XLA Ops:
  7.2 0.0 copy-start
  7.2 0.0 all-gather.2.cloned.1.call-start
  7.2 0.8 iota_add_fusion
  8.0 1.2 multiply_convert_fusion.1
  9.3 0.0 copy-done
  9.3 0.3 convolution_bitcast_fusion
  9.5 38.9 %all-reduce.1 = bf16[256,256]{0,1:T(8,128)(2,1)} all-reduce(f32[256,256]{0,1:T(8,128)S(1)} %convolution_bitcast_fusion), channel_id=1, replica_groups=mesh['svc'=32,'tm'=8] {'tm'}, use_global_device_ids=true, to_apply=%region_0.1 | all-reduce | flops 65536 | bytes 393216 | tf_op jit(solution)/shard_map/psum | solution.py:45
  48.5 0.0 copy-start.1
  48.5 0.0 all-gather.2.cloned.1.call-update
  48.5 0.9 multiply_reduce_fusion.7
  49.4 0.9 fusion.33
  50.3 77.2 %all-gather.2.cloned.1.call-done = bf16[8192,256]{0,1:T(8,128)(2,1)} async-done(((bf16[256,256]{0,1:T(8,128)(2,1)}), bf16[8192,256]{0,1:T(8,128)(2,1)}) %all-gather.2.cloned.1.call-update) | async-done | bytes 4194320 | tf_op jit(solution)/shard_map/all_gather | solution.py:48
  127.4 1.2 multiply_reduce_fusion.3
  128.7 1.2 convolution_multiply_fusion
  129.9 1.2 convolution_multiply_fusion.2
  131.2 1.2 convolution_multiply_fusion.4
  132.4 1.2 convolution_multiply_fusion.6
  133.6 0.0 copy-done.1
  133.6 1.4 divide_bitcast_fusion
  135.0 1.4 divide_bitcast_fusion.1
  136.4 1.4 divide_bitcast_fusion.2
  137.8 1.4 divide_bitcast_fusion.3
  139.2 2.3 %pad_maximum_fusion = f32[4,256,1024]{2,1,0:T(8,128)} fusion(f32[1,256,1024]{2,1,0:T(8,128)S(1)} %get-tuple-element.19, f32[1,256,1024]{2,1,0:T(8,128)S(1)} %get-tuple-element.16, f32[1,256,1024]{2,1,0:T(8,128)S(1)} %get-tuple-element.13, f32[1,256,1024]{2,1,0:T(8,128)S(1)} %get-tuple-element.10), kind=kLoop, calls=%fused_computation.1 | loop fusion | flops 3145728 | bytes 8388608 | tf_op jit(solution)/shard_map/stack | solution.py:59
  141.5 2.6 %maximum_maximum_fusion = bf16[4,2,256,1024]{3,2,1,0:T(8,128)(2,1)} fusion(bf16[1,1,256,1024]{3,2,1,0:T(8,128)(2,1)S(1)} %get-tuple-element.21, bf16[1,1,256,1024]{3,2,1,0:T(8,128)(2,1)S(1)} %get-tuple-element.20, bf16[1,1,256,1024]{3,2,1,0:T(8,128)(2,1)S(1)} %get-tuple-element.18, bf16[1,1,256,1024]{3,2,1,0:T(8,128)(2,1)S(1)} %get-tuple-element.17, ...), kind=kLoop, calls=%fused_computation | loop fusion | flops 14680064 | bytes 8388608 | tf_op jit(solution)/shard_map/stack | solution.py:59
  (6 shorter events, 0.1 us)
Async XLA Ops:
  7.2 2.1 %copy-start = (bf16[256,512]{1,0:T(8,128)(2,1)S(1)}, bf16[256,512]{1,0:T(8,128)(2,1)}, u32[]{:S(2)}) copy-start(bf16[256,512]{1,0:T(8,128)(2,1)} %param.2) | copy-start | bytes 786436
  7.2 120.3 %all-gather.2.cloned.1.call-start = ((), (), s32[]{:S(2)}) async-start(), calls=%async_computation | async-start | bytes 4325376 | tf_op jit(solution)/shard_map/all_gather | solution.py:48
  48.5 85.2 %copy-start.1 = (bf16[256,256]{0,1:T(8,128)(2,1)S(1)}, bf16[256,256]{0,1:T(8,128)(2,1)}, u32[]{:S(2)}) copy-start(bf16[256,256]{0,1:T(8,128)(2,1)} %all-reduce.1) | copy-start | bytes 393220
Sparse Core Ops, SparseCore 0:
  48.6 78.7 all-gather.1
where the time goes:
time: 151 us
  waiting for transfers between devices  77.2 us (51%)
  blocking collectives  38.9 us (26%)
  between operations  14.2 us (9%)
  matrix products  10.7 us (7%)
  other arithmetic  9.9 us (7%)
    all_gather x1, waiting for transfers between devices, body(): gathered = lax.all_gather(spectra, 'svc', axis=0, tiled=True)  77.2 us
    psum x1, blocking collectives, body(): spectra = lax.psum(partial_value, 'tm').astype(jnp.bfloat16)  38.9 us
    dot_general x4, matrix products, band_products(): lax.dot_general(row_spec, col_spec, dims, preferred_element_type=jnp.floa...  5.53 us
    another operation x2, other arithmetic, body(): return (jnp.stack(cross_list, axis=0), jnp.stack(coherence_list, axis=0))  4.9 us
    dot_general x4, matrix products, band_products(): lax.dot_general(swapped, col_spec, dims, preferred_element_type=jnp.float32)  4.89 us
  transfers between devices with their start and end apart: 1, of which 1 were waited for; matrix products, arithmetic and copies ran while one was open for 1% of the time, Pallas kernels for 0%

commit v1 on v0

--- a/solution.py
+++ b/solution.py
@@ -38,15 +38,35 @@
 def body(metrics, band_starts):
     row_count = metrics.shape[0]
     local_minutes = metrics.shape[1]
+    n_tm = lax.axis_size("tm")
+    n_svc = lax.axis_size("svc")
+    owners = n_svc // n_tm
+    width = BANDS * 2 * BINS
+    chunk = width // n_tm
     time_index = lax.axis_index("tm")
     minutes = time_index * local_minutes + jnp.arange(local_minutes, dtype=jnp.int32)
-    dft_table = make_table(minutes, band_starts)
-    partial_value = jnp.dot(metrics, dft_table, preferred_element_type=jnp.float32)
-    spectra = lax.psum(partial_value, "tm").astype(jnp.bfloat16)
-    owners = lax.axis_size("svc") // lax.axis_size("tm")
-    col_count = row_count * owners
-    gathered = lax.all_gather(spectra, "svc", axis=0, tiled=True)
-    columns_panel = lax.dynamic_slice_in_dim(gathered, time_index * col_count, col_count, 0)
+    dft_table = make_table(minutes, band_starts).reshape(local_minutes, n_tm, chunk)
+    partial_value = jnp.einsum(
+        "nt,tcb->cnb", metrics, dft_table, preferred_element_type=jnp.float32
+    )
+    piece = lax.psum_scatter(partial_value, "tm", scatter_dimension=0, tiled=True)
+    piece = piece.astype(jnp.bfloat16)
+    row_chunks = lax.all_gather(piece, "tm", axis=0, tiled=True)
+    spectra = jnp.transpose(row_chunks, (1, 0, 2)).reshape(row_count, width)
+    perm = []
+    for s_src in range(n_svc):
+        g_src, r_src = divmod(s_src, owners)
+        for t_src in range(n_tm):
+            s_dst = t_src * owners + r_src
+            t_dst = g_src
+            perm.append((s_src * n_tm + t_src, s_dst * n_tm + t_dst))
+    moved = lax.ppermute(piece, ("svc", "tm"), perm)
+    col_chunks = lax.all_gather(moved, "svc", axis=0, tiled=True)
+    columns_panel = (
+        col_chunks.reshape(n_tm, owners, row_count, chunk)
+        .transpose(1, 2, 0, 3)
+        .reshape(owners * row_count, width)
+    )
     cross_list = []
     coherence_list = []
     for band in range(BANDS):

time: 151 us -> 182 us (1.21)
  blocking collectives: 38.9 us -> 75.7 us
  matrix products: 10.7 us -> 3.91 us
  waiting for transfers between devices: 77.2 us -> 79.3 us
  other arithmetic: 9.9 us -> 7.89 us
    reduce_scatter x0 -> x1, waiting for transfers between devices: none -> 79.3 us  [body(): lax.psum_scatter(partial_value, 'tm', scatter_dimension=0, tiled=True)]
    all_gather x1 -> x0, waiting for transfers between devices: 77.2 us -> none  [body(): gathered = lax.all_gather(spectra, 'svc', axis=0, tiled=True)]
    all_gather x0 -> x2, blocking collectives: none -> 75.7 us  [the longest x1 41.4 us: body(): col_chunks = lax.all_gather(moved, 'svc', axis=0, tiled=True)]
    psum x1 -> x0, blocking collectives: 38.9 us -> none  [body(): spectra = lax.psum(partial_value, 'tm').astype(jnp.bfloat16)]
    dot_general x4, matrix products: 5.53 us -> 1.7 us  [band_products(): lax.dot_general(row_spec, col_spec, dims, preferred_element_type=jnp.floa...]
    dot_general x4, matrix products: 4.89 us -> 1.26 us  [band_products(): lax.dot_general(swapped, col_spec, dims, preferred_element_type=jnp.float32)]
  transfers between devices with their start and end apart: 1 -> 2, of which waited for: 1 -> 1; matrix products, arithmetic and copies ran while one was open for 1% -> 0% of each run, Pallas kernels for 0% -> 0%
where the time goes in v1:
time: 182 us
  waiting for transfers between devices  79.3 us (44%)
  blocking collectives  75.7 us (42%)
  between operations  14.2 us (8%)
  other arithmetic  7.89 us (4%)
  matrix products  3.91 us (2%)
    reduce_scatter x1, waiting for transfers between devices, body(): lax.psum_scatter(partial_value, 'tm', scatter_dimension=0, tiled=True)  79.3 us
    all_gather x1, blocking collectives, body(): col_chunks = lax.all_gather(moved, 'svc', axis=0, tiled=True)  41.4 us
    all_gather x1, blocking collectives, body(): row_chunks = lax.all_gather(piece, 'tm', axis=0, tiled=True)  34.3 us
    another operation x2, other arithmetic, body(): return (jnp.stack(cross_list, axis=0), jnp.stack(coherence_list, axis=0))  4.9 us
  transfers between devices with their start and end apart: 2, of which 1 were waited for; matrix products, arithmetic and copies ran while one was open for 0% of the time, Pallas kernels for 0%

profile of v1, /device:TPU:1, one launch (start us, length us, event | category | flops | bytes accessed | tf_op | source)
XLA Modules:
  0.0 182.2 jit_solution(15294440074042725612)
XLA Ops:
  7.2 0.0 copy-start
  7.2 0.0 reduce-scatter.2.cloned.1.call-start
  7.2 0.8 iota_add_fusion
  8.0 1.2 multiply_convert_fusion.1
  9.3 0.0 copy-done
  9.3 1.0 convolution_bitcast_fusion
  10.2 0.0 reduce-scatter.2.cloned.1.call-update
  10.3 79.3 %reduce-scatter.2.cloned.1.call-done = f32[1,256,32]{1,2,0:T(8,128)} async-done(((f32[8,256,32]{1,2,0:T(8,128)}), f32[1,256,32]{1,2,0:T(8,128)}) %reduce-scatter.2.cloned.1.call-update) | async-done | bytes 32784 | tf_op jit(solution)/shard_map/reduce_scatter | solution.py:52
  89.6 0.8 convert_element_type.80
  90.3 0.7 collective-permute-start
  91.0 34.3 %all_gather.6 = bf16[8,256,32]{1,2,0:T(8,128)(2,1)S(1)} all-gather(bf16[1,256,32]{1,2,0:T(8,128)(2,1)S(1)} %convert_element_type.80), channel_id=1, replica_groups=mesh['svc'=32,'tm'=8] {'tm'}, dimensions={0}, use_global_device_ids=true | all-gather | bytes 147456 | tf_op jit(solution)/shard_map/all_gather | solution.py:54
  125.4 0.0 collective-permute-done
  125.4 41.4 %all_gather.7 = bf16[32,256,32]{1,2,0:T(8,128)(2,1)S(1)} all-gather(bf16[1,256,32]{1,2,0:T(8,128)(2,1)S(1)} %collective-permute-done), channel_id=1, replica_groups=mesh['svc'=32,'tm'=8] {'svc'}, dimensions={0}, use_global_device_ids=true | all-gather | bytes 540672 | tf_op jit(solution)/shard_map/all_gather | solution.py:64
  166.8 0.4 copy.5
  167.2 0.1 copy.6
  167.3 0.1 multiply_reduce_fusion.3
  167.5 0.3 convolution_multiply_fusion.6
  167.8 0.3 convolution_multiply_fusion.2
  168.1 0.3 convolution_multiply_fusion
  168.4 0.3 convolution_multiply_fusion.4
  168.8 0.4 divide_bitcast_fusion.2
  169.2 0.4 divide_bitcast_fusion
  169.6 0.4 divide_bitcast_fusion.1
  170.1 0.4 divide_bitcast_fusion.3
  170.5 2.3 %pad_maximum_fusion = f32[4,256,1024]{2,1,0:T(8,128)} fusion(f32[1,256,1024]{2,1,0:T(8,128)S(1)} %get-tuple-element.19, f32[1,256,1024]{2,1,0:T(8,128)S(1)} %get-tuple-element.16, f32[1,256,1024]{2,1,0:T(8,128)S(1)} %get-tuple-element.13, f32[1,256,1024]{2,1,0:T(8,128)S(1)} %get-tuple-element.10), kind=kLoop, calls=%fused_computation.1 | loop fusion | flops 3145728 | bytes 8388608 | tf_op jit(solution)/shard_map/stack | solution.py:79
  172.8 2.6 %maximum_maximum_fusion = bf16[4,2,256,1024]{3,2,1,0:T(8,128)(2,1)} fusion(bf16[1,1,256,1024]{3,2,1,0:T(8,128)(2,1)S(1)} %get-tuple-element.21, bf16[1,1,256,1024]{3,2,1,0:T(8,128)(2,1)S(1)} %get-tuple-element.20, bf16[1,1,256,1024]{3,2,1,0:T(8,128)(2,1)S(1)} %get-tuple-element.18, bf16[1,1,256,1024]{3,2,1,0:T(8,128)(2,1)S(1)} %get-tuple-element.17, ...), kind=kLoop, calls=%fused_computation | loop fusion | flops 14680064 | bytes 8388608 | tf_op jit(solution)/shard_map/stack | solution.py:79
  (8 shorter events, 0.1 us)
Async XLA Ops:
  7.2 2.1 %copy-start = (bf16[256,512]{1,0:T(8,128)(2,1)S(1)}, bf16[256,512]{1,0:T(8,128)(2,1)}, u32[]{:S(2)}) copy-start(bf16[256,512]{1,0:T(8,128)(2,1)} %param.2) | copy-start | bytes 786436
  7.2 82.4 %reduce-scatter.2.cloned.1.call-start = ((), (), s32[]{:S(2)}) async-start(), calls=%async_computation.1 | async-start | bytes 294912 | tf_op jit(solution)/shard_map/reduce_scatter | solution.py:52
  90.3 35.0 %collective-permute-start = (bf16[1,256,32]{1,2,0:T(8,128)(2,1)S(1)}, bf16[1,256,32]{1,2,0:T(8,128)(2,1)S(1)}, u32[]{:S(2)}, u32[]{:S(2)}) collective-permute-start(bf16[1,256,32]{1,2,0:T(8,128)(2,1)S(1)} %convert_element_type.80), channel_id=1, source_target_pairs={{0,0},{1,32},{2,64},{3,96},{4,128},{5,160},{6,192},{7,224},{8,8},{... | collective-permute-start | bytes 49160 | tf_op jit(solution)/shard_map/ppermute | solution.py:63
Sparse Core Ops, SparseCore 0:
  12.4 77.0 reduce-scatter.1

commit v2 on v1

v2 whole, which is shorter than its diff:
```python
import jax
import jax.numpy as jnp
from jax import lax
from jax.sharding import PartitionSpec as P

TLEN = 4096
BANDS = 4
BINS = 32


epsilon = 1e-06


def make_table(minutes, band_starts):
    offsets = jnp.arange(BINS, dtype=jnp.int32)
    freqs = band_starts[:, None] + offsets[None, :]
    phase_index = minutes[:, None, None] * freqs[None, :, :] % TLEN
    phases = 2.0 * jnp.pi / TLEN * phase_index.astype(jnp.float32)
    norm = 1.0 / jnp.sqrt(jnp.float32(TLEN))
    stacked = jnp.stack([jnp.cos(phases) * norm, -jnp.sin(phases) * norm], axis=2)
    return stacked.reshape(minutes.shape[0], BANDS * 2 * BINS).astype(jnp.bfloat16)


def all_bands(row_spec, col_spec):
    swapped = jnp.concatenate([row_spec[..., BINS:], -row_spec[..., :BINS]], axis=-1)
    lhs = jnp.stack([row_spec, swapped], axis=1)
    cross_f32 = jnp.einsum("bpik,bjk->bpij", lhs, col_spec, preferred_element_type=jnp.float32) / BINS
    row_power = jnp.sum(jnp.square(row_spec.astype(jnp.float32)), axis=-1) / BINS
    col_power = jnp.sum(jnp.square(col_spec.astype(jnp.float32)), axis=-1) / BINS
    real_part = cross_f32[:, 0]
    imag_part = cross_f32[:, 1]
    coherence = (real_part * real_part + imag_part * imag_part) / (
        (row_power[:, :, None] + epsilon) * (col_power[:, None, :] + epsilon)
    )
    return (cross_f32.astype(jnp.bfloat16), coherence)


def gather_by_all_to_all(x, axis, size):
    return lax.all_to_all(jnp.broadcast_to(x, (size,) + x.shape[1:]), axis, 0, 0, tiled=True)


def body(metrics, band_starts):
    row_count = metrics.shape[0]
    local_minutes = metrics.shape[1]
    n_tm = lax.axis_size("tm")
    n_svc = lax.axis_size("svc")
    owners = n_svc // n_tm
    width = BANDS * 2 * BINS
    chunk = width // n_tm
    time_index = lax.axis_index("tm")
    minutes = time_index * local_minutes + jnp.arange(local_minutes, dtype=jnp.int32)
    dft_table = make_table(minutes, band_starts).reshape(local_minutes, n_tm, chunk)
    partial_value = jnp.einsum(
        "nt,tcb->cnb", metrics, dft_table, preferred_element_type=jnp.float32
    )
    partials = lax.all_to_all(partial_value, "tm", 0, 0, tiled=True)
    piece = jnp.sum(partials, axis=0, keepdims=True).astype(jnp.bfloat16)
    perm = []
    for s_src in range(n_svc):
        g_src, r_src = divmod(s_src, owners)
        for t_src in range(n_tm):
            s_dst = t_src * owners + r_src
            t_dst = g_src
            perm.append((s_src * n_tm + t_src, s_dst * n_tm + t_dst))
    moved = lax.ppermute(piece, ("svc", "tm"), perm)
    row_chunks = gather_by_all_to_all(piece, "tm", n_tm)
    col_chunks = gather_by_all_to_all(moved, "svc", n_svc)
    bands_row = row_chunks.reshape(BANDS, 2, row_count, BINS)
    row_spec = jnp.transpose(bands_row, (0, 2, 1, 3)).reshape(BANDS, row_count, 2 * BINS)
    bands_col = col_chunks.reshape(BANDS, 2, owners, row_count, BINS)
    col_spec = jnp.transpose(bands_col, (0, 2, 3, 1, 4)).reshape(BANDS, owners * row_count, 2 * BINS)
    return all_bands(row_spec, col_spec)


def solution(mesh):
    return jax.shard_map(
        body,
        mesh=mesh,
        in_specs=(P("svc", "tm"), P()),
        out_specs=(P(None, None, "svc", "tm"), P(None, "svc", "tm")),
        check_vma=False,
    )
```

time: 182 us -> 71 us (0.39)
  blocking collectives: 75.7 us -> 15.1 us
  waiting for transfers between devices: 79.3 us -> 22.7 us
  starting transfers between devices: 0.69 us -> 20.7 us
  between operations: 14.2 us -> 0.76 us
  other arithmetic: 7.89 us -> 4.77 us
    reduce_scatter x1 -> x0, waiting for transfers between devices: 79.3 us -> none  [body(): lax.psum_scatter(partial_value, 'tm', scatter_dimension=0, tiled=True)]
    all_gather x2 -> x0, blocking collectives: 75.7 us -> none  [the longest x1 41.4 us: body(): col_chunks = lax.all_gather(moved, 'svc', axis=0, tiled=True)]
    all_to_all x0 -> x2, waiting for transfers between devices: none -> 22.7 us  [gather_by_all_to_all(): lax.all_to_all(jnp.broadcast_to(x, (size,) + x.shape[1:]), axis, 0, 0, ti...]
    all_to_all x0 -> x2, starting transfers between devices: none -> 20 us  [gather_by_all_to_all(): lax.all_to_all(jnp.broadcast_to(x, (size,) + x.shape[1:]), axis, 0, 0, ti...]
    all_to_all x0 -> x1, blocking collectives: none -> 15.1 us  [body(): partials = lax.all_to_all(partial_value, 'tm', 0, 0, tiled=True)]
    another operation x3 -> x2, other arithmetic: 6.12 us -> 1.23 us  [the longest x2 4.9 us: body(): return (jnp.stack(cross_list, axis=0), jnp.stack(coherence_list, axis=0))]
    div x0 -> x1, other arithmetic: none -> 2.5 us  [all_bands(): (real_part * real_part + imag_part * imag_part) / ((row_power[:, :, None]...]
  transfers between devices with their start and end apart: 2 -> 3, of which waited for: 1 -> 2; matrix products, arithmetic and copies ran while one was open for 0% -> 0% of each run, Pallas kernels for 0% -> 0%
where the time goes in v2:
time: 71 us; the launch traced here: 69.8 us
  waiting for transfers between devices  22.7 us (32%)
  starting transfers between devices  20.7 us (29%)
  blocking collectives  15.1 us (21%)
  other arithmetic  4.77 us (7%)
  matrix products  3.57 us (5%)
  local copies, waits for them, and re-layouts  2.31 us (3%)
  between operations  0.76 us (1%)
    all_to_all x2, waiting for transfers between devices, gather_by_all_to_all(): lax.all_to_all(jnp.broadcast_to(x, (size,) + x.shape[1:]), axis, 0, 0, ti...  22.7 us
    all_to_all x2, starting transfers between devices, gather_by_all_to_all(): lax.all_to_all(jnp.broadcast_to(x, (size,) + x.shape[1:]), axis, 0, 0, ti...  20 us
    all_to_all x1, blocking collectives, body(): partials = lax.all_to_all(partial_value, 'tm', 0, 0, tiled=True)  15.1 us
    dot_general x1, matrix products, all_bands(): jnp.einsum('bpik,bjk->bpij', lhs, col_spec, preferred_element_type=jnp.fl...  3.31 us
    div x1, other arithmetic, all_bands(): (real_part * real_part + imag_part * imag_part) / ((row_power[:, :, None]...  2.5 us
    broadcast_in_dim x2, local copies, waits for them, and re-layouts, gather_by_all_to_all(): jnp.broadcast_to(x, (size,) + x.shape[1:])  1.52 us
  transfers between devices with their start and end apart: 3, of which 2 were waited for; matrix products, arithmetic and copies ran while one was open for 0% of the time, Pallas kernels for 0%

profile of v2, /device:TPU:1, one launch (start us, length us, event | category | flops | bytes accessed | tf_op | source)
XLA Modules:
  0.0 69.8 jit_solution(15752689819290285066)
XLA Ops:
  0.6 0.0 copy-start
  0.7 0.8 %iota_add_fusion = s32[4,32]{1,0:T(4,128)S(1)} fusion(s32[4]{0:T(128)} %param.3), kind=kLoop, calls=%fused_computation.29 | loop fusion | flops 128 | bytes 528 | tf_op jit(solution)/shard_map/add | solution.py:16
  1.4 1.2 %multiply_convert_fusion.1 = (bf16[512,4,1,32]{0,3,2,1:T(8,128)(2,1)S(1)}, bf16[512,4,1,32]{0,3,2,1:T(8,128)(2,1)S(1)}) fusion(s32[4,32]{1,0:T(4,128)S(1)} %iota_add_fusion, s32[512]{0:T(512)S(1)} %iota_add_fusion.1), kind=kLoop, calls=%fused_computation.24 | loop fusion | flops 1245184 | bytes 264704 | tf_op jit(solution)/shard_map/convert
  2.7 0.0 copy-done
  2.7 0.3 convolution_bitcast_fusion
  3.0 15.1 %all_to_all.15 = f32[8,256,32]{1,2,0:T(8,128)S(1)} all-to-all(f32[8,256,32]{1,2,0:T(8,128)S(1)} %convolution_bitcast_fusion), channel_id=1, replica_groups=mesh['svc'=32,'tm'=8] {'tm'}, dimensions={0} | all-to-all | bytes 524288 | tf_op jit(solution)/shard_map/all_to_all | solution.py:56
  18.1 0.7 broadcast_in_dim.6
  18.7 3.4 %all-to-all-start.1 = ((bf16[8,256,32]{1,2,0:T(8,128)(2,1)}), bf16[8,256,32]{1,2,0:T(8,128)(2,1)S(1)}, u32[]{:S(2)}, u32[]{:S(2)}) async-start(bf16[8,256,32]{1,2,0:T(8,128)(2,1)} %broadcast_in_dim.6), calls=%async_computation.1 | async-start | bytes 262144 | tf_op jit(solution)/shard_map/all_to_all | solution.py:39
  22.1 0.7 collective-permute-start
  22.8 0.0 collective-permute-done
  22.8 6.2 %all-to-all-done.1 = bf16[8,256,32]{1,2,0:T(8,128)(2,1)S(1)} async-done(((bf16[8,256,32]{1,2,0:T(8,128)(2,1)}), bf16[8,256,32]{1,2,0:T(8,128)(2,1)S(1)}, u32[]{:S(2)}, u32[]{:S(2)}) %all-to-all-start.1) | async-done | bytes 131104 | tf_op jit(solution)/shard_map/all_to_all | solution.py:39
  29.0 0.9 %broadcast_in_dim.8 = bf16[32,256,32]{1,2,0:T(8,128)(2,1)} broadcast(bf16[256,32]{0,1:T(8,128)(2,1)S(1)} %bitcast.43), dimensions={1,2} | broadcast | bytes 540672 | tf_op jit(solution)/shard_map/broadcast_in_dim | solution.py:39
  29.8 16.6 %all-to-all-start.2 = ((bf16[32,256,32]{1,2,0:T(8,128)(2,1)}), bf16[32,256,32]{1,2,0:T(8,128)(2,1)S(1)}, u32[]{:S(2)}, u32[]{:S(2)}) async-start(bf16[32,256,32]{1,2,0:T(8,128)(2,1)} %broadcast_in_dim.8), calls=%async_computation.2 | async-start | bytes 1048576 | tf_op jit(solution)/shard_map/all_to_all | solution.py:39
  46.6 16.5 %all-to-all-done.2 = bf16[32,256,32]{1,2,0:T(8,128)(2,1)S(1)} async-done(((bf16[32,256,32]{1,2,0:T(8,128)(2,1)}), bf16[32,256,32]{1,2,0:T(8,128)(2,1)S(1)}, u32[]{:S(2)}, u32[]{:S(2)}) %all-to-all-start.2) | async-done | bytes 524320 | tf_op jit(solution)/shard_map/all_to_all | solution.py:39
  63.1 0.1 multiply_reduce_fusion
  63.2 0.4 copy.5
  63.6 0.4 reshape.134
  64.0 3.3 %fusion.13 = (bf16[4,2,256,1024]{3,2,1,0:T(8,128)(2,1)}, f32[4,2,256,1024]{3,2,1,0:T(8,128)S(1)}) fusion(bf16[4,1024,64,1]{1,2,0,3:T(8,128)(2,1)S(1)} %reshape.134, bf16[4,1,256,64]{2,3,1,0:T(8,128)(2,1)S(1)} %maximum_bitcast_fusion, bf16[4,1,256,64]{2,3,1,0:T(8,128)(2,1)S(1)} %bitcast.39), kind=kOutput, calls=%fused_computation.33 | convolution fusion | flops 272760832 | bytes 13369344 | tf_op jit(solution)/shard_map/bpik,bjk->bpij/dot_general | solution.py:27
  67.3 2.5 %fusion.2 = f32[4,256,1024]{2,1,0:T(8,128)} fusion(f32[4,2,256,1024]{3,2,1,0:T(8,128)S(1)} %get-tuple-element.7, f32[4,1024]{1,0:T(4,128)S(1)} %bitcast.41, f32[4,256]{1,0:T(4,128)S(1)} %multiply_add_fusion), kind=kLoop, calls=%fused_computation.3 | loop fusion | flops 5242880 | bytes 12603392 | tf_op jit(solution)/shard_map/div | solution.py:32
  (9 shorter events, 0.1 us)
Async XLA Ops:
  0.6 2.1 %copy-start = (bf16[256,512]{1,0:T(8,128)(2,1)S(1)}, bf16[256,512]{1,0:T(8,128)(2,1)}, u32[]{:S(2)}) copy-start(bf16[256,512]{1,0:T(8,128)(2,1)} %param.2) | copy-start | bytes 786436
  18.7 10.3 %all-to-all-start.1 = ((bf16[8,256,32]{1,2,0:T(8,128)(2,1)}), bf16[8,256,32]{1,2,0:T(8,128)(2,1)S(1)}, u32[]{:S(2)}, u32[]{:S(2)}) async-start(bf16[8,256,32]{1,2,0:T(8,128)(2,1)} %broadcast_in_dim.6), calls=%async_computation.1 | async-start | bytes 262144 | tf_op jit(solution)/shard_map/all_to_all | solution.py:39
  22.1 0.7 collective-permute-start
  29.8 33.2 %all-to-all-start.2 = ((bf16[32,256,32]{1,2,0:T(8,128)(2,1)}), bf16[32,256,32]{1,2,0:T(8,128)(2,1)S(1)}, u32[]{:S(2)}, u32[]{:S(2)}) async-start(bf16[32,256,32]{1,2,0:T(8,128)(2,1)} %broadcast_in_dim.8), calls=%async_computation.2 | async-start | bytes 1048576 | tf_op jit(solution)/shard_map/all_to_all | solution.py:39

commit v3 on v2

--- a/solution.py
+++ b/solution.py
@@ -1,6 +1,8 @@
 import jax
 import jax.numpy as jnp
 from jax import lax
+from jax.experimental import pallas as pl
+from jax.experimental.pallas import tpu as pltpu
 from jax.sharding import PartitionSpec as P
 
 TLEN = 4096
@@ -21,18 +23,59 @@
     return stacked.reshape(minutes.shape[0], BANDS * 2 * BINS).astype(jnp.bfloat16)
 
 
-def all_bands(row_spec, col_spec):
-    swapped = jnp.concatenate([row_spec[..., BINS:], -row_spec[..., :BINS]], axis=-1)
-    lhs = jnp.stack([row_spec, swapped], axis=1)
-    cross_f32 = jnp.einsum("bpik,bjk->bpij", lhs, col_spec, preferred_element_type=jnp.float32) / BINS
-    row_power = jnp.sum(jnp.square(row_spec.astype(jnp.float32)), axis=-1) / BINS
-    col_power = jnp.sum(jnp.square(col_spec.astype(jnp.float32)), axis=-1) / BINS
-    real_part = cross_f32[:, 0]
-    imag_part = cross_f32[:, 1]
-    coherence = (real_part * real_part + imag_part * imag_part) / (
-        (row_power[:, :, None] + epsilon) * (col_power[:, None, :] + epsilon)
+def cross_kernel(row_ref, col_ref, row_power_ref, col_power_ref, cross_ref, coherence_ref):
+    row_re = row_ref[0]
+    row_im = row_ref[1]
+    col_re = col_ref[0]
+    col_im = col_ref[1]
+    dims = (((1,), (1,)), ((), ()))
+
+    def dot(a, b):
+        return lax.dot_general(a, b, dims, preferred_element_type=jnp.float32)
+
+    real_part = (dot(row_re, col_re) + dot(row_im, col_im)) / BINS
+    imag_part = (dot(row_im, col_re) - dot(row_re, col_im)) / BINS
+    cross_ref[0, 0] = real_part.astype(cross_ref.dtype)
+    cross_ref[0, 1] = imag_part.astype(cross_ref.dtype)
+    coherence_ref[0] = (real_part * real_part + imag_part * imag_part) / (
+        (row_power_ref[0] + epsilon) * (col_power_ref[0] + epsilon)
     )
-    return (cross_f32.astype(jnp.bfloat16), coherence)
+
+
+def all_bands(row_chunks, col_chunks):
+    parts, rows, bins = row_chunks.shape
+    cols = col_chunks.shape[1]
+    bands = parts // 2
+    tile = 128
+    row_power = jnp.sum(
+        jnp.square(row_chunks.astype(jnp.float32)).reshape(bands, 2, rows, bins), axis=(1, 3)
+    ) / BINS
+    col_power = jnp.sum(
+        jnp.square(col_chunks.astype(jnp.float32)).reshape(bands, 2, cols, bins), axis=(1, 3)
+    ) / BINS
+    return pl.pallas_call(
+        cross_kernel,
+        grid=(bands, rows // tile),
+        in_specs=[
+            pl.BlockSpec((2, tile, bins), lambda b, i: (b, i, 0)),
+            pl.BlockSpec((2, cols, bins), lambda b, i: (b, 0, 0)),
+            pl.BlockSpec((1, tile, 1), lambda b, i: (b, i, 0)),
+            pl.BlockSpec((1, 1, cols), lambda b, i: (b, 0, 0)),
+        ],
+        out_specs=[
+            pl.BlockSpec((1, 2, tile, cols), lambda b, i: (b, 0, i, 0)),
+            pl.BlockSpec((1, tile, cols), lambda b, i: (b, i, 0)),
+        ],
+        out_shape=[
+            jax.ShapeDtypeStruct((bands, 2, rows, cols), jnp.bfloat16),
+            jax.ShapeDtypeStruct((bands, rows, cols), jnp.float32),
+        ],
+        cost_estimate=pl.CostEstimate(
+            flops=8 * bands * rows * cols * bins + 6 * bands * rows * cols,
+            transcendentals=0,
+            bytes_accessed=6 * bands * rows * cols,
+        ),
+    )(row_chunks, col_chunks, row_power[:, :, None], col_power[:, None, :])
 
 
 def gather_by_all_to_all(x, axis, size):
@@ -65,11 +108,8 @@
     moved = lax.ppermute(piece, ("svc", "tm"), perm)
     row_chunks = gather_by_all_to_all(piece, "tm", n_tm)
     col_chunks = gather_by_all_to_all(moved, "svc", n_svc)
-    bands_row = row_chunks.reshape(BANDS, 2, row_count, BINS)
-    row_spec = jnp.transpose(bands_row, (0, 2, 1, 3)).reshape(BANDS, row_count, 2 * BINS)
-    bands_col = col_chunks.reshape(BANDS, 2, owners, row_count, BINS)
-    col_spec = jnp.transpose(bands_col, (0, 2, 3, 1, 4)).reshape(BANDS, owners * row_count, 2 * BINS)
-    return all_bands(row_spec, col_spec)
+    col_chunks = col_chunks.reshape(n_tm, owners * row_count, chunk)
+    return all_bands(row_chunks, col_chunks)
 
 
 def solution(mesh):

time: 71 us -> 76 us (1.070)
  Pallas kernels: 0 us -> 9.1 us
  local copies, waits for them, and re-layouts: 2.31 us -> 6.01 us
  matrix products: 3.57 us -> 0.26 us
  other arithmetic: 4.77 us -> 2.32 us
  waiting for transfers between devices: 22.7 us -> 20.6 us
    pallas_call x0 -> x1, Pallas kernels: none -> 9.1 us  [all_bands(): pl.pallas_call(cross_kernel, grid=(bands, rows // tile), in_specs=[pl.Blo...]
    dot_general x1 -> x0, matrix products: 3.31 us -> none  [all_bands(): jnp.einsum('bpik,bjk->bpij', lhs, col_spec, preferred_element_type=jnp.fl...]
    all_to_all x0 -> x2, local copies, waits for them, and re-layouts: none -> 2.79 us  [gather_by_all_to_all(): lax.all_to_all(jnp.broadcast_to(x, (size,) + x.shape[1:]), axis, 0, 0, ti...]
    div x1 -> x2, other arithmetic: 2.5 us -> 0.01 us  [the longest x1 0.01 us: all_bands(): jnp.sum(jnp.square(col_chunks.astype(jnp.float32)).reshape(bands, 2, cols...]
    all_to_all x2, waiting for transfers between devices: 22.7 us -> 20.6 us  [gather_by_all_to_all(): lax.all_to_all(jnp.broadcast_to(x, (size,) + x.shape[1:]), axis, 0, 0, ti...]
    div x0 -> x2, local copies, waits for them, and re-layouts: none -> 1.65 us  [the longest x1 1.04 us: all_bands(): jnp.sum(jnp.square(row_chunks.astype(jnp.float32)).reshape(bands, 2, rows...]
  transfers between devices with their start and end apart: 3 -> 3, of which waited for: 2 -> 2; matrix products, arithmetic and copies ran while one was open for 0% -> 3% of each run, Pallas kernels for 0% -> 0%
where the time goes in v3:
time: 76 us; the launch traced here: 74.8 us
  starting transfers between devices  20.7 us (27%)
  waiting for transfers between devices  20.6 us (27%)
  blocking collectives  15.1 us (20%)
  Pallas kernels  9.1 us (12%)
  local copies, waits for them, and re-layouts  6.01 us (8%)
  other arithmetic  2.32 us (3%)
  between operations  0.76 us (1%)
    all_to_all x2, waiting for transfers between devices, gather_by_all_to_all(): lax.all_to_all(jnp.broadcast_to(x, (size,) + x.shape[1:]), axis, 0, 0, ti...  20.6 us
    all_to_all x2, starting transfers between devices, gather_by_all_to_all(): lax.all_to_all(jnp.broadcast_to(x, (size,) + x.shape[1:]), axis, 0, 0, ti...  20 us
    all_to_all x1, blocking collectives, body(): partials = lax.all_to_all(partial_value, 'tm', 0, 0, tiled=True)  15.1 us
    pallas_call x1, Pallas kernels, all_bands(): pl.pallas_call(cross_kernel, grid=(bands, rows // tile), in_specs=[pl.Blo...  9.1 us
    all_to_all x2, local copies, waits for them, and re-layouts, gather_by_all_to_all(): lax.all_to_all(jnp.broadcast_to(x, (size,) + x.shape[1:]), axis, 0, 0, ti...  2.79 us
  transfers between devices with their start and end apart: 3, of which 2 were waited for; matrix products, arithmetic and copies ran while one was open for 3% of the time, Pallas kernels for 0%

profile of v3, /device:TPU:1, one launch (start us, length us, event | category | flops | bytes accessed | tf_op | source)
XLA Modules:
  0.0 74.8 jit_solution(7963900302404073779)
XLA Ops:
  0.6 0.0 copy-start
  0.7 0.8 %iota_add_fusion = s32[4,32]{1,0:T(4,128)S(1)} fusion(s32[4]{0:T(128)} %param.3), kind=kLoop, calls=%fused_computation.17 | loop fusion | flops 128 | bytes 528 | tf_op jit(solution)/shard_map/add | solution.py:18
  1.4 1.2 %multiply_convert_fusion.1 = (bf16[512,4,1,32]{0,3,2,1:T(8,128)(2,1)S(1)}, bf16[512,4,1,32]{0,3,2,1:T(8,128)(2,1)S(1)}) fusion(s32[4,32]{1,0:T(4,128)S(1)} %iota_add_fusion, s32[512]{0:T(512)S(1)} %iota_add_fusion.1), kind=kLoop, calls=%fused_computation.14 | loop fusion | flops 1245184 | bytes 264704 | tf_op jit(solution)/shard_map/convert
  2.7 0.0 copy-done
  2.7 0.3 convolution_bitcast_fusion
  3.0 15.1 %all_to_all.15 = f32[8,256,32]{1,2,0:T(8,128)S(1)} all-to-all(f32[8,256,32]{1,2,0:T(8,128)S(1)} %convolution_bitcast_fusion), channel_id=1, replica_groups=mesh['svc'=32,'tm'=8] {'tm'}, dimensions={0} | all-to-all | bytes 524288 | tf_op jit(solution)/shard_map/all_to_all | solution.py:99
  18.1 0.7 broadcast_in_dim.6
  18.7 3.4 %all-to-all-start.1 = ((bf16[8,256,32]{1,2,0:T(8,128)(2,1)}), bf16[8,256,32]{1,2,0:T(8,128)(2,1)S(1)}, u32[]{:S(2)}, u32[]{:S(2)}) async-start(bf16[8,256,32]{1,2,0:T(8,128)(2,1)} %broadcast_in_dim.6), calls=%async_computation.1 | async-start | bytes 262144 | tf_op jit(solution)/shard_map/all_to_all | solution.py:82
  22.1 0.7 collective-permute-start
  22.8 0.0 collective-permute-done
  22.8 6.2 %all-to-all-done.1 = bf16[8,256,32]{1,2,0:T(8,128)(2,1)S(1)} async-done(((bf16[8,256,32]{1,2,0:T(8,128)(2,1)}), bf16[8,256,32]{1,2,0:T(8,128)(2,1)S(1)}, u32[]{:S(2)}, u32[]{:S(2)}) %all-to-all-start.1) | async-done | bytes 131104 | tf_op jit(solution)/shard_map/all_to_all | solution.py:82
  29.0 0.9 %broadcast_in_dim.8 = bf16[32,256,32]{1,2,0:T(8,128)(2,1)} broadcast(bf16[256,32]{0,1:T(8,128)(2,1)S(1)} %bitcast.15), dimensions={1,2} | broadcast | bytes 540672 | tf_op jit(solution)/shard_map/broadcast_in_dim | solution.py:82
  29.8 16.6 %all-to-all-start.2 = ((bf16[32,256,32]{1,2,0:T(8,128)(2,1)}), bf16[32,256,32]{1,2,0:T(8,128)(2,1)S(1)}, u32[]{:S(2)}, u32[]{:S(2)}) async-start(bf16[32,256,32]{1,2,0:T(8,128)(2,1)} %broadcast_in_dim.8), calls=%async_computation.2 | async-start | bytes 1048576 | tf_op jit(solution)/shard_map/all_to_all | solution.py:82
  46.6 1.0 %copy.15.row_power_ref = f32[4,256,1]{2,1,0:T(8,128)} copy(f32[4,256,1]{1,0,2:T(4,128)S(1)} %multiply_bitcast_fusion) | data formatting | bytes 8192 | tf_op jit(solution)/shard_map/div | solution.py:50
  47.6 1.0 %copy.14.row_ref = bf16[8,256,32]{2,1,0:T(8,128)(2,1)} copy(bf16[8,256,32]{1,2,0:T(8,128)(2,1)S(1)} %all-to-all-done.1) | data formatting | bytes 262144 | tf_op jit(solution)/shard_map/all_to_all | solution.py:82
  48.6 14.4 %all-to-all-done.2 = bf16[32,256,32]{1,2,0:T(8,128)(2,1)S(1)} async-done(((bf16[32,256,32]{1,2,0:T(8,128)(2,1)}), bf16[32,256,32]{1,2,0:T(8,128)(2,1)S(1)}, u32[]{:S(2)}, u32[]{:S(2)}) %all-to-all-start.2) | async-done | bytes 524320 | tf_op jit(solution)/shard_map/all_to_all | solution.py:82
  63.1 0.2 multiply_reduce_fusion
  63.3 0.6 div.21.col_power_ref
  63.9 1.8 %copy.11 = bf16[32,256,32]{2,1,0:T(8,128)(2,1)} copy(bf16[32,256,32]{1,2,0:T(8,128)(2,1)S(1)} %all-to-all-done.2) | data formatting | bytes 1048576 | tf_op jit(solution)/shard_map/all_to_all | solution.py:82
  65.7 9.1 %shard_map.41 = (bf16[4,2,256,1024]{3,2,1,0:T(8,128)(2,1)}, f32[4,256,1024]{2,1,0:T(8,128)}) custom-call(bf16[8,256,32]{2,1,0:T(8,128)(2,1)} %copy.14.row_ref, bf16[8,1024,32]{2,1,0:T(8,128)(2,1)} %bitcast.12, f32[4,256,1]{2,1,0:T(8,128)} %copy.15.row_power_ref, f32[4,1,1024]{2,1,0:T(1,128)} %div.21.col_power_ref), custom_call_target="tpu_custom_call" | custom-call | flops 274726912 | bytes 6291456 | tf_op jit(solution)/shard_map/pallas_call | solution.py:56
  (10 shorter events, 0.2 us)
Async XLA Ops:
  0.6 2.1 %copy-start = (bf16[256,512]{1,0:T(8,128)(2,1)S(1)}, bf16[256,512]{1,0:T(8,128)(2,1)}, u32[]{:S(2)}) copy-start(bf16[256,512]{1,0:T(8,128)(2,1)} %param.2) | copy-start | bytes 786436
  18.7 10.3 %all-to-all-start.1 = ((bf16[8,256,32]{1,2,0:T(8,128)(2,1)}), bf16[8,256,32]{1,2,0:T(8,128)(2,1)S(1)}, u32[]{:S(2)}, u32[]{:S(2)}) async-start(bf16[8,256,32]{1,2,0:T(8,128)(2,1)} %broadcast_in_dim.6), calls=%async_computation.1 | async-start | bytes 262144 | tf_op jit(solution)/shard_map/all_to_all | solution.py:82
  22.1 0.7 collective-permute-start
  29.8 33.2 %all-to-all-start.2 = ((bf16[32,256,32]{1,2,0:T(8,128)(2,1)}), bf16[32,256,32]{1,2,0:T(8,128)(2,1)S(1)}, u32[]{:S(2)}, u32[]{:S(2)}) async-start(bf16[32,256,32]{1,2,0:T(8,128)(2,1)} %broadcast_in_dim.8), calls=%async_computation.2 | async-start | bytes 1048576 | tf_op jit(solution)/shard_map/all_to_all | solution.py:82

commit v4 on v3

--- a/solution.py
+++ b/solution.py
@@ -23,44 +23,41 @@
     return stacked.reshape(minutes.shape[0], BANDS * 2 * BINS).astype(jnp.bfloat16)
 
 
-def cross_kernel(row_ref, col_ref, row_power_ref, col_power_ref, cross_ref, coherence_ref):
-    row_re = row_ref[0]
-    row_im = row_ref[1]
-    col_re = col_ref[0]
-    col_im = col_ref[1]
-    dims = (((1,), (1,)), ((), ()))
+def cross_kernel(row_ref, col_ref, cross_ref, coherence_ref):
+    row_re = row_ref[0].astype(jnp.float32)
+    row_im = row_ref[1].astype(jnp.float32)
+    col_re = col_ref[0].astype(jnp.float32)
+    col_im = col_ref[1].astype(jnp.float32)
 
     def dot(a, b):
-        return lax.dot_general(a, b, dims, preferred_element_type=jnp.float32)
+        return jnp.dot(a, b, preferred_element_type=jnp.float32)
 
-    real_part = (dot(row_re, col_re) + dot(row_im, col_im)) / BINS
-    imag_part = (dot(row_im, col_re) - dot(row_re, col_im)) / BINS
+    real_part = (dot(row_ref[0], col_ref[0]) + dot(row_ref[1], col_ref[1])) / BINS
+    imag_part = (dot(row_ref[1], col_ref[0]) - dot(row_ref[0], col_ref[1])) / BINS
+    row_power = (
+        jnp.sum(row_re * row_re, axis=1, keepdims=True) + jnp.sum(row_im * row_im, axis=1, keepdims=True)
+    ) / BINS
+    col_power = (
+        jnp.sum(col_re * col_re, axis=0, keepdims=True) + jnp.sum(col_im * col_im, axis=0, keepdims=True)
+    ) / BINS
     cross_ref[0, 0] = real_part.astype(cross_ref.dtype)
     cross_ref[0, 1] = imag_part.astype(cross_ref.dtype)
     coherence_ref[0] = (real_part * real_part + imag_part * imag_part) / (
-        (row_power_ref[0] + epsilon) * (col_power_ref[0] + epsilon)
+        (row_power + epsilon) * (col_power + epsilon)
     )
 
 
 def all_bands(row_chunks, col_chunks):
     parts, rows, bins = row_chunks.shape
-    cols = col_chunks.shape[1]
+    cols = col_chunks.shape[2]
     bands = parts // 2
     tile = 128
-    row_power = jnp.sum(
-        jnp.square(row_chunks.astype(jnp.float32)).reshape(bands, 2, rows, bins), axis=(1, 3)
-    ) / BINS
-    col_power = jnp.sum(
-        jnp.square(col_chunks.astype(jnp.float32)).reshape(bands, 2, cols, bins), axis=(1, 3)
-    ) / BINS
     return pl.pallas_call(
         cross_kernel,
         grid=(bands, rows // tile),
         in_specs=[
             pl.BlockSpec((2, tile, bins), lambda b, i: (b, i, 0)),
-            pl.BlockSpec((2, cols, bins), lambda b, i: (b, 0, 0)),
-            pl.BlockSpec((1, tile, 1), lambda b, i: (b, i, 0)),
-            pl.BlockSpec((1, 1, cols), lambda b, i: (b, 0, 0)),
+            pl.BlockSpec((2, bins, cols), lambda b, i: (b, 0, 0)),
         ],
         out_specs=[
             pl.BlockSpec((1, 2, tile, cols), lambda b, i: (b, 0, i, 0)),
@@ -75,7 +72,7 @@
             transcendentals=0,
             bytes_accessed=6 * bands * rows * cols,
         ),
-    )(row_chunks, col_chunks, row_power[:, :, None], col_power[:, None, :])
+    )(row_chunks, col_chunks)
 
 
 def gather_by_all_to_all(x, axis, size):
@@ -108,7 +105,7 @@
     moved = lax.ppermute(piece, ("svc", "tm"), perm)
     row_chunks = gather_by_all_to_all(piece, "tm", n_tm)
     col_chunks = gather_by_all_to_all(moved, "svc", n_svc)
-    col_chunks = col_chunks.reshape(n_tm, owners * row_count, chunk)
+    col_chunks = jnp.swapaxes(col_chunks.reshape(n_tm, owners * row_count, chunk), 1, 2)
     return all_bands(row_chunks, col_chunks)
 
 

time: 76 us -> 74.2 us (0.976)
  local copies, waits for them, and re-layouts: 6.01 us -> 4.23 us
  waiting for transfers between devices: 20.6 us -> 21.8 us
  Pallas kernels: 9.1 us -> 8.12 us
    div x2 -> x0, local copies, waits for them, and re-layouts: 1.65 us -> none  [the longest x1 1.04 us: all_bands(): jnp.sum(jnp.square(row_chunks.astype(jnp.float32)).reshape(bands, 2, rows...]
    all_to_all x2, local copies, waits for them, and re-layouts: 2.79 us -> 1.3 us  [gather_by_all_to_all(): lax.all_to_all(jnp.broadcast_to(x, (size,) + x.shape[1:]), axis, 0, 0, ti...]
    reshape x0 -> x2, local copies, waits for them, and re-layouts: none -> 1.41 us  [body(): col_chunks.reshape(n_tm, owners * row_count, chunk)]
    all_to_all x2, waiting for transfers between devices: 20.6 us -> 21.8 us  [gather_by_all_to_all(): lax.all_to_all(jnp.broadcast_to(x, (size,) + x.shape[1:]), axis, 0, 0, ti...]
    pallas_call x1, Pallas kernels: 9.1 us -> 8.12 us  [all_bands(): pl.pallas_call(cross_kernel, grid=(bands, rows // tile), in_specs=[pl.Blo...]
  transfers between devices with their start and end apart: 3 -> 3, of which waited for: 2 -> 2; matrix products, arithmetic and copies ran while one was open for 3% -> 1% of each run, Pallas kernels for 0% -> 0%
where the time goes in v4:
time: 74.2 us; the launch traced here: 72.9 us
  waiting for transfers between devices  21.8 us (29%)
  starting transfers between devices  20.7 us (28%)
  blocking collectives  15.1 us (20%)
  Pallas kernels  8.12 us (11%)
  local copies, waits for them, and re-layouts  4.23 us (6%)
  other arithmetic  2.04 us (3%)
    all_to_all x2, waiting for transfers between devices, gather_by_all_to_all(): lax.all_to_all(jnp.broadcast_to(x, (size,) + x.shape[1:]), axis, 0, 0, ti...  21.8 us
    all_to_all x2, starting transfers between devices, gather_by_all_to_all(): lax.all_to_all(jnp.broadcast_to(x, (size,) + x.shape[1:]), axis, 0, 0, ti...  20 us
    all_to_all x1, blocking collectives, body(): partials = lax.all_to_all(partial_value, 'tm', 0, 0, tiled=True)  15.1 us
    pallas_call x1, Pallas kernels, all_bands(): pl.pallas_call(cross_kernel, grid=(bands, rows // tile), in_specs=[pl.Blo...  8.12 us
    broadcast_in_dim x2, local copies, waits for them, and re-layouts, gather_by_all_to_all(): jnp.broadcast_to(x, (size,) + x.shape[1:])  1.52 us
  transfers between devices with their start and end apart: 3, of which 2 were waited for; matrix products, arithmetic and copies ran while one was open for 1% of the time, Pallas kernels for 0%

profile of v4, /device:TPU:1, one launch (start us, length us, event | category | flops | bytes accessed | tf_op | source)
XLA Modules:
  0.0 72.9 jit_solution(17556164479341030978)
XLA Ops:
  0.6 0.0 copy-start
  0.7 0.8 %iota_add_fusion = s32[4,32]{1,0:T(4,128)S(1)} fusion(s32[4]{0:T(128)} %param.3), kind=kLoop, calls=%fused_computation.14 | loop fusion | flops 128 | bytes 528 | tf_op jit(solution)/shard_map/add | solution.py:18
  1.4 1.2 %multiply_convert_fusion.1 = (bf16[512,4,1,32]{0,3,2,1:T(8,128)(2,1)S(1)}, bf16[512,4,1,32]{0,3,2,1:T(8,128)(2,1)S(1)}) fusion(s32[4,32]{1,0:T(4,128)S(1)} %iota_add_fusion, s32[512]{0:T(512)S(1)} %iota_add_fusion.1), kind=kLoop, calls=%fused_computation.13 | loop fusion | flops 1245184 | bytes 264704 | tf_op jit(solution)/shard_map/convert
  2.7 0.0 copy-done
  2.7 0.3 convolution_bitcast_fusion
  3.0 15.1 %all_to_all.15 = f32[8,256,32]{1,2,0:T(8,128)S(1)} all-to-all(f32[8,256,32]{1,2,0:T(8,128)S(1)} %convolution_bitcast_fusion), channel_id=1, replica_groups=mesh['svc'=32,'tm'=8] {'tm'}, dimensions={0} | all-to-all | bytes 524288 | tf_op jit(solution)/shard_map/all_to_all | solution.py:96
  18.1 0.7 broadcast_in_dim.6
  18.7 3.4 %all-to-all-start.1 = ((bf16[8,256,32]{1,2,0:T(8,128)(2,1)}), bf16[8,256,32]{1,2,0:T(8,128)(2,1)S(1)}, u32[]{:S(2)}, u32[]{:S(2)}) async-start(bf16[8,256,32]{1,2,0:T(8,128)(2,1)} %broadcast_in_dim.6), calls=%async_computation.1 | async-start | bytes 262144 | tf_op jit(solution)/shard_map/all_to_all | solution.py:79
  22.1 0.7 collective-permute-start
  22.8 0.0 collective-permute-done
  22.8 6.2 %all-to-all-done.1 = bf16[8,256,32]{1,2,0:T(8,128)(2,1)S(1)} async-done(((bf16[8,256,32]{1,2,0:T(8,128)(2,1)}), bf16[8,256,32]{1,2,0:T(8,128)(2,1)S(1)}, u32[]{:S(2)}, u32[]{:S(2)}) %all-to-all-start.1) | async-done | bytes 131104 | tf_op jit(solution)/shard_map/all_to_all | solution.py:79
  29.0 0.9 %broadcast_in_dim.8 = bf16[32,256,32]{1,2,0:T(8,128)(2,1)} broadcast(bf16[256,32]{0,1:T(8,128)(2,1)S(1)} %bitcast.17), dimensions={1,2} | broadcast | bytes 540672 | tf_op jit(solution)/shard_map/broadcast_in_dim | solution.py:79
  29.8 16.6 %all-to-all-start.2 = ((bf16[32,256,32]{1,2,0:T(8,128)(2,1)}), bf16[32,256,32]{1,2,0:T(8,128)(2,1)S(1)}, u32[]{:S(2)}, u32[]{:S(2)}) async-start(bf16[32,256,32]{1,2,0:T(8,128)(2,1)} %broadcast_in_dim.8), calls=%async_computation.2 | async-start | bytes 1048576 | tf_op jit(solution)/shard_map/all_to_all | solution.py:79
  46.5 1.0 %copy.8.row_ref = bf16[8,256,32]{2,1,0:T(8,128)(2,1)} copy(bf16[8,256,32]{1,2,0:T(8,128)(2,1)S(1)} %all-to-all-done.1) | data formatting | bytes 262144 | tf_op jit(solution)/shard_map/all_to_all | solution.py:79
  47.5 15.6 %all-to-all-done.2 = bf16[32,256,32]{1,2,0:T(8,128)(2,1)S(1)} async-done(((bf16[32,256,32]{1,2,0:T(8,128)(2,1)}), bf16[32,256,32]{1,2,0:T(8,128)(2,1)S(1)}, u32[]{:S(2)}, u32[]{:S(2)}) %all-to-all-start.2) | async-done | bytes 524320 | tf_op jit(solution)/shard_map/all_to_all | solution.py:79
  63.1 0.3 copy.6
  63.4 0.3 reshape.99
  63.7 1.1 %copy.10 = bf16[8,1024,32]{1,2,0:T(8,128)(2,1)} copy(bf16[8,1024,32]{1,0,2:T(8,128)(2,1)S(1)} %reshape.99) | data formatting | bytes 1048576 | tf_op jit(solution)/shard_map/reshape | solution.py:108
  64.8 8.1 %shard_map.41 = (bf16[4,2,256,1024]{3,2,1,0:T(8,128)(2,1)}, f32[4,256,1024]{2,1,0:T(8,128)}) custom-call(bf16[8,256,32]{2,1,0:T(8,128)(2,1)} %copy.8.row_ref, bf16[8,32,1024]{2,1,0:T(8,128)(2,1)} %bitcast.14), custom_call_target="tpu_custom_call" | custom-call | flops 274726912 | bytes 6291456 | tf_op jit(solution)/shard_map/pallas_call | solution.py:55
  (3 shorter events, 0.1 us)
Async XLA Ops:
  0.6 2.1 %copy-start = (bf16[256,512]{1,0:T(8,128)(2,1)S(1)}, bf16[256,512]{1,0:T(8,128)(2,1)}, u32[]{:S(2)}) copy-start(bf16[256,512]{1,0:T(8,128)(2,1)} %param.2) | copy-start | bytes 786436
  18.7 10.3 %all-to-all-start.1 = ((bf16[8,256,32]{1,2,0:T(8,128)(2,1)}), bf16[8,256,32]{1,2,0:T(8,128)(2,1)S(1)}, u32[]{:S(2)}, u32[]{:S(2)}) async-start(bf16[8,256,32]{1,2,0:T(8,128)(2,1)} %broadcast_in_dim.6), calls=%async_computation.1 | async-start | bytes 262144 | tf_op jit(solution)/shard_map/all_to_all | solution.py:79
  22.1 0.7 collective-permute-start
  29.8 33.2 %all-to-all-start.2 = ((bf16[32,256,32]{1,2,0:T(8,128)(2,1)}), bf16[32,256,32]{1,2,0:T(8,128)(2,1)S(1)}, u32[]{:S(2)}, u32[]{:S(2)}) async-start(bf16[32,256,32]{1,2,0:T(8,128)(2,1)} %broadcast_in_dim.8), calls=%async_computation.2 | async-start | bytes 1048576 | tf_op jit(solution)/shard_map/all_to_all | solution.py:79

commit v5 on v4

--- a/solution.py
+++ b/solution.py
@@ -23,23 +23,15 @@
     return stacked.reshape(minutes.shape[0], BANDS * 2 * BINS).astype(jnp.bfloat16)
 
 
-def cross_kernel(row_ref, col_ref, cross_ref, coherence_ref):
-    row_re = row_ref[0].astype(jnp.float32)
-    row_im = row_ref[1].astype(jnp.float32)
-    col_re = col_ref[0].astype(jnp.float32)
-    col_im = col_ref[1].astype(jnp.float32)
-
-    def dot(a, b):
-        return jnp.dot(a, b, preferred_element_type=jnp.float32)
-
-    real_part = (dot(row_ref[0], col_ref[0]) + dot(row_ref[1], col_ref[1])) / BINS
-    imag_part = (dot(row_ref[1], col_ref[0]) - dot(row_ref[0], col_ref[1])) / BINS
-    row_power = (
-        jnp.sum(row_re * row_re, axis=1, keepdims=True) + jnp.sum(row_im * row_im, axis=1, keepdims=True)
-    ) / BINS
-    col_power = (
-        jnp.sum(col_re * col_re, axis=0, keepdims=True) + jnp.sum(col_im * col_im, axis=0, keepdims=True)
-    ) / BINS
+def cross_kernel(lhs_ref, rhs_ref, cross_ref, coherence_ref):
+    row_spec = lhs_ref[0, 0]
+    col_spec = rhs_ref[0]
+    real_part = jnp.dot(row_spec, col_spec, preferred_element_type=jnp.float32) / BINS
+    imag_part = jnp.dot(lhs_ref[0, 1], col_spec, preferred_element_type=jnp.float32) / BINS
+    row_values = row_spec.astype(jnp.float32)
+    col_values = col_spec.astype(jnp.float32)
+    row_power = jnp.sum(row_values * row_values, axis=1, keepdims=True) / BINS
+    col_power = jnp.sum(col_values * col_values, axis=0, keepdims=True) / BINS
     cross_ref[0, 0] = real_part.astype(cross_ref.dtype)
     cross_ref[0, 1] = imag_part.astype(cross_ref.dtype)
     coherence_ref[0] = (real_part * real_part + imag_part * imag_part) / (
@@ -47,17 +39,18 @@
     )
 
 
-def all_bands(row_chunks, col_chunks):
-    parts, rows, bins = row_chunks.shape
-    cols = col_chunks.shape[2]
-    bands = parts // 2
+def all_bands(row_spec, col_spec):
+    bands, rows, depth = row_spec.shape
+    cols = col_spec.shape[2]
+    swapped = jnp.concatenate([row_spec[..., BINS:], -row_spec[..., :BINS]], axis=-1)
+    lhs = jnp.stack([row_spec, swapped], axis=1)
     tile = 128
     return pl.pallas_call(
         cross_kernel,
         grid=(bands, rows // tile),
         in_specs=[
-            pl.BlockSpec((2, tile, bins), lambda b, i: (b, i, 0)),
-            pl.BlockSpec((2, bins, cols), lambda b, i: (b, 0, 0)),
+            pl.BlockSpec((1, 2, tile, depth), lambda b, i: (b, 0, i, 0)),
+            pl.BlockSpec((1, depth, cols), lambda b, i: (b, 0, 0)),
         ],
         out_specs=[
             pl.BlockSpec((1, 2, tile, cols), lambda b, i: (b, 0, i, 0)),
@@ -68,11 +61,11 @@
             jax.ShapeDtypeStruct((bands, rows, cols), jnp.float32),
         ],
         cost_estimate=pl.CostEstimate(
-            flops=8 * bands * rows * cols * bins + 6 * bands * rows * cols,
+            flops=4 * bands * rows * cols * depth + 6 * bands * rows * cols,
             transcendentals=0,
             bytes_accessed=6 * bands * rows * cols,
         ),
-    )(row_chunks, col_chunks)
+    )(lhs, col_spec)
 
 
 def gather_by_all_to_all(x, axis, size):
@@ -105,8 +98,11 @@
     moved = lax.ppermute(piece, ("svc", "tm"), perm)
     row_chunks = gather_by_all_to_all(piece, "tm", n_tm)
     col_chunks = gather_by_all_to_all(moved, "svc", n_svc)
-    col_chunks = jnp.swapaxes(col_chunks.reshape(n_tm, owners * row_count, chunk), 1, 2)
-    return all_bands(row_chunks, col_chunks)
+    bands_row = row_chunks.reshape(BANDS, 2, row_count, BINS)
+    row_spec = jnp.transpose(bands_row, (0, 2, 1, 3)).reshape(BANDS, row_count, 2 * BINS)
+    col_spec = jnp.swapaxes(col_chunks.reshape(BANDS, 2, owners * row_count, BINS), 2, 3)
+    col_spec = col_spec.reshape(BANDS, 2 * BINS, owners * row_count)
+    return all_bands(row_spec, col_spec)
 
 
 def solution(mesh):

time: 74.2 us -> 73.3 us (0.988)
  other arithmetic: 2.04 us -> 3.14 us
    reshape x2 -> x1, local copies, waits for them, and re-layouts: 1.41 us -> 0.2 us  [body(): col_chunks.reshape(BANDS, 2, owners * row_count, BINS)]
    transpose x0 -> x1, local copies, waits for them, and re-layouts: none -> 1.08 us  [body(): jnp.swapaxes(col_chunks.reshape(BANDS, 2, owners * row_count, BINS), 2, 3)]
    another operation x1 -> x3, other arithmetic: 1.22 us -> 2.27 us
    all_to_all x2 -> x1, local copies, waits for them, and re-layouts: 1.3 us -> 0.29 us  [gather_by_all_to_all(): lax.all_to_all(jnp.broadcast_to(x, (size,) + x.shape[1:]), axis, 0, 0, ti...]
  transfers between devices with their start and end apart: 3 -> 3, of which waited for: 2 -> 2; matrix products, arithmetic and copies ran while one was open for 1% -> 2% of each run, Pallas kernels for 0% -> 0%
where the time goes in v5:
time: 73.3 us; the launch traced here: 72.1 us
  waiting for transfers between devices  21.1 us (29%)
  starting transfers between devices  20.7 us (28%)
  blocking collectives  15.1 us (21%)
  Pallas kernels  7.41 us (10%)
  local copies, waits for them, and re-layouts  3.63 us (5%)
  other arithmetic  3.14 us (4%)
  between operations  0.77 us (1%)
    all_to_all x2, waiting for transfers between devices, gather_by_all_to_all(): lax.all_to_all(jnp.broadcast_to(x, (size,) + x.shape[1:]), axis, 0, 0, ti...  21.1 us
    all_to_all x2, starting transfers between devices, gather_by_all_to_all(): lax.all_to_all(jnp.broadcast_to(x, (size,) + x.shape[1:]), axis, 0, 0, ti...  20 us
    all_to_all x1, blocking collectives, body(): partials = lax.all_to_all(partial_value, 'tm', 0, 0, tiled=True)  15.1 us
    pallas_call x1, Pallas kernels, all_bands(): pl.pallas_call(cross_kernel, grid=(bands, rows // tile), in_specs=[pl.Blo...  7.41 us
    broadcast_in_dim x2, local copies, waits for them, and re-layouts, gather_by_all_to_all(): jnp.broadcast_to(x, (size,) + x.shape[1:])  1.52 us
  transfers between devices with their start and end apart: 3, of which 2 were waited for; matrix products, arithmetic and copies ran while one was open for 2% of the time, Pallas kernels for 0%

profile of v5, /device:TPU:1, one launch (start us, length us, event | category | flops | bytes accessed | tf_op | source)
XLA Modules:
  0.0 72.1 jit_solution(87987775590177149)
XLA Ops:
  0.6 0.0 copy-start
  0.7 0.8 %iota_add_fusion = s32[4,32]{1,0:T(4,128)S(1)} fusion(s32[4]{0:T(128)} %param.3), kind=kLoop, calls=%fused_computation.15 | loop fusion | flops 128 | bytes 528 | tf_op jit(solution)/shard_map/add | solution.py:18
  1.4 1.2 %multiply_convert_fusion.1 = (bf16[512,4,1,32]{0,3,2,1:T(8,128)(2,1)S(1)}, bf16[512,4,1,32]{0,3,2,1:T(8,128)(2,1)S(1)}) fusion(s32[4,32]{1,0:T(4,128)S(1)} %iota_add_fusion, s32[512]{0:T(512)S(1)} %iota_add_fusion.1), kind=kLoop, calls=%fused_computation.14 | loop fusion | flops 1245184 | bytes 264704 | tf_op jit(solution)/shard_map/convert
  2.7 0.0 copy-done
  2.7 0.3 convolution_bitcast_fusion
  3.0 15.1 %all_to_all.15 = f32[8,256,32]{1,2,0:T(8,128)S(1)} all-to-all(f32[8,256,32]{1,2,0:T(8,128)S(1)} %convolution_bitcast_fusion), channel_id=1, replica_groups=mesh['svc'=32,'tm'=8] {'tm'}, dimensions={0} | all-to-all | bytes 524288 | tf_op jit(solution)/shard_map/all_to_all | solution.py:89
  18.1 0.7 broadcast_in_dim.6
  18.7 3.4 %all-to-all-start.1 = ((bf16[8,256,32]{1,2,0:T(8,128)(2,1)}), bf16[8,256,32]{1,2,0:T(8,128)(2,1)S(1)}, u32[]{:S(2)}, u32[]{:S(2)}) async-start(bf16[8,256,32]{1,2,0:T(8,128)(2,1)} %broadcast_in_dim.6), calls=%async_computation.1 | async-start | bytes 262144 | tf_op jit(solution)/shard_map/all_to_all | solution.py:72
  22.1 0.7 collective-permute-start
  22.8 0.0 collective-permute-done
  22.8 6.2 %all-to-all-done.1 = bf16[8,256,32]{1,2,0:T(8,128)(2,1)S(1)} async-done(((bf16[8,256,32]{1,2,0:T(8,128)(2,1)}), bf16[8,256,32]{1,2,0:T(8,128)(2,1)S(1)}, u32[]{:S(2)}, u32[]{:S(2)}) %all-to-all-start.1) | async-done | bytes 131104 | tf_op jit(solution)/shard_map/all_to_all | solution.py:72
  29.0 0.9 %broadcast_in_dim.8 = bf16[32,256,32]{1,2,0:T(8,128)(2,1)} broadcast(bf16[256,32]{0,1:T(8,128)(2,1)S(1)} %bitcast.28), dimensions={1,2} | broadcast | bytes 540672 | tf_op jit(solution)/shard_map/broadcast_in_dim | solution.py:72
  29.8 16.6 %all-to-all-start.2 = ((bf16[32,256,32]{1,2,0:T(8,128)(2,1)}), bf16[32,256,32]{1,2,0:T(8,128)(2,1)S(1)}, u32[]{:S(2)}, u32[]{:S(2)}) async-start(bf16[32,256,32]{1,2,0:T(8,128)(2,1)} %broadcast_in_dim.8), calls=%async_computation.2 | async-start | bytes 1048576 | tf_op jit(solution)/shard_map/all_to_all | solution.py:72
  46.5 0.2 copy.13
  46.7 0.2 copy.14
  46.9 0.1 neg.14
  46.9 0.2 copy.10
  47.1 0.1 maximum_bitcast_fusion
  47.3 0.9 %pad_maximum_fusion.lhs_ref = bf16[4,2,256,64]{3,2,1,0:T(8,128)(2,1)} fusion(bf16[4,1,256,64]{3,2,1,0:T(8,128)(2,1)S(1)} %maximum_bitcast_fusion, bf16[4,1,256,64]{3,2,1,0:T(8,128)(2,1)S(1)} %copy.10), kind=kLoop, calls=%fused_computation.1 | loop fusion | flops 131072 | bytes 524288 | tf_op jit(solution)/shard_map/stack | solution.py:46
  48.2 14.9 %all-to-all-done.2 = bf16[32,256,32]{1,2,0:T(8,128)(2,1)S(1)} async-done(((bf16[32,256,32]{1,2,0:T(8,128)(2,1)}), bf16[32,256,32]{1,2,0:T(8,128)(2,1)S(1)}, u32[]{:S(2)}, u32[]{:S(2)}) %all-to-all-start.2) | async-done | bytes 524320 | tf_op jit(solution)/shard_map/all_to_all | solution.py:72
  63.1 0.3 copy.11
  63.4 0.2 reshape.110
  63.6 1.1 %copy.12 = bf16[4,2,32,1024]{3,2,1,0:T(8,128)(2,1)} copy(bf16[4,2,32,1024]{3,1,0,2:T(2,128)(2,1)S(1)} %bitcast.23) | data formatting | bytes 1048576 | tf_op jit(solution)/shard_map/transpose | solution.py:103
  64.6 7.4 %shard_map.41 = (bf16[4,2,256,1024]{3,2,1,0:T(8,128)(2,1)}, f32[4,256,1024]{2,1,0:T(8,128)}) custom-call(bf16[4,2,256,64]{3,2,1,0:T(8,128)(2,1)} %pad_maximum_fusion.lhs_ref, bf16[4,64,1024]{2,1,0:T(8,128)(2,1)} %bitcast.22), custom_call_target="tpu_custom_call" | custom-call | flops 274726912 | bytes 6291456 | tf_op jit(solution)/shard_map/pallas_call | solution.py:48
  (4 shorter events, 0.1 us)
Async XLA Ops:
  0.6 2.1 %copy-start = (bf16[256,512]{1,0:T(8,128)(2,1)S(1)}, bf16[256,512]{1,0:T(8,128)(2,1)}, u32[]{:S(2)}) copy-start(bf16[256,512]{1,0:T(8,128)(2,1)} %param.2) | copy-start | bytes 786436
  18.7 10.3 %all-to-all-start.1 = ((bf16[8,256,32]{1,2,0:T(8,128)(2,1)}), bf16[8,256,32]{1,2,0:T(8,128)(2,1)S(1)}, u32[]{:S(2)}, u32[]{:S(2)}) async-start(bf16[8,256,32]{1,2,0:T(8,128)(2,1)} %broadcast_in_dim.6), calls=%async_computation.1 | async-start | bytes 262144 | tf_op jit(solution)/shard_map/all_to_all | solution.py:72
  22.1 0.7 collective-permute-start
  29.8 33.2 %all-to-all-start.2 = ((bf16[32,256,32]{1,2,0:T(8,128)(2,1)}), bf16[32,256,32]{1,2,0:T(8,128)(2,1)S(1)}, u32[]{:S(2)}, u32[]{:S(2)}) async-start(bf16[32,256,32]{1,2,0:T(8,128)(2,1)} %broadcast_in_dim.8), calls=%async_computation.2 | async-start | bytes 1048576 | tf_op jit(solution)/shard_map/all_to_all | solution.py:72

commit v6 on v5

--- a/solution.py
+++ b/solution.py
@@ -26,17 +26,18 @@
 def cross_kernel(lhs_ref, rhs_ref, cross_ref, coherence_ref):
     row_spec = lhs_ref[0, 0]
     col_spec = rhs_ref[0]
-    real_part = jnp.dot(row_spec, col_spec, preferred_element_type=jnp.float32) / BINS
-    imag_part = jnp.dot(lhs_ref[0, 1], col_spec, preferred_element_type=jnp.float32) / BINS
+    scale = 1.0 / BINS
+    real_part = jnp.dot(row_spec, col_spec, preferred_element_type=jnp.float32) * scale
+    imag_part = jnp.dot(lhs_ref[0, 1], col_spec, preferred_element_type=jnp.float32) * scale
     row_values = row_spec.astype(jnp.float32)
     col_values = col_spec.astype(jnp.float32)
-    row_power = jnp.sum(row_values * row_values, axis=1, keepdims=True) / BINS
-    col_power = jnp.sum(col_values * col_values, axis=0, keepdims=True) / BINS
+    row_power = jnp.sum(row_values * row_values, axis=1, keepdims=True) * scale
+    col_power = jnp.sum(col_values * col_values, axis=0, keepdims=True) * scale
     cross_ref[0, 0] = real_part.astype(cross_ref.dtype)
     cross_ref[0, 1] = imag_part.astype(cross_ref.dtype)
-    coherence_ref[0] = (real_part * real_part + imag_part * imag_part) / (
-        (row_power + epsilon) * (col_power + epsilon)
-    )
+    row_inverse = 1.0 / (row_power + epsilon)
+    col_inverse = 1.0 / (col_power + epsilon)
+    coherence_ref[0] = (real_part * real_part + imag_part * imag_part) * row_inverse * col_inverse
 
 
 def all_bands(row_spec, col_spec):

time: 73.3 us -> 73.4 us (level)
  no operation moved by 1% of the time
where the time goes in v6:
time: 73.4 us; the launch traced here: 72.1 us
  waiting for transfers between devices  21.1 us (29%)
  starting transfers between devices  20.7 us (28%)
  blocking collectives  15.1 us (21%)
  Pallas kernels  7.47 us (10%)
  local copies, waits for them, and re-layouts  3.63 us (5%)
  other arithmetic  3.14 us (4%)
  between operations  0.77 us (1%)
    all_to_all x2, waiting for transfers between devices, gather_by_all_to_all(): lax.all_to_all(jnp.broadcast_to(x, (size,) + x.shape[1:]), axis, 0, 0, ti...  21.1 us
    all_to_all x2, starting transfers between devices, gather_by_all_to_all(): lax.all_to_all(jnp.broadcast_to(x, (size,) + x.shape[1:]), axis, 0, 0, ti...  20 us
    all_to_all x1, blocking collectives, body(): partials = lax.all_to_all(partial_value, 'tm', 0, 0, tiled=True)  15.1 us
    pallas_call x1, Pallas kernels, all_bands(): pl.pallas_call(cross_kernel, grid=(bands, rows // tile), in_specs=[pl.Blo...  7.47 us
    broadcast_in_dim x2, local copies, waits for them, and re-layouts, gather_by_all_to_all(): jnp.broadcast_to(x, (size,) + x.shape[1:])  1.52 us
  transfers between devices with their start and end apart: 3, of which 2 were waited for; matrix products, arithmetic and copies ran while one was open for 2% of the time, Pallas kernels for 0%

profile of v6, /device:TPU:1, one launch (start us, length us, event | category | flops | bytes accessed | tf_op | source)
XLA Modules:
  0.0 72.1 jit_solution(7654061977460671322)
XLA Ops:
  0.6 0.0 copy-start
  0.7 0.8 %iota_add_fusion = s32[4,32]{1,0:T(4,128)S(1)} fusion(s32[4]{0:T(128)} %param.3), kind=kLoop, calls=%fused_computation.15 | loop fusion | flops 128 | bytes 528 | tf_op jit(solution)/shard_map/add | solution.py:18
  1.4 1.2 %multiply_convert_fusion.1 = (bf16[512,4,1,32]{0,3,2,1:T(8,128)(2,1)S(1)}, bf16[512,4,1,32]{0,3,2,1:T(8,128)(2,1)S(1)}) fusion(s32[4,32]{1,0:T(4,128)S(1)} %iota_add_fusion, s32[512]{0:T(512)S(1)} %iota_add_fusion.1), kind=kLoop, calls=%fused_computation.14 | loop fusion | flops 1245184 | bytes 264704 | tf_op jit(solution)/shard_map/convert
  2.7 0.0 copy-done
  2.7 0.3 convolution_bitcast_fusion
  3.0 15.1 %all_to_all.15 = f32[8,256,32]{1,2,0:T(8,128)S(1)} all-to-all(f32[8,256,32]{1,2,0:T(8,128)S(1)} %convolution_bitcast_fusion), channel_id=1, replica_groups=mesh['svc'=32,'tm'=8] {'tm'}, dimensions={0} | all-to-all | bytes 524288 | tf_op jit(solution)/shard_map/all_to_all | solution.py:90
  18.1 0.7 broadcast_in_dim.6
  18.7 3.4 %all-to-all-start.1 = ((bf16[8,256,32]{1,2,0:T(8,128)(2,1)}), bf16[8,256,32]{1,2,0:T(8,128)(2,1)S(1)}, u32[]{:S(2)}, u32[]{:S(2)}) async-start(bf16[8,256,32]{1,2,0:T(8,128)(2,1)} %broadcast_in_dim.6), calls=%async_computation.1 | async-start | bytes 262144 | tf_op jit(solution)/shard_map/all_to_all | solution.py:73
  22.1 0.7 collective-permute-start
  22.8 0.0 collective-permute-done
  22.8 6.2 %all-to-all-done.1 = bf16[8,256,32]{1,2,0:T(8,128)(2,1)S(1)} async-done(((bf16[8,256,32]{1,2,0:T(8,128)(2,1)}), bf16[8,256,32]{1,2,0:T(8,128)(2,1)S(1)}, u32[]{:S(2)}, u32[]{:S(2)}) %all-to-all-start.1) | async-done | bytes 131104 | tf_op jit(solution)/shard_map/all_to_all | solution.py:73
  29.0 0.9 %broadcast_in_dim.8 = bf16[32,256,32]{1,2,0:T(8,128)(2,1)} broadcast(bf16[256,32]{0,1:T(8,128)(2,1)S(1)} %bitcast.28), dimensions={1,2} | broadcast | bytes 540672 | tf_op jit(solution)/shard_map/broadcast_in_dim | solution.py:73
  29.8 16.6 %all-to-all-start.2 = ((bf16[32,256,32]{1,2,0:T(8,128)(2,1)}), bf16[32,256,32]{1,2,0:T(8,128)(2,1)S(1)}, u32[]{:S(2)}, u32[]{:S(2)}) async-start(bf16[32,256,32]{1,2,0:T(8,128)(2,1)} %broadcast_in_dim.8), calls=%async_computation.2 | async-start | bytes 1048576 | tf_op jit(solution)/shard_map/all_to_all | solution.py:73
  46.5 0.2 copy.13
  46.7 0.2 copy.14
  46.9 0.1 neg.14
  46.9 0.2 copy.10
  47.1 0.1 maximum_bitcast_fusion
  47.3 0.9 %pad_maximum_fusion.lhs_ref = bf16[4,2,256,64]{3,2,1,0:T(8,128)(2,1)} fusion(bf16[4,1,256,64]{3,2,1,0:T(8,128)(2,1)S(1)} %maximum_bitcast_fusion, bf16[4,1,256,64]{3,2,1,0:T(8,128)(2,1)S(1)} %copy.10), kind=kLoop, calls=%fused_computation.1 | loop fusion | flops 131072 | bytes 524288 | tf_op jit(solution)/shard_map/stack | solution.py:47
  48.2 14.9 %all-to-all-done.2 = bf16[32,256,32]{1,2,0:T(8,128)(2,1)S(1)} async-done(((bf16[32,256,32]{1,2,0:T(8,128)(2,1)}), bf16[32,256,32]{1,2,0:T(8,128)(2,1)S(1)}, u32[]{:S(2)}, u32[]{:S(2)}) %all-to-all-start.2) | async-done | bytes 524320 | tf_op jit(solution)/shard_map/all_to_all | solution.py:73
  63.1 0.3 copy.11
  63.4 0.2 reshape.110
  63.6 1.1 %copy.12 = bf16[4,2,32,1024]{3,2,1,0:T(8,128)(2,1)} copy(bf16[4,2,32,1024]{3,1,0,2:T(2,128)(2,1)S(1)} %bitcast.23) | data formatting | bytes 1048576 | tf_op jit(solution)/shard_map/transpose | solution.py:104
  64.6 7.5 %shard_map.41 = (bf16[4,2,256,1024]{3,2,1,0:T(8,128)(2,1)}, f32[4,256,1024]{2,1,0:T(8,128)}) custom-call(bf16[4,2,256,64]{3,2,1,0:T(8,128)(2,1)} %pad_maximum_fusion.lhs_ref, bf16[4,64,1024]{2,1,0:T(8,128)(2,1)} %bitcast.22), custom_call_target="tpu_custom_call" | custom-call | flops 274726912 | bytes 6291456 | tf_op jit(solution)/shard_map/pallas_call | solution.py:49
  (4 shorter events, 0.1 us)
Async XLA Ops:
  0.6 2.1 %copy-start = (bf16[256,512]{1,0:T(8,128)(2,1)S(1)}, bf16[256,512]{1,0:T(8,128)(2,1)}, u32[]{:S(2)}) copy-start(bf16[256,512]{1,0:T(8,128)(2,1)} %param.2) | copy-start | bytes 786436
  18.7 10.3 %all-to-all-start.1 = ((bf16[8,256,32]{1,2,0:T(8,128)(2,1)}), bf16[8,256,32]{1,2,0:T(8,128)(2,1)S(1)}, u32[]{:S(2)}, u32[]{:S(2)}) async-start(bf16[8,256,32]{1,2,0:T(8,128)(2,1)} %broadcast_in_dim.6), calls=%async_computation.1 | async-start | bytes 262144 | tf_op jit(solution)/shard_map/all_to_all | solution.py:73
  22.1 0.7 collective-permute-start
  29.8 33.2 %all-to-all-start.2 = ((bf16[32,256,32]{1,2,0:T(8,128)(2,1)}), bf16[32,256,32]{1,2,0:T(8,128)(2,1)S(1)}, u32[]{:S(2)}, u32[]{:S(2)}) async-start(bf16[32,256,32]{1,2,0:T(8,128)(2,1)} %broadcast_in_dim.8), calls=%async_computation.2 | async-start | bytes 1048576 | tf_op jit(solution)/shard_map/all_to_all | solution.py:73

commit v7 on v2

--- a/solution.py
+++ b/solution.py
@@ -43,7 +43,7 @@
     row_count = metrics.shape[0]
     local_minutes = metrics.shape[1]
     n_tm = lax.axis_size("tm")
-    n_svc = lax.axis_size("svc")
+    n_svc = lax.axis_size(SVC)
     owners = n_svc // n_tm
     width = BANDS * 2 * BINS
     chunk = width // n_tm
@@ -62,9 +62,11 @@
             s_dst = t_src * owners + r_src
             t_dst = g_src
             perm.append((s_src * n_tm + t_src, s_dst * n_tm + t_dst))
-    moved = lax.ppermute(piece, ("svc", "tm"), perm)
+    moved = lax.ppermute(piece, SVC + ("tm",), perm)
     row_chunks = gather_by_all_to_all(piece, "tm", n_tm)
-    col_chunks = gather_by_all_to_all(moved, "svc", n_svc)
+    by_group = gather_by_all_to_all(moved, "group", n_svc // owners)
+    by_owner = lax.all_to_all(jnp.broadcast_to(by_group[None], (owners,) + by_group.shape), "owner", 0, 0, tiled=True)
+    col_chunks = jnp.swapaxes(by_owner, 0, 1).reshape((n_svc,) + moved.shape[1:])
     bands_row = row_chunks.reshape(BANDS, 2, row_count, BINS)
     row_spec = jnp.transpose(bands_row, (0, 2, 1, 3)).reshape(BANDS, row_count, 2 * BINS)
     bands_col = col_chunks.reshape(BANDS, 2, owners, row_count, BINS)
@@ -72,11 +74,17 @@
     return all_bands(row_spec, col_spec)
 
 
+SVC = ("group", "owner")
+
+
 def solution(mesh):
+    n_svc, n_tm = mesh.shape["svc"], mesh.shape["tm"]
+    owners = n_svc // n_tm
+    split = jax.sharding.Mesh(mesh.devices.reshape(n_svc // owners, owners, n_tm), SVC + ("tm",))
     return jax.shard_map(
         body,
-        mesh=mesh,
-        in_specs=(P("svc", "tm"), P()),
-        out_specs=(P(None, None, "svc", "tm"), P(None, "svc", "tm")),
+        mesh=split,
+        in_specs=(P(SVC, "tm"), P()),
+        out_specs=(P(None, None, SVC, "tm"), P(None, SVC, "tm")),
         check_vma=False,
     )

time: 71 us -> 73.9 us (1.041); the launches traced: 69.8 us -> 73.6 us
  blocking collectives: 15.1 us -> 35.8 us
  starting transfers between devices: 20.7 us -> 12 us
  waiting for transfers between devices: 22.7 us -> 14.1 us
    all_to_all x0 -> x1, blocking collectives: none -> 20.7 us  [gather_by_all_to_all(): lax.all_to_all(jnp.broadcast_to(x, (size,) + x.shape[1:]), axis, 0, 0, ti...]
    all_to_all x2 -> x1, starting transfers between devices: 20 us -> 3.37 us  [gather_by_all_to_all(): lax.all_to_all(jnp.broadcast_to(x, (size,) + x.shape[1:]), axis, 0, 0, ti...]
    all_to_all x2 -> x1, waiting for transfers between devices: 22.7 us -> 6.19 us  [gather_by_all_to_all(): lax.all_to_all(jnp.broadcast_to(x, (size,) + x.shape[1:]), axis, 0, 0, ti...]
    all_to_all x0 -> x1, starting transfers between devices: none -> 7.94 us  [body(): lax.all_to_all(jnp.broadcast_to(by_group[None], (owners,) + by_group.shap...]
    all_to_all x0 -> x1, waiting for transfers between devices: none -> 7.89 us  [body(): lax.all_to_all(jnp.broadcast_to(by_group[None], (owners,) + by_group.shap...]
    broadcast_in_dim x0 -> x1, local copies, waits for them, and re-layouts: none -> 0.85 us  [body(): jnp.broadcast_to(by_group[None], (owners,) + by_group.shape)]
    broadcast_in_dim x2, local copies, waits for them, and re-layouts: 1.52 us -> 0.67 us  [gather_by_all_to_all(): jnp.broadcast_to(x, (size,) + x.shape[1:])]
where the time goes in v7:
time: 73.9 us; the launch traced here: 73.6 us
  blocking collectives  35.8 us (48%)
  waiting for transfers between devices  14.1 us (19%)
  starting transfers between devices  12 us (16%)
  other arithmetic  5.05 us (7%)
  matrix products  3.57 us (5%)
  local copies, waits for them, and re-layouts  2.32 us (3%)
  between operations  0.76 us (1%)
    all_to_all x1, blocking collectives, gather_by_all_to_all(): lax.all_to_all(jnp.broadcast_to(x, (size,) + x.shape[1:]), axis, 0, 0, ti...  20.7 us
    all_to_all x1, blocking collectives, body(): partials = lax.all_to_all(partial_value, 'tm', 0, 0, tiled=True)  15.1 us
    all_to_all x1, starting transfers between devices, body(): lax.all_to_all(jnp.broadcast_to(by_group[None], (owners,) + by_group.shap...  7.94 us
    all_to_all x1, waiting for transfers between devices, body(): lax.all_to_all(jnp.broadcast_to(by_group[None], (owners,) + by_group.shap...  7.89 us
    all_to_all x1, waiting for transfers between devices, gather_by_all_to_all(): lax.all_to_all(jnp.broadcast_to(x, (size,) + x.shape[1:]), axis, 0, 0, ti...  6.19 us
    all_to_all x1, starting transfers between devices, gather_by_all_to_all(): lax.all_to_all(jnp.broadcast_to(x, (size,) + x.shape[1:]), axis, 0, 0, ti...  3.37 us
    dot_general x1, matrix products, all_bands(): jnp.einsum('bpik,bjk->bpij', lhs, col_spec, preferred_element_type=jnp.fl...  3.31 us
    div x1, other arithmetic, all_bands(): (real_part * real_part + imag_part * imag_part) / ((row_power[:, :, None]...  2.5 us
  transfers between devices with their start and end apart: 3, of which 2 were waited for; matrix products, arithmetic and copies ran while one was open for 0% of the time, Pallas kernels for 0%

profile of v7, /device:TPU:1, one launch (start us, length us, event | category | flops | bytes accessed | tf_op | source)
XLA Modules:
  0.0 73.6 jit_solution(15488611913248120839)
XLA Ops:
  0.6 0.0 copy-start
  0.7 0.8 %iota_add_fusion = s32[4,32]{1,0:T(4,128)S(1)} fusion(s32[4]{0:T(128)} %param.3), kind=kLoop, calls=%fused_computation.30 | loop fusion | flops 128 | bytes 528 | tf_op jit(solution)/shard_map/add | solution.py:16
  1.4 1.2 %multiply_convert_fusion.1 = (bf16[512,4,1,32]{0,3,2,1:T(8,128)(2,1)S(1)}, bf16[512,4,1,32]{0,3,2,1:T(8,128)(2,1)S(1)}) fusion(s32[4,32]{1,0:T(4,128)S(1)} %iota_add_fusion, s32[512]{0:T(512)S(1)} %iota_add_fusion.1), kind=kLoop, calls=%fused_computation.25 | loop fusion | flops 1245184 | bytes 264704 | tf_op jit(solution)/shard_map/convert
  2.7 0.0 copy-done
  2.7 0.3 convolution_bitcast_fusion
  3.0 15.1 %all_to_all.20 = f32[8,256,32]{1,2,0:T(8,128)S(1)} all-to-all(f32[8,256,32]{1,2,0:T(8,128)S(1)} %convolution_bitcast_fusion), channel_id=1, replica_groups=mesh['group'=8,'owner'=4,'tm'=8] {'tm'}, dimensions={0} | all-to-all | bytes 524288 | tf_op jit(solution)/shard_map/all_to_all | solution.py:56
  18.1 0.7 broadcast_in_dim.8
  18.7 3.4 %all-to-all-start.1 = ((bf16[8,256,32]{1,2,0:T(8,128)(2,1)}), bf16[8,256,32]{1,2,0:T(8,128)(2,1)S(1)}, u32[]{:S(2)}, u32[]{:S(2)}) async-start(bf16[8,256,32]{1,2,0:T(8,128)(2,1)} %broadcast_in_dim.8), calls=%async_computation.1 | async-start | bytes 262144 | tf_op jit(solution)/shard_map/all_to_all | solution.py:39
  22.1 0.7 collective-permute-start
  22.8 0.0 collective-permute-done
  22.8 6.2 %all-to-all-done.1 = bf16[8,256,32]{1,2,0:T(8,128)(2,1)S(1)} async-done(((bf16[8,256,32]{1,2,0:T(8,128)(2,1)}), bf16[8,256,32]{1,2,0:T(8,128)(2,1)S(1)}, u32[]{:S(2)}, u32[]{:S(2)}) %all-to-all-start.1) | async-done | bytes 131104 | tf_op jit(solution)/shard_map/all_to_all | solution.py:39
  29.0 20.7 %all_to_all.21 = bf16[8,256,32]{1,2,0:T(8,128)(2,1)S(1)} all-to-all(bf16[8,256,32]{1,2,0:T(8,128)(2,1)S(1)} %broadcast_in_dim.10), channel_id=1, replica_groups=mesh['group'=8,'owner'=4,'tm'=8] {'group'}, dimensions={0} | all-to-all | bytes 262144 | tf_op jit(solution)/shard_map/all_to_all | solution.py:39
  49.8 0.9 %broadcast_in_dim.11 = bf16[4,8,256,32]{2,3,1,0:T(8,128)(2,1)} broadcast(bf16[8,256,32]{1,2,0:T(8,128)(2,1)S(1)} %all_to_all.21), dimensions={1,2,3} | broadcast | bytes 655360 | tf_op jit(solution)/shard_map/broadcast_in_dim | solution.py:68
  50.6 7.9 %all-to-all-start.3 = ((bf16[4,8,256,32]{2,3,1,0:T(8,128)(2,1)}), bf16[4,8,256,32]{2,3,1,0:T(8,128)(2,1)S(1)}, u32[]{:S(2)}, u32[]{:S(2)}) async-start(bf16[4,8,256,32]{2,3,1,0:T(8,128)(2,1)} %broadcast_in_dim.11), calls=%async_computation.3 | async-start | bytes 1048576 | tf_op jit(solution)/shard_map/all_to_all | solution.py:68
  58.6 7.9 %all-to-all-done.3 = bf16[4,8,256,32]{2,3,1,0:T(8,128)(2,1)S(1)} async-done(((bf16[4,8,256,32]{2,3,1,0:T(8,128)(2,1)}), bf16[4,8,256,32]{2,3,1,0:T(8,128)(2,1)S(1)}, u32[]{:S(2)}, u32[]{:S(2)}) %all-to-all-start.3) | async-done | bytes 524320 | tf_op jit(solution)/shard_map/all_to_all | solution.py:68
  66.5 0.4 multiply_reduce_fusion
  67.0 0.4 copy.10
  67.4 0.4 reshape.131
  67.8 3.3 %fusion.13 = (bf16[4,2,256,1024]{3,2,1,0:T(8,128)(2,1)}, f32[4,2,256,1024]{3,2,1,0:T(8,128)S(1)}) fusion(bf16[4,1024,64,1]{1,2,0,3:T(8,128)(2,1)S(1)} %reshape.131, bf16[4,1,256,64]{2,3,1,0:T(8,128)(2,1)S(1)} %maximum_bitcast_fusion, bf16[4,1,256,64]{2,3,1,0:T(8,128)(2,1)S(1)} %bitcast.44), kind=kOutput, calls=%fused_computation.34 | convolution fusion | flops 272760832 | bytes 13369344 | tf_op jit(solution)/shard_map/bpik,bjk->bpij/dot_general | solution.py:27
  71.1 2.5 %fusion.2 = f32[4,256,1024]{2,1,0:T(8,128)} fusion(f32[4,2,256,1024]{3,2,1,0:T(8,128)S(1)} %get-tuple-element.7, f32[4,1024]{1,0:T(4,128)S(1)} %bitcast.47, f32[4,256]{1,0:T(4,128)S(1)} %multiply_add_fusion), kind=kLoop, calls=%fused_computation.3 | loop fusion | flops 5242880 | bytes 12603392 | tf_op jit(solution)/shard_map/div | solution.py:32
  (10 shorter events, 0.1 us)
Async XLA Ops:
  0.6 2.1 %copy-start = (bf16[256,512]{1,0:T(8,128)(2,1)S(1)}, bf16[256,512]{1,0:T(8,128)(2,1)}, u32[]{:S(2)}) copy-start(bf16[256,512]{1,0:T(8,128)(2,1)} %param.2) | copy-start | bytes 786436
  18.7 10.3 %all-to-all-start.1 = ((bf16[8,256,32]{1,2,0:T(8,128)(2,1)}), bf16[8,256,32]{1,2,0:T(8,128)(2,1)S(1)}, u32[]{:S(2)}, u32[]{:S(2)}) async-start(bf16[8,256,32]{1,2,0:T(8,128)(2,1)} %broadcast_in_dim.8), calls=%async_computation.1 | async-start | bytes 262144 | tf_op jit(solution)/shard_map/all_to_all | solution.py:39
  22.1 0.7 collective-permute-start
  50.6 15.9 %all-to-all-start.3 = ((bf16[4,8,256,32]{2,3,1,0:T(8,128)(2,1)}), bf16[4,8,256,32]{2,3,1,0:T(8,128)(2,1)S(1)}, u32[]{:S(2)}, u32[]{:S(2)}) async-start(bf16[4,8,256,32]{2,3,1,0:T(8,128)(2,1)} %broadcast_in_dim.11), calls=%async_computation.3 | async-start | bytes 1048576 | tf_op jit(solution)/shard_map/all_to_all | solution.py:68

commit v8 on v2

--- a/solution.py
+++ b/solution.py
@@ -11,14 +11,23 @@
 epsilon = 1e-06
 
 
-def make_table(minutes, band_starts):
+def unit_phasors(minutes, freqs):
+    phase_index = minutes[:, None, None] * freqs[None, :, :] % TLEN
+    phases = 2.0 * jnp.pi / TLEN * phase_index.astype(jnp.float32)
+    return jnp.cos(phases), jnp.sin(phases)
+
+
+def make_table(first_minute, count, band_starts):
     offsets = jnp.arange(BINS, dtype=jnp.int32)
     freqs = band_starts[:, None] + offsets[None, :]
-    phase_index = minutes[:, None, None] * freqs[None, :, :] % TLEN
-    phases = 2.0 * jnp.pi / TLEN * phase_index.astype(jnp.float32)
+    step = 64
+    fine_cos, fine_sin = unit_phasors(first_minute + jnp.arange(step, dtype=jnp.int32), freqs)
+    coarse_cos, coarse_sin = unit_phasors(step * jnp.arange(count // step, dtype=jnp.int32), freqs)
+    cos_value = coarse_cos[:, None] * fine_cos[None] - coarse_sin[:, None] * fine_sin[None]
+    sin_value = coarse_sin[:, None] * fine_cos[None] + coarse_cos[:, None] * fine_sin[None]
     norm = 1.0 / jnp.sqrt(jnp.float32(TLEN))
-    stacked = jnp.stack([jnp.cos(phases) * norm, -jnp.sin(phases) * norm], axis=2)
-    return stacked.reshape(minutes.shape[0], BANDS * 2 * BINS).astype(jnp.bfloat16)
+    stacked = jnp.stack([cos_value * norm, -sin_value * norm], axis=3)
+    return stacked.reshape(count, BANDS * 2 * BINS).astype(jnp.bfloat16)
 
 
 def all_bands(row_spec, col_spec):
@@ -48,8 +57,8 @@
     width = BANDS * 2 * BINS
     chunk = width // n_tm
     time_index = lax.axis_index("tm")
-    minutes = time_index * local_minutes + jnp.arange(local_minutes, dtype=jnp.int32)
-    dft_table = make_table(minutes, band_starts).reshape(local_minutes, n_tm, chunk)
+    dft_table = make_table(time_index * local_minutes, local_minutes, band_starts)
+    dft_table = dft_table.reshape(local_minutes, n_tm, chunk)
     partial_value = jnp.einsum(
         "nt,tcb->cnb", metrics, dft_table, preferred_element_type=jnp.float32
     )

time: 71 us -> 71.2 us (level)
    another operation x2, other arithmetic: 1.25 us -> 0.45 us
where the time goes in v8:
time: 71.2 us; the launch traced here: 70 us
  waiting for transfers between devices  22.7 us (32%)
  starting transfers between devices  20.7 us (29%)
  blocking collectives  15.1 us (21%)
  other arithmetic  4.63 us (7%)
  matrix products  3.56 us (5%)
  local copies, waits for them, and re-layouts  2.63 us (4%)
  between operations  0.79 us (1%)
    all_to_all x2, waiting for transfers between devices, gather_by_all_to_all(): lax.all_to_all(jnp.broadcast_to(x, (size,) + x.shape[1:]), axis, 0, 0, ti...  22.7 us
    all_to_all x2, starting transfers between devices, gather_by_all_to_all(): lax.all_to_all(jnp.broadcast_to(x, (size,) + x.shape[1:]), axis, 0, 0, ti...  20 us
    all_to_all x1, blocking collectives, body(): partials = lax.all_to_all(partial_value, 'tm', 0, 0, tiled=True)  15.1 us
    dot_general x1, matrix products, all_bands(): jnp.einsum('bpik,bjk->bpij', lhs, col_spec, preferred_element_type=jnp.fl...  3.31 us
    div x1, other arithmetic, all_bands(): (real_part * real_part + imag_part * imag_part) / ((row_power[:, :, None]...  2.5 us
    broadcast_in_dim x2, local copies, waits for them, and re-layouts, gather_by_all_to_all(): jnp.broadcast_to(x, (size,) + x.shape[1:])  1.52 us
  transfers between devices with their start and end apart: 3, of which 2 were waited for; matrix products, arithmetic and copies ran while one was open for 0% of the time, Pallas kernels for 0%

profile of v8, /device:TPU:1, one launch (start us, length us, event | category | flops | bytes accessed | tf_op | source)
XLA Modules:
  0.0 70.0 jit_solution(9270951608120882574)
XLA Ops:
  0.6 0.0 copy-start
  0.7 0.8 %iota_add_fusion = s32[4,32]{1,0:T(4,128)S(1)} fusion(s32[4]{0:T(128)} %param.3), kind=kLoop, calls=%fused_computation.41 | loop fusion | flops 128 | bytes 528 | tf_op jit(solution)/shard_map/add | solution.py:22
  1.4 0.3 fusion.15
  1.8 0.3 fusion.17
  2.1 0.3 multiply_convert_fusion.1
  2.5 0.1 pad_maximum_fusion
  2.6 0.3 convert_element_type.53
  2.9 0.0 copy-done
  2.9 0.3 convolution_bitcast_fusion
  3.2 15.1 %all_to_all.15 = f32[8,256,32]{1,2,0:T(8,128)S(1)} all-to-all(f32[8,256,32]{1,2,0:T(8,128)S(1)} %convolution_bitcast_fusion), channel_id=1, replica_groups=mesh['svc'=32,'tm'=8] {'tm'}, dimensions={0} | all-to-all | bytes 524288 | tf_op jit(solution)/shard_map/all_to_all | solution.py:65
  18.3 0.7 broadcast_in_dim.6
  18.9 3.4 %all-to-all-start.1 = ((bf16[8,256,32]{1,2,0:T(8,128)(2,1)}), bf16[8,256,32]{1,2,0:T(8,128)(2,1)S(1)}, u32[]{:S(2)}, u32[]{:S(2)}) async-start(bf16[8,256,32]{1,2,0:T(8,128)(2,1)} %broadcast_in_dim.6), calls=%async_computation.1 | async-start | bytes 262144 | tf_op jit(solution)/shard_map/all_to_all | solution.py:48
  22.3 0.7 collective-permute-start
  23.0 0.0 collective-permute-done
  23.0 6.2 %all-to-all-done.1 = bf16[8,256,32]{1,2,0:T(8,128)(2,1)S(1)} async-done(((bf16[8,256,32]{1,2,0:T(8,128)(2,1)}), bf16[8,256,32]{1,2,0:T(8,128)(2,1)S(1)}, u32[]{:S(2)}, u32[]{:S(2)}) %all-to-all-start.1) | async-done | bytes 131104 | tf_op jit(solution)/shard_map/all_to_all | solution.py:48
  29.2 0.9 %broadcast_in_dim.8 = bf16[32,256,32]{1,2,0:T(8,128)(2,1)} broadcast(bf16[256,32]{0,1:T(8,128)(2,1)S(1)} %bitcast.45), dimensions={1,2} | broadcast | bytes 540672 | tf_op jit(solution)/shard_map/broadcast_in_dim | solution.py:48
  30.1 16.6 %all-to-all-start.2 = ((bf16[32,256,32]{1,2,0:T(8,128)(2,1)}), bf16[32,256,32]{1,2,0:T(8,128)(2,1)S(1)}, u32[]{:S(2)}, u32[]{:S(2)}) async-start(bf16[32,256,32]{1,2,0:T(8,128)(2,1)} %broadcast_in_dim.8), calls=%async_computation.2 | async-start | bytes 1048576 | tf_op jit(solution)/shard_map/all_to_all | solution.py:48
  46.8 16.5 %all-to-all-done.2 = bf16[32,256,32]{1,2,0:T(8,128)(2,1)S(1)} async-done(((bf16[32,256,32]{1,2,0:T(8,128)(2,1)}), bf16[32,256,32]{1,2,0:T(8,128)(2,1)S(1)}, u32[]{:S(2)}, u32[]{:S(2)}) %all-to-all-start.2) | async-done | bytes 524320 | tf_op jit(solution)/shard_map/all_to_all | solution.py:48
  63.3 0.1 multiply_reduce_fusion
  63.4 0.4 copy.5
  63.8 0.4 reshape.140
  64.2 3.3 %fusion.20 = (bf16[4,2,256,1024]{3,2,1,0:T(8,128)(2,1)}, f32[4,2,256,1024]{3,2,1,0:T(8,128)S(1)}) fusion(bf16[4,1024,64,1]{1,2,0,3:T(8,128)(2,1)S(1)} %reshape.140, bf16[4,1,256,64]{2,3,1,0:T(8,128)(2,1)S(1)} %maximum_bitcast_fusion, bf16[4,1,256,64]{2,3,1,0:T(8,128)(2,1)S(1)} %bitcast.42), kind=kOutput, calls=%fused_computation.46 | convolution fusion | flops 272760832 | bytes 13369344 | tf_op jit(solution)/shard_map/bpik,bjk->bpij/dot_general | solution.py:36
  67.5 2.5 %fusion.2 = f32[4,256,1024]{2,1,0:T(8,128)} fusion(f32[4,2,256,1024]{3,2,1,0:T(8,128)S(1)} %get-tuple-element.11, f32[4,1024]{1,0:T(4,128)S(1)} %bitcast.43, f32[4,256]{1,0:T(4,128)S(1)} %multiply_add_fusion), kind=kLoop, calls=%fused_computation.3 | loop fusion | flops 5242880 | bytes 12603392 | tf_op jit(solution)/shard_map/div | solution.py:41
  (9 shorter events, 0.1 us)
Async XLA Ops:
  0.6 2.3 %copy-start = (bf16[256,512]{1,0:T(8,128)(2,1)S(1)}, bf16[256,512]{1,0:T(8,128)(2,1)}, u32[]{:S(2)}) copy-start(bf16[256,512]{1,0:T(8,128)(2,1)} %param.2) | copy-start | bytes 786436
  18.9 10.3 %all-to-all-start.1 = ((bf16[8,256,32]{1,2,0:T(8,128)(2,1)}), bf16[8,256,32]{1,2,0:T(8,128)(2,1)S(1)}, u32[]{:S(2)}, u32[]{:S(2)}) async-start(bf16[8,256,32]{1,2,0:T(8,128)(2,1)} %broadcast_in_dim.6), calls=%async_computation.1 | async-start | bytes 262144 | tf_op jit(solution)/shard_map/all_to_all | solution.py:48
  22.3 0.7 collective-permute-start
  30.1 33.2 %all-to-all-start.2 = ((bf16[32,256,32]{1,2,0:T(8,128)(2,1)}), bf16[32,256,32]{1,2,0:T(8,128)(2,1)S(1)}, u32[]{:S(2)}, u32[]{:S(2)}) async-start(bf16[32,256,32]{1,2,0:T(8,128)(2,1)} %broadcast_in_dim.8), calls=%async_computation.2 | async-start | bytes 1048576 | tf_op jit(solution)/shard_map/all_to_all | solution.py:48

commit v9 on v2

--- a/solution.py
+++ b/solution.py
@@ -63,7 +63,12 @@
             t_dst = g_src
             perm.append((s_src * n_tm + t_src, s_dst * n_tm + t_dst))
     moved = lax.ppermute(piece, ("svc", "tm"), perm)
-    row_chunks = gather_by_all_to_all(piece, "tm", n_tm)
+    row_parts = [piece]
+    for shift in range(1, n_tm):
+        pairs = [(a * n_tm + b, a * n_tm + (b + shift) % n_tm) for a in range(n_svc) for b in range(n_tm)]
+        row_parts.append(lax.ppermute(piece, ("svc", "tm"), pairs))
+    order = (time_index - jnp.arange(n_tm, dtype=jnp.int32)) % n_tm
+    row_chunks = jnp.take(jnp.concatenate(row_parts, axis=0), order, axis=0)
     col_chunks = gather_by_all_to_all(moved, "svc", n_svc)
     bands_row = row_chunks.reshape(BANDS, 2, row_count, BINS)
     row_spec = jnp.transpose(bands_row, (0, 2, 1, 3)).reshape(BANDS, row_count, 2 * BINS)

time: 71 us -> 69.1 us (0.973); the launches traced: 69.8 us -> 68.7 us
  blocking collectives: 15.1 us -> 0 us
  starting transfers between devices: 20.7 us -> 33.1 us
  matrix products: 3.57 us -> 4.28 us
    all_to_all x2 -> x1, waiting for transfers between devices: 22.7 us -> 3.85 us  [gather_by_all_to_all(): lax.all_to_all(jnp.broadcast_to(x, (size,) + x.shape[1:]), axis, 0, 0, ti...]
    ppermute x0 -> x7, starting transfers between devices: none -> 16.8 us  [body(): row_parts.append(lax.ppermute(piece, ('svc', 'tm'), pairs))]
    all_to_all x1 -> x0, blocking collectives: 15.1 us -> none  [body(): partials = lax.all_to_all(partial_value, 'tm', 0, 0, tiled=True)]
    all_to_all x2 -> x1, starting transfers between devices: 20 us -> 8.16 us  [gather_by_all_to_all(): lax.all_to_all(jnp.broadcast_to(x, (size,) + x.shape[1:]), axis, 0, 0, ti...]
    ppermute x0 -> x7, waiting for transfers between devices: none -> 11.8 us  [body(): row_parts.append(lax.ppermute(piece, ('svc', 'tm'), pairs))]
    all_to_all x0 -> x1, waiting for transfers between devices: none -> 7.76 us  [body(): partials = lax.all_to_all(partial_value, 'tm', 0, 0, tiled=True)]
    all_to_all x0 -> x1, starting transfers between devices: none -> 7.48 us  [body(): partials = lax.all_to_all(partial_value, 'tm', 0, 0, tiled=True)]
    broadcast_in_dim x2 -> x1, local copies, waits for them, and re-layouts: 1.52 us -> 0.85 us  [gather_by_all_to_all(): jnp.broadcast_to(x, (size,) + x.shape[1:])]
  transfers between devices with their start and end apart: 3 -> 10, of which waited for: 2 -> 4; matrix products, arithmetic and copies ran while one was open for 0% -> 2% of each run, Pallas kernels for 0% -> 0%
where the time goes in v9:
time: 69.1 us; the launch traced here: 68.7 us
  starting transfers between devices  33.1 us (48%)
  waiting for transfers between devices  23.4 us (34%)
  other arithmetic  4.89 us (7%)
  matrix products  4.28 us (6%)
  local copies, waits for them, and re-layouts  2.23 us (3%)
  between operations  0.84 us (1%)
    ppermute x7, starting transfers between devices, body(): row_parts.append(lax.ppermute(piece, ('svc', 'tm'), pairs))  16.8 us
    ppermute x7, waiting for transfers between devices, body(): row_parts.append(lax.ppermute(piece, ('svc', 'tm'), pairs))  11.8 us
    all_to_all x1, starting transfers between devices, gather_by_all_to_all(): lax.all_to_all(jnp.broadcast_to(x, (size,) + x.shape[1:]), axis, 0, 0, ti...  8.16 us
    all_to_all x1, waiting for transfers between devices, body(): partials = lax.all_to_all(partial_value, 'tm', 0, 0, tiled=True)  7.76 us
    all_to_all x1, starting transfers between devices, body(): partials = lax.all_to_all(partial_value, 'tm', 0, 0, tiled=True)  7.48 us
    all_to_all x1, waiting for transfers between devices, gather_by_all_to_all(): lax.all_to_all(jnp.broadcast_to(x, (size,) + x.shape[1:]), axis, 0, 0, ti...  3.85 us
    dot_general x1, matrix products, all_bands(): jnp.einsum('bpik,bjk->bpij', lhs, col_spec, preferred_element_type=jnp.fl...  3.31 us
    div x1, other arithmetic, all_bands(): (real_part * real_part + imag_part * imag_part) / ((row_power[:, :, None]...  2.5 us
  transfers between devices with their start and end apart: 10, of which 4 were waited for; matrix products, arithmetic and copies ran while one was open for 2% of the time, Pallas kernels for 0%

profile of v9, /device:TPU:1, one launch (start us, length us, event | category | flops | bytes accessed | tf_op | source)
XLA Modules:
  0.0 68.7 jit_solution(17601261351740815086)
XLA Ops:
  0.6 0.0 copy-start
  0.7 0.8 %iota_add_fusion = s32[4,32]{1,0:T(4,128)S(1)} fusion(s32[4]{0:T(128)} %param.3), kind=kLoop, calls=%fused_computation.49 | loop fusion | flops 128 | bytes 528 | tf_op jit(solution)/shard_map/add | solution.py:16
  1.4 1.2 %multiply_convert_fusion.1 = (bf16[512,4,1,32]{0,3,2,1:T(8,128)(2,1)S(1)}, bf16[512,4,1,32]{0,3,2,1:T(8,128)(2,1)S(1)}) fusion(s32[4,32]{1,0:T(4,128)S(1)} %iota_add_fusion, s32[512]{0:T(512)S(1)} %iota_add_fusion.1), kind=kLoop, calls=%fused_computation.25 | loop fusion | flops 1245184 | bytes 264704 | tf_op jit(solution)/shard_map/convert
  2.7 0.0 copy-done
  2.7 1.0 %convolution_bitcast_fusion = f32[8,256,32]{1,2,0:T(8,128)} fusion(bf16[512,8,32]{0,2,1:T(8,128)(2,1)S(1)} %bitcast.45, bf16[256,512]{1,0:T(8,128)(2,1)S(1)} %copy-done), kind=kOutput, calls=%fused_computation.7 | convolution fusion | flops 67108864 | bytes 786432 | tf_op jit(solution)/shard_map/nt,tcb->cnb/dot_general | solution.py:53
  3.7 7.5 %all-to-all-start = ((f32[8,256,32]{1,2,0:T(8,128)}), f32[8,256,32]{1,2,0:T(8,128)S(1)}, u32[]{:S(2)}, u32[]{:S(2)}) async-start(f32[8,256,32]{1,2,0:T(8,128)} %convolution_bitcast_fusion), calls=%async_computation | async-start | bytes 524288 | tf_op jit(solution)/shard_map/all_to_all | solution.py:56
  11.2 7.8 %all-to-all-done = f32[8,256,32]{1,2,0:T(8,128)S(1)} async-done(((f32[8,256,32]{1,2,0:T(8,128)}), f32[8,256,32]{1,2,0:T(8,128)S(1)}, u32[]{:S(2)}, u32[]{:S(2)}) %all-to-all-start) | async-done | bytes 262176 | tf_op jit(solution)/shard_map/all_to_all | solution.py:56
  19.0 0.7 collective-permute-start.7
  19.6 11.3 %collective-permute-start.6 = (bf16[1,256,32]{1,2,0:T(8,128)(2,1)S(1)}, bf16[1,256,32]{1,2,0:T(8,128)(2,1)S(1)}, u32[]{:S(2)}, u32[]{:S(2)}) collective-permute-start(bf16[1,256,32]{1,2,0:T(8,128)(2,1)S(1)} %bitcast.48), channel_id=1, source_target_pairs={{0,7},{1,0},{2,1},{3,2},{4,3},{5,4},{6,5},{7,6},{8,15},{9,8},{10,9... | collective-permute-start | bytes 49160 | tf_op jit(solution)/shard_map/ppermute | solution.py:69
  31.0 1.3 %collective-permute-start.5 = (bf16[1,256,32]{1,2,0:T(8,128)(2,1)S(1)}, bf16[1,256,32]{1,2,0:T(8,128)(2,1)S(1)}, u32[]{:S(2)}, u32[]{:S(2)}) collective-permute-start(bf16[1,256,32]{1,2,0:T(8,128)(2,1)S(1)} %bitcast.49), channel_id=1, source_target_pairs={{0,6},{1,7},{2,0},{3,1},{4,2},{5,3},{6,4},{7,5},{8,14},{9,15},{10,... | collective-permute-start | bytes 49160 | tf_op jit(solution)/shard_map/ppermute | solution.py:69
  32.3 1.6 %collective-permute-start.4 = (bf16[1,256,32]{1,2,0:T(8,128)(2,1)S(1)}, bf16[1,256,32]{1,2,0:T(8,128)(2,1)S(1)}, u32[]{:S(2)}, u32[]{:S(2)}) collective-permute-start(bf16[1,256,32]{1,2,0:T(8,128)(2,1)S(1)} %bitcast.50), channel_id=1, source_target_pairs={{0,5},{1,6},{2,7},{3,0},{4,1},{5,2},{6,3},{7,4},{8,13},{9,14},{10,... | collective-permute-start | bytes 49160 | tf_op jit(solution)/shard_map/ppermute | solution.py:69
  33.8 0.6 collective-permute-start
  34.4 0.0 collective-permute-done.7
  34.4 1.9 %collective-permute-start.3 = (bf16[1,256,32]{1,2,0:T(8,128)(2,1)S(1)}, bf16[1,256,32]{1,2,0:T(8,128)(2,1)S(1)}, u32[]{:S(2)}, u32[]{:S(2)}) collective-permute-start(bf16[1,256,32]{1,2,0:T(8,128)(2,1)S(1)} %bitcast.52), channel_id=1, source_target_pairs={{0,4},{1,5},{2,6},{3,7},{4,0},{5,1},{6,2},{7,3},{8,12},{9,13},{10,... | collective-permute-start | bytes 49160 | tf_op jit(solution)/shard_map/ppermute | solution.py:69
  36.3 0.9 %broadcast_in_dim.27 = bf16[32,256,32]{1,2,0:T(8,128)(2,1)} broadcast(bf16[256,32]{0,1:T(8,128)(2,1)S(1)} %bitcast.55), dimensions={1,2} | broadcast | bytes 540672 | tf_op jit(solution)/shard_map/broadcast_in_dim | solution.py:39
  37.2 8.2 %all-to-all-start.1 = ((bf16[32,256,32]{1,2,0:T(8,128)(2,1)}), bf16[32,256,32]{1,2,0:T(8,128)(2,1)S(1)}, u32[]{:S(2)}, u32[]{:S(2)}) async-start(bf16[32,256,32]{1,2,0:T(8,128)(2,1)} %broadcast_in_dim.27), calls=%async_computation.1 | async-start | bytes 1048576 | tf_op jit(solution)/shard_map/all_to_all | solution.py:39
  45.4 0.0 collective-permute-done
  45.4 0.1 collective-permute-start.1
  45.5 6.5 %collective-permute-done.1 = bf16[1,256,32]{1,2,0:T(8,128)(2,1)S(1)} collective-permute-done((bf16[1,256,32]{1,2,0:T(8,128)(2,1)S(1)}, bf16[1,256,32]{1,2,0:T(8,128)(2,1)S(1)}, u32[]{:S(2)}, u32[]{:S(2)}) %collective-permute-start.1) | collective-permute-done | bytes 16416 | tf_op jit(solution)/shard_map/ppermute | solution.py:69
  52.0 0.0 collective-permute-start.2
  52.0 5.3 %collective-permute-done.2 = bf16[1,256,32]{1,2,0:T(8,128)(2,1)S(1)} collective-permute-done((bf16[1,256,32]{1,2,0:T(8,128)(2,1)S(1)}, bf16[1,256,32]{1,2,0:T(8,128)(2,1)S(1)}, u32[]{:S(2)}, u32[]{:S(2)}) %collective-permute-start.2) | collective-permute-done | bytes 16416 | tf_op jit(solution)/shard_map/ppermute | solution.py:69
  57.3 0.0 collective-permute-done.3
  57.3 0.0 collective-permute-done.4
  57.3 0.0 collective-permute-done.5
  57.3 0.0 collective-permute-done.6
  57.3 0.6 gather_fusion
  57.9 0.1 multiply_reduce_fusion.1
  58.1 3.9 %all-to-all-done.1 = bf16[32,256,32]{1,2,0:T(8,128)(2,1)S(1)} async-done(((bf16[32,256,32]{1,2,0:T(8,128)(2,1)}), bf16[32,256,32]{1,2,0:T(8,128)(2,1)S(1)}, u32[]{:S(2)}, u32[]{:S(2)}) %all-to-all-start.1) | async-done | bytes 524320 | tf_op jit(solution)/shard_map/all_to_all | solution.py:39
  61.9 0.1 multiply_reduce_fusion
  62.1 0.4 copy.4
  62.5 0.4 reshape.196
  62.9 3.3 %fusion.16 = (bf16[4,2,256,1024]{3,2,1,0:T(8,128)(2,1)}, f32[4,2,256,1024]{3,2,1,0:T(8,128)S(1)}) fusion(bf16[4,1024,64,1]{1,2,0,3:T(8,128)(2,1)S(1)} %reshape.196, bf16[4,1,256,64]{2,3,1,0:T(8,128)(2,1)S(1)} %maximum_bitcast_fusion, bf16[4,1,256,64]{2,3,1,0:T(8,128)(2,1)S(1)} %bitcast.44), kind=kOutput, calls=%fused_computation.57 | convolution fusion | flops 272760832 | bytes 13369344 | tf_op jit(solution)/shard_map/bpik,bjk->bpij/dot_general | solution.py:27
  66.2 2.5 %fusion.2 = f32[4,256,1024]{2,1,0:T(8,128)} fusion(f32[4,2,256,1024]{3,2,1,0:T(8,128)S(1)} %get-tuple-element.9, f32[4,1024]{1,0:T(4,128)S(1)} %bitcast.46, f32[4,256]{1,0:T(4,128)S(1)} %multiply_add_fusion), kind=kLoop, calls=%fused_computation.4 | loop fusion | flops 5242880 | bytes 12603392 | tf_op jit(solution)/shard_map/div | solution.py:32
  (19 shorter events, 0.2 us)
Async XLA Ops:
  0.6 2.1 %copy-start = (bf16[256,512]{1,0:T(8,128)(2,1)S(1)}, bf16[256,512]{1,0:T(8,128)(2,1)}, u32[]{:S(2)}) copy-start(bf16[256,512]{1,0:T(8,128)(2,1)} %param.2) | copy-start | bytes 786436
  3.7 15.3 %all-to-all-start = ((f32[8,256,32]{1,2,0:T(8,128)}), f32[8,256,32]{1,2,0:T(8,128)S(1)}, u32[]{:S(2)}, u32[]{:S(2)}) async-start(f32[8,256,32]{1,2,0:T(8,128)} %convolution_bitcast_fusion), calls=%async_computation | async-start | bytes 524288 | tf_op jit(solution)/shard_map/all_to_all | solution.py:56
  19.0 15.5 %collective-permute-start.7 = (bf16[1,256,32]{1,2,0:T(8,128)(2,1)S(1)}, bf16[1,256,32]{1,2,0:T(8,128)(2,1)S(1)}, u32[]{:S(2)}, u32[]{:S(2)}) collective-permute-start(bf16[1,256,32]{1,2,0:T(8,128)(2,1)S(1)} %bitcast.47), channel_id=1, source_target_pairs={{0,0},{1,32},{2,64},{3,96},{4,128},{5,160},{6,192},{7,224},{8,8},{... | collective-permute-start | bytes 49160 | tf_op jit(solution)/shard_map/ppermute | solution.py:65
  19.6 37.7 %collective-permute-start.6 = (bf16[1,256,32]{1,2,0:T(8,128)(2,1)S(1)}, bf16[1,256,32]{1,2,0:T(8,128)(2,1)S(1)}, u32[]{:S(2)}, u32[]{:S(2)}) collective-permute-start(bf16[1,256,32]{1,2,0:T(8,128)(2,1)S(1)} %bitcast.48), channel_id=1, source_target_pairs={{0,7},{1,0},{2,1},{3,2},{4,3},{5,4},{6,5},{7,6},{8,15},{9,8},{10,9... | collective-permute-start | bytes 49160 | tf_op jit(solution)/shard_map/ppermute | solution.py:69
  31.0 26.3 %collective-permute-start.5 = (bf16[1,256,32]{1,2,0:T(8,128)(2,1)S(1)}, bf16[1,256,32]{1,2,0:T(8,128)(2,1)S(1)}, u32[]{:S(2)}, u32[]{:S(2)}) collective-permute-start(bf16[1,256,32]{1,2,0:T(8,128)(2,1)S(1)} %bitcast.49), channel_id=1, source_target_pairs={{0,6},{1,7},{2,0},{3,1},{4,2},{5,3},{6,4},{7,5},{8,14},{9,15},{10,... | collective-permute-start | bytes 49160 | tf_op jit(solution)/shard_map/ppermute | solution.py:69
  32.3 25.0 %collective-permute-start.4 = (bf16[1,256,32]{1,2,0:T(8,128)(2,1)S(1)}, bf16[1,256,32]{1,2,0:T(8,128)(2,1)S(1)}, u32[]{:S(2)}, u32[]{:S(2)}) collective-permute-start(bf16[1,256,32]{1,2,0:T(8,128)(2,1)S(1)} %bitcast.50), channel_id=1, source_target_pairs={{0,5},{1,6},{2,7},{3,0},{4,1},{5,2},{6,3},{7,4},{8,13},{9,14},{10,... | collective-permute-start | bytes 49160 | tf_op jit(solution)/shard_map/ppermute | solution.py:69
  33.8 11.5 %collective-permute-start = (bf16[1,256,32]{1,2,0:T(8,128)(2,1)S(1)}, bf16[1,256,32]{1,2,0:T(8,128)(2,1)S(1)}, u32[]{:S(2)}, u32[]{:S(2)}) collective-permute-start(bf16[1,256,32]{1,2,0:T(8,128)(2,1)S(1)} %bitcast.51), channel_id=1, source_target_pairs={{0,1},{1,2},{2,3},{3,4},{4,5},{5,6},{6,7},{7,0},{8,9},{9,10},{10,1... | collective-permute-start | bytes 49160 | tf_op jit(solution)/shard_map/ppermute | solution.py:69
  34.4 22.8 %collective-permute-start.3 = (bf16[1,256,32]{1,2,0:T(8,128)(2,1)S(1)}, bf16[1,256,32]{1,2,0:T(8,128)(2,1)S(1)}, u32[]{:S(2)}, u32[]{:S(2)}) collective-permute-start(bf16[1,256,32]{1,2,0:T(8,128)(2,1)S(1)} %bitcast.52), channel_id=1, source_target_pairs={{0,4},{1,5},{2,6},{3,7},{4,0},{5,1},{6,2},{7,3},{8,12},{9,13},{10,... | collective-permute-start | bytes 49160 | tf_op jit(solution)/shard_map/ppermute | solution.py:69
  37.2 24.7 %all-to-all-start.1 = ((bf16[32,256,32]{1,2,0:T(8,128)(2,1)}), bf16[32,256,32]{1,2,0:T(8,128)(2,1)S(1)}, u32[]{:S(2)}, u32[]{:S(2)}) async-start(bf16[32,256,32]{1,2,0:T(8,128)(2,1)} %broadcast_in_dim.27), calls=%async_computation.1 | async-start | bytes 1048576 | tf_op jit(solution)/shard_map/all_to_all | solution.py:39
  45.4 6.6 %collective-permute-start.1 = (bf16[1,256,32]{1,2,0:T(8,128)(2,1)S(1)}, bf16[1,256,32]{1,2,0:T(8,128)(2,1)S(1)}, u32[]{:S(2)}, u32[]{:S(2)}) collective-permute-start(bf16[1,256,32]{1,2,0:T(8,128)(2,1)S(1)} %bitcast.53), channel_id=1, source_target_pairs={{0,2},{1,3},{2,4},{3,5},{4,6},{5,7},{6,0},{7,1},{8,10},{9,11},{10,... | collective-permute-start | bytes 49160 | tf_op jit(solution)/shard_map/ppermute | solution.py:69
  52.0 5.3 %collective-permute-start.2 = (bf16[1,256,32]{1,2,0:T(8,128)(2,1)S(1)}, bf16[1,256,32]{1,2,0:T(8,128)(2,1)S(1)}, u32[]{:S(2)}, u32[]{:S(2)}) collective-permute-start(bf16[1,256,32]{1,2,0:T(8,128)(2,1)S(1)} %bitcast.54), channel_id=1, source_target_pairs={{0,3},{1,4},{2,5},{3,6},{4,7},{5,0},{6,1},{7,2},{8,11},{9,12},{10,... | collective-permute-start | bytes 49160 | tf_op jit(solution)/shard_map/ppermute | solution.py:69

commit v10 on v2

--- a/solution.py
+++ b/solution.py
@@ -63,7 +63,18 @@
             t_dst = g_src
             perm.append((s_src * n_tm + t_src, s_dst * n_tm + t_dst))
     moved = lax.ppermute(piece, ("svc", "tm"), perm)
-    row_chunks = gather_by_all_to_all(piece, "tm", n_tm)
+    row_chunks = piece
+    distance = 1
+    while distance < n_tm:
+        pairs = [(a * n_tm + b, a * n_tm + (b ^ distance)) for a in range(n_svc) for b in range(n_tm)]
+        received = lax.ppermute(row_chunks, ("svc", "tm"), pairs)
+        upper = (time_index & distance) != 0
+        row_chunks = jnp.where(
+            upper,
+            jnp.concatenate([received, row_chunks], axis=0),
+            jnp.concatenate([row_chunks, received], axis=0),
+        )
+        distance *= 2
     col_chunks = gather_by_all_to_all(moved, "svc", n_svc)
     bands_row = row_chunks.reshape(BANDS, 2, row_count, BINS)
     row_spec = jnp.transpose(bands_row, (0, 2, 1, 3)).reshape(BANDS, row_count, 2 * BINS)

time: 71 us -> 67 us (0.944); the launches traced: 69.8 us -> 66.7 us
  waiting for transfers between devices: 22.7 us -> 17.6 us
  starting transfers between devices: 20.7 us -> 23.2 us
    all_to_all x2 -> x1, waiting for transfers between devices: 22.7 us -> 11.3 us  [gather_by_all_to_all(): lax.all_to_all(jnp.broadcast_to(x, (size,) + x.shape[1:]), axis, 0, 0, ti...]
    ppermute x0 -> x3, starting transfers between devices: none -> 10.3 us  [body(): received = lax.ppermute(row_chunks, ('svc', 'tm'), pairs)]
    all_to_all x2 -> x1, starting transfers between devices: 20 us -> 12.3 us  [gather_by_all_to_all(): lax.all_to_all(jnp.broadcast_to(x, (size,) + x.shape[1:]), axis, 0, 0, ti...]
    ppermute x0 -> x3, waiting for transfers between devices: none -> 6.29 us  [body(): received = lax.ppermute(row_chunks, ('svc', 'tm'), pairs)]
    broadcast_in_dim x2 -> x1, local copies, waits for them, and re-layouts: 1.52 us -> 0.85 us  [gather_by_all_to_all(): jnp.broadcast_to(x, (size,) + x.shape[1:])]
  transfers between devices with their start and end apart: 3 -> 5, of which waited for: 2 -> 3; matrix products, arithmetic and copies ran while one was open for 0% -> 1% of each run, Pallas kernels for 0% -> 0%
where the time goes in v10:
time: 67 us; the launch traced here: 66.7 us
  starting transfers between devices  23.2 us (35%)
  waiting for transfers between devices  17.6 us (26%)
  blocking collectives  15.1 us (23%)
  other arithmetic  4.8 us (7%)
  matrix products  3.57 us (5%)
  local copies, waits for them, and re-layouts  1.65 us (2%)
  between operations  0.78 us (1%)
    all_to_all x1, blocking collectives, body(): partials = lax.all_to_all(partial_value, 'tm', 0, 0, tiled=True)  15.1 us
    all_to_all x1, starting transfers between devices, gather_by_all_to_all(): lax.all_to_all(jnp.broadcast_to(x, (size,) + x.shape[1:]), axis, 0, 0, ti...  12.3 us
    all_to_all x1, waiting for transfers between devices, gather_by_all_to_all(): lax.all_to_all(jnp.broadcast_to(x, (size,) + x.shape[1:]), axis, 0, 0, ti...  11.3 us
    ppermute x3, starting transfers between devices, body(): received = lax.ppermute(row_chunks, ('svc', 'tm'), pairs)  10.3 us
    ppermute x3, waiting for transfers between devices, body(): received = lax.ppermute(row_chunks, ('svc', 'tm'), pairs)  6.29 us
    dot_general x1, matrix products, all_bands(): jnp.einsum('bpik,bjk->bpij', lhs, col_spec, preferred_element_type=jnp.fl...  3.31 us
    div x1, other arithmetic, all_bands(): (real_part * real_part + imag_part * imag_part) / ((row_power[:, :, None]...  2.5 us
  transfers between devices with their start and end apart: 5, of which 3 were waited for; matrix products, arithmetic and copies ran while one was open for 1% of the time, Pallas kernels for 0%

profile of v10, /device:TPU:1, one launch (start us, length us, event | category | flops | bytes accessed | tf_op | source)
XLA Modules:
  0.0 66.7 jit_solution(15816593688631605403)
XLA Ops:
  0.6 0.0 copy-start
  0.7 0.8 %iota_add_fusion = s32[4,32]{1,0:T(4,128)S(1)} fusion(s32[4]{0:T(128)} %param.3), kind=kLoop, calls=%fused_computation.33 | loop fusion | flops 128 | bytes 528 | tf_op jit(solution)/shard_map/add | solution.py:16
  1.4 1.2 %multiply_convert_fusion.1 = (bf16[512,4,1,32]{0,3,2,1:T(8,128)(2,1)S(1)}, bf16[512,4,1,32]{0,3,2,1:T(8,128)(2,1)S(1)}) fusion(s32[4,32]{1,0:T(4,128)S(1)} %iota_add_fusion, s32[512]{0:T(512)S(1)} %iota_add_fusion.1), kind=kLoop, calls=%fused_computation.24 | loop fusion | flops 1245184 | bytes 264704 | tf_op jit(solution)/shard_map/convert
  2.7 0.0 copy-done
  2.7 0.3 convolution_bitcast_fusion
  3.0 15.1 %all_to_all.10 = f32[8,256,32]{1,2,0:T(8,128)S(1)} all-to-all(f32[8,256,32]{1,2,0:T(8,128)S(1)} %convolution_bitcast_fusion), channel_id=1, replica_groups=mesh['svc'=32,'tm'=8] {'tm'}, dimensions={0} | all-to-all | bytes 524288 | tf_op jit(solution)/shard_map/all_to_all | solution.py:56
  18.1 0.6 collective-permute-start
  18.6 0.7 collective-permute-start.3
  19.3 1.5 %collective-permute-done = bf16[1,256,32]{1,2,0:T(8,128)(2,1)S(1)} collective-permute-done((bf16[1,256,32]{1,2,0:T(8,128)(2,1)S(1)}, bf16[1,256,32]{1,2,0:T(8,128)(2,1)S(1)}, u32[]{:S(2)}, u32[]{:S(2)}) %collective-permute-start) | collective-permute-done | bytes 16416 | tf_op jit(solution)/shard_map/ppermute | solution.py:70
  20.8 9.5 %collective-permute-start.1 = (bf16[2,256,32]{1,2,0:T(8,128)(2,1)S(1)}, bf16[2,256,32]{1,2,0:T(8,128)(2,1)S(1)}, u32[]{:S(2)}, u32[]{:S(2)}) collective-permute-start(bf16[2,256,32]{1,2,0:T(8,128)(2,1)S(1)} %maximum_select_fusion.2), channel_id=1, source_target_pairs={{0,2},{1,3},{2,0},{3,1},{4,6},{5,7},{6,4},{7,5},{8,10},{9,11},{10,... | collective-permute-start | bytes 98312 | tf_op jit(solution)/shard_map/ppermute | solution.py:70
  30.2 0.0 collective-permute-done.3
  30.3 0.9 %broadcast_in_dim.5 = bf16[32,256,32]{1,2,0:T(8,128)(2,1)} broadcast(bf16[256,32]{0,1:T(8,128)(2,1)S(1)} %bitcast.47), dimensions={1,2} | broadcast | bytes 540672 | tf_op jit(solution)/shard_map/broadcast_in_dim | solution.py:39
  31.1 12.3 %all-to-all-start.1 = ((bf16[32,256,32]{1,2,0:T(8,128)(2,1)}), bf16[32,256,32]{1,2,0:T(8,128)(2,1)S(1)}, u32[]{:S(2)}, u32[]{:S(2)}) async-start(bf16[32,256,32]{1,2,0:T(8,128)(2,1)} %broadcast_in_dim.5), calls=%async_computation.1 | async-start | bytes 1048576 | tf_op jit(solution)/shard_map/all_to_all | solution.py:39
  43.4 0.0 collective-permute-done.1
  43.4 0.3 collective-permute-start.2
  43.7 4.8 %collective-permute-done.2 = bf16[4,256,32]{1,2,0:T(8,128)(2,1)S(1)} collective-permute-done((bf16[4,256,32]{1,2,0:T(8,128)(2,1)S(1)}, bf16[4,256,32]{1,2,0:T(8,128)(2,1)S(1)}, u32[]{:S(2)}, u32[]{:S(2)}) %collective-permute-start.2) | collective-permute-done | bytes 65568 | tf_op jit(solution)/shard_map/ppermute | solution.py:70
  48.6 11.3 %all-to-all-done.1 = bf16[32,256,32]{1,2,0:T(8,128)(2,1)S(1)} async-done(((bf16[32,256,32]{1,2,0:T(8,128)(2,1)}), bf16[32,256,32]{1,2,0:T(8,128)(2,1)S(1)}, u32[]{:S(2)}, u32[]{:S(2)}) %all-to-all-start.1) | async-done | bytes 524320 | tf_op jit(solution)/shard_map/all_to_all | solution.py:39
  59.9 0.1 multiply_reduce_fusion
  60.1 0.4 copy.5
  60.5 0.4 reshape.135
  60.9 3.3 %fusion.13 = (bf16[4,2,256,1024]{3,2,1,0:T(8,128)(2,1)}, f32[4,2,256,1024]{3,2,1,0:T(8,128)S(1)}) fusion(bf16[4,1024,64,1]{1,2,0,3:T(8,128)(2,1)S(1)} %reshape.135, bf16[4,1,256,64]{2,3,1,0:T(8,128)(2,1)S(1)} %maximum_bitcast_fusion, bf16[4,1,256,64]{2,3,1,0:T(8,128)(2,1)S(1)} %bitcast.41), kind=kOutput, calls=%fused_computation.37 | convolution fusion | flops 272760832 | bytes 13369344 | tf_op jit(solution)/shard_map/bpik,bjk->bpij/dot_general | solution.py:27
  64.2 2.5 %fusion.2 = f32[4,256,1024]{2,1,0:T(8,128)} fusion(f32[4,2,256,1024]{3,2,1,0:T(8,128)S(1)} %get-tuple-element.7, f32[4,1024]{1,0:T(4,128)S(1)} %bitcast.43, f32[4,256]{1,0:T(4,128)S(1)} %multiply_add_fusion), kind=kLoop, calls=%fused_computation.3 | loop fusion | flops 5242880 | bytes 12603392 | tf_op jit(solution)/shard_map/div | solution.py:32
  (12 shorter events, 0.2 us)
Async XLA Ops:
  0.6 2.1 %copy-start = (bf16[256,512]{1,0:T(8,128)(2,1)S(1)}, bf16[256,512]{1,0:T(8,128)(2,1)}, u32[]{:S(2)}) copy-start(bf16[256,512]{1,0:T(8,128)(2,1)} %param.2) | copy-start | bytes 786436
  18.1 2.7 %collective-permute-start = (bf16[1,256,32]{1,2,0:T(8,128)(2,1)S(1)}, bf16[1,256,32]{1,2,0:T(8,128)(2,1)S(1)}, u32[]{:S(2)}, u32[]{:S(2)}) collective-permute-start(bf16[1,256,32]{1,2,0:T(8,128)(2,1)S(1)} %bitcast.44), channel_id=1, source_target_pairs={{0,1},{1,0},{2,3},{3,2},{4,5},{5,4},{6,7},{7,6},{8,9},{9,8},{10,11... | collective-permute-start | bytes 49160 | tf_op jit(solution)/shard_map/ppermute | solution.py:70
  18.6 11.6 %collective-permute-start.3 = (bf16[1,256,32]{1,2,0:T(8,128)(2,1)S(1)}, bf16[1,256,32]{1,2,0:T(8,128)(2,1)S(1)}, u32[]{:S(2)}, u32[]{:S(2)}) collective-permute-start(bf16[1,256,32]{1,2,0:T(8,128)(2,1)S(1)} %bitcast.45), channel_id=1, source_target_pairs={{0,0},{1,32},{2,64},{3,96},{4,128},{5,160},{6,192},{7,224},{8,8},{... | collective-permute-start | bytes 49160 | tf_op jit(solution)/shard_map/ppermute | solution.py:65
  20.8 22.6 %collective-permute-start.1 = (bf16[2,256,32]{1,2,0:T(8,128)(2,1)S(1)}, bf16[2,256,32]{1,2,0:T(8,128)(2,1)S(1)}, u32[]{:S(2)}, u32[]{:S(2)}) collective-permute-start(bf16[2,256,32]{1,2,0:T(8,128)(2,1)S(1)} %maximum_select_fusion.2), channel_id=1, source_target_pairs={{0,2},{1,3},{2,0},{3,1},{4,6},{5,7},{6,4},{7,5},{8,10},{9,11},{10,... | collective-permute-start | bytes 98312 | tf_op jit(solution)/shard_map/ppermute | solution.py:70
  31.1 28.8 %all-to-all-start.1 = ((bf16[32,256,32]{1,2,0:T(8,128)(2,1)}), bf16[32,256,32]{1,2,0:T(8,128)(2,1)S(1)}, u32[]{:S(2)}, u32[]{:S(2)}) async-start(bf16[32,256,32]{1,2,0:T(8,128)(2,1)} %broadcast_in_dim.5), calls=%async_computation.1 | async-start | bytes 1048576 | tf_op jit(solution)/shard_map/all_to_all | solution.py:39
  43.4 5.1 %collective-permute-start.2 = (bf16[4,256,32]{1,2,0:T(8,128)(2,1)S(1)}, bf16[4,256,32]{1,2,0:T(8,128)(2,1)S(1)}, u32[]{:S(2)}, u32[]{:S(2)}) collective-permute-start(bf16[4,256,32]{1,2,0:T(8,128)(2,1)S(1)} %maximum_select_fusion.1), channel_id=1, source_target_pairs={{0,4},{1,5},{2,6},{3,7},{4,0},{5,1},{6,2},{7,3},{8,12},{9,13},{10,... | collective-permute-start | bytes 196616 | tf_op jit(solution)/shard_map/ppermute | solution.py:70

commit v11 on v10

--- a/solution.py
+++ b/solution.py
@@ -53,8 +53,17 @@
     partial_value = jnp.einsum(
         "nt,tcb->cnb", metrics, dft_table, preferred_element_type=jnp.float32
     )
-    partials = lax.all_to_all(partial_value, "tm", 0, 0, tiled=True)
-    piece = jnp.sum(partials, axis=0, keepdims=True).astype(jnp.bfloat16)
+    held = partial_value
+    distance = n_tm // 2
+    while distance >= 1:
+        half = held.shape[0] // 2
+        upper = ((time_index & distance) != 0).astype(jnp.int32)
+        kept = lax.dynamic_slice_in_dim(held, upper * half, half, 0)
+        sent = lax.dynamic_slice_in_dim(held, (1 - upper) * half, half, 0)
+        pairs = [(a * n_tm + b, a * n_tm + (b ^ distance)) for a in range(n_svc) for b in range(n_tm)]
+        held = kept + lax.ppermute(sent, ("svc", "tm"), pairs)
+        distance //= 2
+    piece = held.astype(jnp.bfloat16)
     perm = []
     for s_src in range(n_svc):
         g_src, r_src = divmod(s_src, owners)

time: 67 us -> 69.7 us (1.040)
  blocking collectives: 15.1 us -> 0 us
  starting transfers between devices: 23.2 us -> 37.7 us
  waiting for transfers between devices: 17.6 us -> 20.9 us
    all_to_all x1 -> x0, blocking collectives: 15.1 us -> none  [body(): partials = lax.all_to_all(partial_value, 'tm', 0, 0, tiled=True)]
    ppermute x0 -> x3, starting transfers between devices: none -> 8.78 us  [body(): held = kept + lax.ppermute(sent, ('svc', 'tm'), pairs)]
    ppermute x0 -> x3, waiting for transfers between devices: none -> 5.64 us  [body(): held = kept + lax.ppermute(sent, ('svc', 'tm'), pairs)]
    ppermute x3, starting transfers between devices: 10.3 us -> 13.3 us  [body(): received = lax.ppermute(row_chunks, ('svc', 'tm'), pairs)]
    all_to_all x1, starting transfers between devices: 12.3 us -> 15 us  [gather_by_all_to_all(): lax.all_to_all(jnp.broadcast_to(x, (size,) + x.shape[1:]), axis, 0, 0, ti...]
    ppermute x3, waiting for transfers between devices: 6.29 us -> 4.08 us  [body(): received = lax.ppermute(row_chunks, ('svc', 'tm'), pairs)]
  transfers between devices with their start and end apart: 5 -> 8, of which waited for: 3 -> 6; matrix products, arithmetic and copies ran while one was open for 1% -> 1% of each run, Pallas kernels for 0% -> 0%
where the time goes in v11:
time: 69.7 us; the launch traced here: 69.4 us
  starting transfers between devices  37.7 us (54%)
  waiting for transfers between devices  20.9 us (30%)
  other arithmetic  4.81 us (7%)
  matrix products  3.56 us (5%)
  local copies, waits for them, and re-layouts  1.69 us (2%)
  between operations  0.81 us (1%)
    all_to_all x1, starting transfers between devices, gather_by_all_to_all(): lax.all_to_all(jnp.broadcast_to(x, (size,) + x.shape[1:]), axis, 0, 0, ti...  15 us
    ppermute x3, starting transfers between devices, body(): received = lax.ppermute(row_chunks, ('svc', 'tm'), pairs)  13.3 us
    all_to_all x1, waiting for transfers between devices, gather_by_all_to_all(): lax.all_to_all(jnp.broadcast_to(x, (size,) + x.shape[1:]), axis, 0, 0, ti...  11.1 us
    ppermute x3, starting transfers between devices, body(): held = kept + lax.ppermute(sent, ('svc', 'tm'), pairs)  8.78 us
    ppermute x3, waiting for transfers between devices, body(): held = kept + lax.ppermute(sent, ('svc', 'tm'), pairs)  5.64 us
    ppermute x3, waiting for transfers between devices, body(): received = lax.ppermute(row_chunks, ('svc', 'tm'), pairs)  4.08 us
    dot_general x1, matrix products, all_bands(): jnp.einsum('bpik,bjk->bpij', lhs, col_spec, preferred_element_type=jnp.fl...  3.31 us
    div x1, other arithmetic, all_bands(): (real_part * real_part + imag_part * imag_part) / ((row_power[:, :, None]...  2.5 us
  transfers between devices with their start and end apart: 8, of which 6 were waited for; matrix products, arithmetic and copies ran while one was open for 1% of the time, Pallas kernels for 0%

profile of v11, /device:TPU:1, one launch (start us, length us, event | category | flops | bytes accessed | tf_op | source)
XLA Modules:
  0.0 69.4 jit_solution(834957407898723737)
XLA Ops:
  0.6 0.0 copy-start
  0.7 0.8 %iota_add_fusion = s32[4,32]{1,0:T(4,128)S(1)} fusion(s32[4]{0:T(128)} %param.3), kind=kLoop, calls=%fused_computation.36 | loop fusion | flops 128 | bytes 528 | tf_op jit(solution)/shard_map/add | solution.py:16
  1.4 1.2 %multiply_convert_fusion.1 = (bf16[512,4,1,32]{0,3,2,1:T(8,128)(2,1)S(1)}, bf16[512,4,1,32]{0,3,2,1:T(8,128)(2,1)S(1)}) fusion(s32[4,32]{1,0:T(4,128)S(1)} %iota_add_fusion, s32[512]{0:T(512)S(1)} %iota_add_fusion.1), kind=kLoop, calls=%fused_computation.24 | loop fusion | flops 1245184 | bytes 264704 | tf_op jit(solution)/shard_map/convert
  2.7 0.0 copy-done
  2.7 0.3 fusion.10
  3.0 3.8 %collective-permute-start = (f32[4,256,32]{1,2,0:T(8,128)S(1)}, f32[4,256,32]{1,2,0:T(8,128)S(1)}, u32[]{:S(2)}, u32[]{:S(2)}) collective-permute-start(f32[4,256,32]{1,2,0:T(8,128)S(1)} %dynamic-slice_bitcast_fusion), channel_id=1, source_target_pairs={{0,4},{1,5},{2,6},{3,7},{4,0},{5,1},{6,2},{7,3},{8,12},{9,13},{10,... | collective-permute-start | bytes 393224 | tf_op jit(solution)/shard_map/ppermute | solution.py:64
  6.8 2.4 %collective-permute-done = f32[4,256,32]{1,2,0:T(8,128)S(1)} collective-permute-done((f32[4,256,32]{1,2,0:T(8,128)S(1)}, f32[4,256,32]{1,2,0:T(8,128)S(1)}, u32[]{:S(2)}, u32[]{:S(2)}) %collective-permute-start) | collective-permute-done | bytes 131104 | tf_op jit(solution)/shard_map/ppermute | solution.py:64
  9.2 3.4 %collective-permute-start.1 = (f32[2,256,32]{1,2,0:T(8,128)S(1)}, f32[2,256,32]{1,2,0:T(8,128)S(1)}, u32[]{:S(2)}, u32[]{:S(2)}) collective-permute-start(f32[2,256,32]{1,2,0:T(8,128)S(1)} %constant_dynamic-slice_fusion.1), channel_id=1, source_target_pairs={{0,2},{1,3},{2,0},{3,1},{4,6},{5,7},{6,4},{7,5},{8,10},{9,11},{10,... | collective-permute-start | bytes 196616 | tf_op jit(solution)/shard_map/ppermute | solution.py:64
  12.7 1.7 %collective-permute-done.1 = f32[2,256,32]{1,2,0:T(8,128)S(1)} collective-permute-done((f32[2,256,32]{1,2,0:T(8,128)S(1)}, f32[2,256,32]{1,2,0:T(8,128)S(1)}, u32[]{:S(2)}, u32[]{:S(2)}) %collective-permute-start.1) | collective-permute-done | bytes 65568 | tf_op jit(solution)/shard_map/ppermute | solution.py:64
  14.3 1.5 %collective-permute-start.2 = (f32[1,256,32]{1,2,0:T(8,128)S(1)}, f32[1,256,32]{1,2,0:T(8,128)S(1)}, u32[]{:S(2)}, u32[]{:S(2)}) collective-permute-start(f32[1,256,32]{1,2,0:T(8,128)S(1)} %constant_dynamic-slice_fusion), channel_id=1, source_target_pairs={{0,1},{1,0},{2,3},{3,2},{4,5},{5,4},{6,7},{7,6},{8,9},{9,8},{10,11... | collective-permute-start | bytes 98312 | tf_op jit(solution)/shard_map/ppermute | solution.py:64
  15.9 1.6 %collective-permute-done.2 = f32[1,256,32]{1,2,0:T(8,128)S(1)} collective-permute-done((f32[1,256,32]{1,2,0:T(8,128)S(1)}, f32[1,256,32]{1,2,0:T(8,128)S(1)}, u32[]{:S(2)}, u32[]{:S(2)}) %collective-permute-start.2) | collective-permute-done | bytes 32800 | tf_op jit(solution)/shard_map/ppermute | solution.py:64
  17.5 1.1 %collective-permute-start.3 = (bf16[1,256,32]{1,2,0:T(8,128)(2,1)S(1)}, bf16[1,256,32]{1,2,0:T(8,128)(2,1)S(1)}, u32[]{:S(2)}, u32[]{:S(2)}) collective-permute-start(bf16[1,256,32]{1,2,0:T(8,128)(2,1)S(1)} %add_convert_fusion), channel_id=1, source_target_pairs={{0,1},{1,0},{2,3},{3,2},{4,5},{5,4},{6,7},{7,6},{8,9},{9,8},{10,11... | collective-permute-start | bytes 49160 | tf_op jit(solution)/shard_map/ppermute | solution.py:79
  18.6 0.7 collective-permute-start.6
  19.3 0.8 %collective-permute-done.3 = bf16[1,256,32]{1,2,0:T(8,128)(2,1)S(1)} collective-permute-done((bf16[1,256,32]{1,2,0:T(8,128)(2,1)S(1)}, bf16[1,256,32]{1,2,0:T(8,128)(2,1)S(1)}, u32[]{:S(2)}, u32[]{:S(2)}) %collective-permute-start.3) | collective-permute-done | bytes 16416 | tf_op jit(solution)/shard_map/ppermute | solution.py:79
  20.1 10.2 %collective-permute-start.4 = (bf16[2,256,32]{1,2,0:T(8,128)(2,1)S(1)}, bf16[2,256,32]{1,2,0:T(8,128)(2,1)S(1)}, u32[]{:S(2)}, u32[]{:S(2)}) collective-permute-start(bf16[2,256,32]{1,2,0:T(8,128)(2,1)S(1)} %maximum_select_fusion.2), channel_id=1, source_target_pairs={{0,2},{1,3},{2,0},{3,1},{4,6},{5,7},{6,4},{7,5},{8,10},{9,11},{10,... | collective-permute-start | bytes 98312 | tf_op jit(solution)/shard_map/ppermute | solution.py:79
  30.3 0.0 collective-permute-done.6
  30.3 0.9 %broadcast_in_dim.5 = bf16[32,256,32]{1,2,0:T(8,128)(2,1)} broadcast(bf16[256,32]{0,1:T(8,128)(2,1)S(1)} %bitcast.43), dimensions={1,2} | broadcast | bytes 540672 | tf_op jit(solution)/shard_map/broadcast_in_dim | solution.py:39
  31.1 15.0 %all-to-all-start = ((bf16[32,256,32]{1,2,0:T(8,128)(2,1)}), bf16[32,256,32]{1,2,0:T(8,128)(2,1)S(1)}, u32[]{:S(2)}, u32[]{:S(2)}) async-start(bf16[32,256,32]{1,2,0:T(8,128)(2,1)} %broadcast_in_dim.5), calls=%async_computation | async-start | bytes 1048576 | tf_op jit(solution)/shard_map/all_to_all | solution.py:39
  46.1 0.0 collective-permute-done.4
  46.1 2.0 %collective-permute-start.5 = (bf16[4,256,32]{1,2,0:T(8,128)(2,1)S(1)}, bf16[4,256,32]{1,2,0:T(8,128)(2,1)S(1)}, u32[]{:S(2)}, u32[]{:S(2)}) collective-permute-start(bf16[4,256,32]{1,2,0:T(8,128)(2,1)S(1)} %maximum_select_fusion.1), channel_id=1, source_target_pairs={{0,4},{1,5},{2,6},{3,7},{4,0},{5,1},{6,2},{7,3},{8,12},{9,13},{10,... | collective-permute-start | bytes 196616 | tf_op jit(solution)/shard_map/ppermute | solution.py:79
  48.1 3.3 %collective-permute-done.5 = bf16[4,256,32]{1,2,0:T(8,128)(2,1)S(1)} collective-permute-done((bf16[4,256,32]{1,2,0:T(8,128)(2,1)S(1)}, bf16[4,256,32]{1,2,0:T(8,128)(2,1)S(1)}, u32[]{:S(2)}, u32[]{:S(2)}) %collective-permute-start.5) | collective-permute-done | bytes 65568 | tf_op jit(solution)/shard_map/ppermute | solution.py:79
  51.5 11.1 %all-to-all-done = bf16[32,256,32]{1,2,0:T(8,128)(2,1)S(1)} async-done(((bf16[32,256,32]{1,2,0:T(8,128)(2,1)}), bf16[32,256,32]{1,2,0:T(8,128)(2,1)S(1)}, u32[]{:S(2)}, u32[]{:S(2)}) %all-to-all-start) | async-done | bytes 524320 | tf_op jit(solution)/shard_map/all_to_all | solution.py:39
  62.7 0.1 multiply_reduce_fusion
  62.8 0.4 copy.5
  63.2 0.4 reshape.126
  63.6 3.3 %fusion.14 = (bf16[4,2,256,1024]{3,2,1,0:T(8,128)(2,1)}, f32[4,2,256,1024]{3,2,1,0:T(8,128)S(1)}) fusion(bf16[4,1024,64,1]{1,2,0,3:T(8,128)(2,1)S(1)} %reshape.126, bf16[4,1,256,64]{2,3,1,0:T(8,128)(2,1)S(1)} %maximum_bitcast_fusion, bf16[4,1,256,64]{2,3,1,0:T(8,128)(2,1)S(1)} %bitcast.40), kind=kOutput, calls=%fused_computation.42 | convolution fusion | flops 272760832 | bytes 13369344 | tf_op jit(solution)/shard_map/bpik,bjk->bpij/dot_general | solution.py:27
  66.9 2.5 %fusion.2 = f32[4,256,1024]{2,1,0:T(8,128)} fusion(f32[4,2,256,1024]{3,2,1,0:T(8,128)S(1)} %get-tuple-element.7, f32[4,1024]{1,0:T(4,128)S(1)} %bitcast.42, f32[4,256]{1,0:T(4,128)S(1)} %multiply_add_fusion), kind=kLoop, calls=%fused_computation.3 | loop fusion | flops 5242880 | bytes 12603392 | tf_op jit(solution)/shard_map/div | solution.py:32
  (17 shorter events, 0.2 us)
Async XLA Ops:
  0.6 2.1 %copy-start = (bf16[256,512]{1,0:T(8,128)(2,1)S(1)}, bf16[256,512]{1,0:T(8,128)(2,1)}, u32[]{:S(2)}) copy-start(bf16[256,512]{1,0:T(8,128)(2,1)} %param.2) | copy-start | bytes 786436
  3.0 6.2 %collective-permute-start = (f32[4,256,32]{1,2,0:T(8,128)S(1)}, f32[4,256,32]{1,2,0:T(8,128)S(1)}, u32[]{:S(2)}, u32[]{:S(2)}) collective-permute-start(f32[4,256,32]{1,2,0:T(8,128)S(1)} %dynamic-slice_bitcast_fusion), channel_id=1, source_target_pairs={{0,4},{1,5},{2,6},{3,7},{4,0},{5,1},{6,2},{7,3},{8,12},{9,13},{10,... | collective-permute-start | bytes 393224 | tf_op jit(solution)/shard_map/ppermute | solution.py:64
  9.2 5.1 %collective-permute-start.1 = (f32[2,256,32]{1,2,0:T(8,128)S(1)}, f32[2,256,32]{1,2,0:T(8,128)S(1)}, u32[]{:S(2)}, u32[]{:S(2)}) collective-permute-start(f32[2,256,32]{1,2,0:T(8,128)S(1)} %constant_dynamic-slice_fusion.1), channel_id=1, source_target_pairs={{0,2},{1,3},{2,0},{3,1},{4,6},{5,7},{6,4},{7,5},{8,10},{9,11},{10,... | collective-permute-start | bytes 196616 | tf_op jit(solution)/shard_map/ppermute | solution.py:64
  14.3 3.1 %collective-permute-start.2 = (f32[1,256,32]{1,2,0:T(8,128)S(1)}, f32[1,256,32]{1,2,0:T(8,128)S(1)}, u32[]{:S(2)}, u32[]{:S(2)}) collective-permute-start(f32[1,256,32]{1,2,0:T(8,128)S(1)} %constant_dynamic-slice_fusion), channel_id=1, source_target_pairs={{0,1},{1,0},{2,3},{3,2},{4,5},{5,4},{6,7},{7,6},{8,9},{9,8},{10,11... | collective-permute-start | bytes 98312 | tf_op jit(solution)/shard_map/ppermute | solution.py:64
  17.5 2.6 %collective-permute-start.3 = (bf16[1,256,32]{1,2,0:T(8,128)(2,1)S(1)}, bf16[1,256,32]{1,2,0:T(8,128)(2,1)S(1)}, u32[]{:S(2)}, u32[]{:S(2)}) collective-permute-start(bf16[1,256,32]{1,2,0:T(8,128)(2,1)S(1)} %add_convert_fusion), channel_id=1, source_target_pairs={{0,1},{1,0},{2,3},{3,2},{4,5},{5,4},{6,7},{7,6},{8,9},{9,8},{10,11... | collective-permute-start | bytes 49160 | tf_op jit(solution)/shard_map/ppermute | solution.py:79
  18.6 11.6 %collective-permute-start.6 = (bf16[1,256,32]{1,2,0:T(8,128)(2,1)S(1)}, bf16[1,256,32]{1,2,0:T(8,128)(2,1)S(1)}, u32[]{:S(2)}, u32[]{:S(2)}) collective-permute-start(bf16[1,256,32]{1,2,0:T(8,128)(2,1)S(1)} %add_convert_fusion), channel_id=1, source_target_pairs={{0,0},{1,32},{2,64},{3,96},{4,128},{5,160},{6,192},{7,224},{8,8},{... | collective-permute-start | bytes 49160 | tf_op jit(solution)/shard_map/ppermute | solution.py:74
  20.1 26.0 %collective-permute-start.4 = (bf16[2,256,32]{1,2,0:T(8,128)(2,1)S(1)}, bf16[2,256,32]{1,2,0:T(8,128)(2,1)S(1)}, u32[]{:S(2)}, u32[]{:S(2)}) collective-permute-start(bf16[2,256,32]{1,2,0:T(8,128)(2,1)S(1)} %maximum_select_fusion.2), channel_id=1, source_target_pairs={{0,2},{1,3},{2,0},{3,1},{4,6},{5,7},{6,4},{7,5},{8,10},{9,11},{10,... | collective-permute-start | bytes 98312 | tf_op jit(solution)/shard_map/ppermute | solution.py:79
  31.1 31.5 %all-to-all-start = ((bf16[32,256,32]{1,2,0:T(8,128)(2,1)}), bf16[32,256,32]{1,2,0:T(8,128)(2,1)S(1)}, u32[]{:S(2)}, u32[]{:S(2)}) async-start(bf16[32,256,32]{1,2,0:T(8,128)(2,1)} %broadcast_in_dim.5), calls=%async_computation | async-start | bytes 1048576 | tf_op jit(solution)/shard_map/all_to_all | solution.py:39
  46.1 5.3 %collective-permute-start.5 = (bf16[4,256,32]{1,2,0:T(8,128)(2,1)S(1)}, bf16[4,256,32]{1,2,0:T(8,128)(2,1)S(1)}, u32[]{:S(2)}, u32[]{:S(2)}) collective-permute-start(bf16[4,256,32]{1,2,0:T(8,128)(2,1)S(1)} %maximum_select_fusion.1), channel_id=1, source_target_pairs={{0,4},{1,5},{2,6},{3,7},{4,0},{5,1},{6,2},{7,3},{8,12},{9,13},{10,... | collective-permute-start | bytes 196616 | tf_op jit(solution)/shard_map/ppermute | solution.py:79

commit v12 on v2

--- a/solution.py
+++ b/solution.py
@@ -53,8 +53,12 @@
     partial_value = jnp.einsum(
         "nt,tcb->cnb", metrics, dft_table, preferred_element_type=jnp.float32
     )
-    partials = lax.all_to_all(partial_value, "tm", 0, 0, tiled=True)
-    piece = jnp.sum(partials, axis=0, keepdims=True).astype(jnp.bfloat16)
+    span = n_tm // 2
+    groups = partial_value.reshape(n_tm // span, span, row_count, chunk)
+    outgoing = jnp.repeat(groups, span, axis=0)
+    partials = lax.all_to_all(outgoing, "tm", 0, 0, tiled=True)
+    own_group = jnp.sum(partials, axis=0).astype(jnp.bfloat16)
+    piece = lax.dynamic_slice_in_dim(own_group, time_index % span, 1, 0)
     perm = []
     for s_src in range(n_svc):
         g_src, r_src = divmod(s_src, owners)
@@ -63,7 +67,14 @@
             t_dst = g_src
             perm.append((s_src * n_tm + t_src, s_dst * n_tm + t_dst))
     moved = lax.ppermute(piece, ("svc", "tm"), perm)
-    row_chunks = gather_by_all_to_all(piece, "tm", n_tm)
+    pairs = [(a * n_tm + b, a * n_tm + (b ^ span)) for a in range(n_svc) for b in range(n_tm)]
+    received = lax.ppermute(own_group, ("svc", "tm"), pairs)
+    upper = (time_index & span) != 0
+    row_chunks = jnp.where(
+        upper,
+        jnp.concatenate([received, own_group], axis=0),
+        jnp.concatenate([own_group, received], axis=0),
+    )
     col_chunks = gather_by_all_to_all(moved, "svc", n_svc)
     bands_row = row_chunks.reshape(BANDS, 2, row_count, BINS)
     row_spec = jnp.transpose(bands_row, (0, 2, 1, 3)).reshape(BANDS, row_count, 2 * BINS)

time: 71 us -> 75.9 us (1.069); the launches traced: 69.8 us -> 75.6 us
  blocking collectives: 15.1 us -> 0 us
  waiting for transfers between devices: 22.7 us -> 33.5 us
  starting transfers between devices: 20.7 us -> 30.1 us
    all_to_all x0 -> x1, waiting for transfers between devices: none -> 17.3 us  [body(): partials = lax.all_to_all(outgoing, 'tm', 0, 0, tiled=True)]
    all_to_all x1 -> x0, blocking collectives: 15.1 us -> none  [body(): partials = lax.all_to_all(partial_value, 'tm', 0, 0, tiled=True)]
    all_to_all x2 -> x1, waiting for transfers between devices: 22.7 us -> 11.3 us  [gather_by_all_to_all(): lax.all_to_all(jnp.broadcast_to(x, (size,) + x.shape[1:]), axis, 0, 0, ti...]
    all_to_all x0 -> x1, starting transfers between devices: none -> 7.48 us  [body(): partials = lax.all_to_all(outgoing, 'tm', 0, 0, tiled=True)]
    ppermute x0 -> x1, waiting for transfers between devices: none -> 4.91 us  [body(): received = lax.ppermute(own_group, ('svc', 'tm'), pairs)]
    all_to_all x2 -> x1, starting transfers between devices: 20 us -> 21.7 us  [gather_by_all_to_all(): lax.all_to_all(jnp.broadcast_to(x, (size,) + x.shape[1:]), axis, 0, 0, ti...]
    broadcast_in_dim x0 -> x1, local copies, waits for them, and re-layouts: none -> 1.1 us  [body(): outgoing = jnp.repeat(groups, span, axis=0)]
  transfers between devices with their start and end apart: 3 -> 4, of which waited for: 2 -> 3; matrix products, arithmetic and copies ran while one was open for 0% -> 0% of each run, Pallas kernels for 0% -> 0%
where the time goes in v12:
time: 75.9 us; the launch traced here: 75.6 us
  waiting for transfers between devices  33.5 us (44%)
  starting transfers between devices  30.1 us (40%)
  other arithmetic  4.83 us (6%)
  matrix products  3.57 us (5%)
  local copies, waits for them, and re-layouts  2.75 us (4%)
  between operations  0.77 us (1%)
    all_to_all x1, starting transfers between devices, gather_by_all_to_all(): lax.all_to_all(jnp.broadcast_to(x, (size,) + x.shape[1:]), axis, 0, 0, ti...  21.7 us
    all_to_all x1, waiting for transfers between devices, body(): partials = lax.all_to_all(outgoing, 'tm', 0, 0, tiled=True)  17.3 us
    all_to_all x1, waiting for transfers between devices, gather_by_all_to_all(): lax.all_to_all(jnp.broadcast_to(x, (size,) + x.shape[1:]), axis, 0, 0, ti...  11.3 us
    all_to_all x1, starting transfers between devices, body(): partials = lax.all_to_all(outgoing, 'tm', 0, 0, tiled=True)  7.48 us
    ppermute x1, waiting for transfers between devices, body(): received = lax.ppermute(own_group, ('svc', 'tm'), pairs)  4.91 us
    dot_general x1, matrix products, all_bands(): jnp.einsum('bpik,bjk->bpij', lhs, col_spec, preferred_element_type=jnp.fl...  3.31 us
    div x1, other arithmetic, all_bands(): (real_part * real_part + imag_part * imag_part) / ((row_power[:, :, None]...  2.5 us
  transfers between devices with their start and end apart: 4, of which 3 were waited for; matrix products, arithmetic and copies ran while one was open for 0% of the time, Pallas kernels for 0%

profile of v12, /device:TPU:1, one launch (start us, length us, event | category | flops | bytes accessed | tf_op | source)
XLA Modules:
  0.0 75.6 jit_solution(16026750189095200492)
XLA Ops:
  0.6 0.0 copy-start
  0.7 0.8 %iota_add_fusion = s32[4,32]{1,0:T(4,128)S(1)} fusion(s32[4]{0:T(128)} %param.3), kind=kLoop, calls=%fused_computation.30 | loop fusion | flops 128 | bytes 528 | tf_op jit(solution)/shard_map/add | solution.py:16
  1.4 1.2 %multiply_convert_fusion.1 = (bf16[512,4,1,32]{0,3,2,1:T(8,128)(2,1)S(1)}, bf16[512,4,1,32]{0,3,2,1:T(8,128)(2,1)S(1)}) fusion(s32[4,32]{1,0:T(4,128)S(1)} %iota_add_fusion, s32[512]{0:T(512)S(1)} %iota_add_fusion.1), kind=kLoop, calls=%fused_computation.24 | loop fusion | flops 1245184 | bytes 264704 | tf_op jit(solution)/shard_map/convert
  2.7 0.0 copy-done
  2.7 0.3 fusion.10
  3.0 1.1 %broadcast_in_dim.6 = f32[2,4,4,256,32]{3,4,2,1,0:T(8,128)} broadcast(f32[2,4,256,32]{2,3,1,0:T(8,128)S(1)} %bitcast.41), dimensions={0,2,3,4} | broadcast | bytes 1310720 | tf_op jit(solution)/shard_map/broadcast_in_dim | solution.py:58
  4.1 7.5 %all-to-all-start = ((f32[8,4,256,32]{2,3,1,0:T(8,128)}), f32[8,4,256,32]{2,3,1,0:T(8,128)S(1)}, u32[]{:S(2)}, u32[]{:S(2)}) async-start(f32[8,4,256,32]{2,3,1,0:T(8,128)} %bitcast.4), calls=%async_computation | async-start | bytes 2097152 | tf_op jit(solution)/shard_map/all_to_all | solution.py:59
  11.5 17.3 %all-to-all-done = f32[8,4,256,32]{2,3,1,0:T(8,128)S(1)} async-done(((f32[8,4,256,32]{2,3,1,0:T(8,128)}), f32[8,4,256,32]{2,3,1,0:T(8,128)S(1)}, u32[]{:S(2)}, u32[]{:S(2)}) %all-to-all-start) | async-done | bytes 1048608 | tf_op jit(solution)/shard_map/all_to_all | solution.py:59
  28.9 0.1 reduce_sum.27
  29.0 0.7 collective-permute-start.1
  29.6 0.0 collective-permute-done.1
  29.6 0.9 %broadcast_in_dim.8 = bf16[32,256,32]{1,2,0:T(8,128)(2,1)} broadcast(bf16[256,32]{0,1:T(8,128)(2,1)S(1)} %bitcast.44), dimensions={1,2} | broadcast | bytes 540672 | tf_op jit(solution)/shard_map/broadcast_in_dim | solution.py:39
  30.5 21.7 %all-to-all-start.1 = ((bf16[32,256,32]{1,2,0:T(8,128)(2,1)}), bf16[32,256,32]{1,2,0:T(8,128)(2,1)S(1)}, u32[]{:S(2)}, u32[]{:S(2)}) async-start(bf16[32,256,32]{1,2,0:T(8,128)(2,1)} %broadcast_in_dim.8), calls=%async_computation.1 | async-start | bytes 1048576 | tf_op jit(solution)/shard_map/all_to_all | solution.py:39
  52.2 0.3 collective-permute-start
  52.5 4.9 %collective-permute-done = bf16[4,256,32]{1,2,0:T(8,128)(2,1)S(1)} collective-permute-done((bf16[4,256,32]{1,2,0:T(8,128)(2,1)S(1)}, bf16[4,256,32]{1,2,0:T(8,128)(2,1)S(1)}, u32[]{:S(2)}, u32[]{:S(2)}) %collective-permute-start) | collective-permute-done | bytes 65568 | tf_op jit(solution)/shard_map/ppermute | solution.py:71
  57.5 11.3 %all-to-all-done.1 = bf16[32,256,32]{1,2,0:T(8,128)(2,1)S(1)} async-done(((bf16[32,256,32]{1,2,0:T(8,128)(2,1)}), bf16[32,256,32]{1,2,0:T(8,128)(2,1)S(1)}, u32[]{:S(2)}, u32[]{:S(2)}) %all-to-all-start.1) | async-done | bytes 524320 | tf_op jit(solution)/shard_map/all_to_all | solution.py:39
  68.8 0.1 multiply_reduce_fusion
  69.0 0.4 copy.8
  69.4 0.4 reshape.134
  69.8 3.3 %fusion.14 = (bf16[4,2,256,1024]{3,2,1,0:T(8,128)(2,1)}, f32[4,2,256,1024]{3,2,1,0:T(8,128)S(1)}) fusion(bf16[4,1024,64,1]{1,2,0,3:T(8,128)(2,1)S(1)} %reshape.134, bf16[4,1,256,64]{2,3,1,0:T(8,128)(2,1)S(1)} %maximum_bitcast_fusion, bf16[4,1,256,64]{2,3,1,0:T(8,128)(2,1)S(1)} %bitcast.40), kind=kOutput, calls=%fused_computation.35 | convolution fusion | flops 272760832 | bytes 13369344 | tf_op jit(solution)/shard_map/bpik,bjk->bpij/dot_general | solution.py:27
  73.1 2.5 %fusion.2 = f32[4,256,1024]{2,1,0:T(8,128)} fusion(f32[4,2,256,1024]{3,2,1,0:T(8,128)S(1)} %get-tuple-element.7, f32[4,1024]{1,0:T(4,128)S(1)} %bitcast.43, f32[4,256]{1,0:T(4,128)S(1)} %multiply_add_fusion), kind=kLoop, calls=%fused_computation.3 | loop fusion | flops 5242880 | bytes 12603392 | tf_op jit(solution)/shard_map/div | solution.py:32
  (10 shorter events, 0.1 us)
Async XLA Ops:
  0.6 2.1 %copy-start = (bf16[256,512]{1,0:T(8,128)(2,1)S(1)}, bf16[256,512]{1,0:T(8,128)(2,1)}, u32[]{:S(2)}) copy-start(bf16[256,512]{1,0:T(8,128)(2,1)} %param.2) | copy-start | bytes 786436
  4.1 24.8 %all-to-all-start = ((f32[8,4,256,32]{2,3,1,0:T(8,128)}), f32[8,4,256,32]{2,3,1,0:T(8,128)S(1)}, u32[]{:S(2)}, u32[]{:S(2)}) async-start(f32[8,4,256,32]{2,3,1,0:T(8,128)} %bitcast.4), calls=%async_computation | async-start | bytes 2097152 | tf_op jit(solution)/shard_map/all_to_all | solution.py:59
  29.0 0.7 collective-permute-start.1
  30.5 38.3 %all-to-all-start.1 = ((bf16[32,256,32]{1,2,0:T(8,128)(2,1)}), bf16[32,256,32]{1,2,0:T(8,128)(2,1)S(1)}, u32[]{:S(2)}, u32[]{:S(2)}) async-start(bf16[32,256,32]{1,2,0:T(8,128)(2,1)} %broadcast_in_dim.8), calls=%async_computation.1 | async-start | bytes 1048576 | tf_op jit(solution)/shard_map/all_to_all | solution.py:39
  52.2 5.2 %collective-permute-start = (bf16[4,256,32]{1,2,0:T(8,128)(2,1)S(1)}, bf16[4,256,32]{1,2,0:T(8,128)(2,1)S(1)}, u32[]{:S(2)}, u32[]{:S(2)}) collective-permute-start(bf16[4,256,32]{1,2,0:T(8,128)(2,1)S(1)} %reduce_sum.27), channel_id=1, source_target_pairs={{0,4},{1,5},{2,6},{3,7},{4,0},{5,1},{6,2},{7,3},{8,12},{9,13},{10,... | collective-permute-start | bytes 196616 | tf_op jit(solution)/shard_map/ppermute | solution.py:71

commit v13 on v2

--- a/solution.py
+++ b/solution.py
@@ -42,18 +42,18 @@
 def body(metrics, band_starts):
     row_count = metrics.shape[0]
     local_minutes = metrics.shape[1]
-    n_tm = lax.axis_size("tm")
+    n_tm = lax.axis_size(TM)
     n_svc = lax.axis_size("svc")
     owners = n_svc // n_tm
     width = BANDS * 2 * BINS
     chunk = width // n_tm
-    time_index = lax.axis_index("tm")
+    time_index = lax.axis_index(TM)
     minutes = time_index * local_minutes + jnp.arange(local_minutes, dtype=jnp.int32)
     dft_table = make_table(minutes, band_starts).reshape(local_minutes, n_tm, chunk)
     partial_value = jnp.einsum(
         "nt,tcb->cnb", metrics, dft_table, preferred_element_type=jnp.float32
     )
-    partials = lax.all_to_all(partial_value, "tm", 0, 0, tiled=True)
+    partials = lax.all_to_all(partial_value, TM, 0, 0, tiled=True)
     piece = jnp.sum(partials, axis=0, keepdims=True).astype(jnp.bfloat16)
     perm = []
     for s_src in range(n_svc):
@@ -62,8 +62,17 @@
             s_dst = t_src * owners + r_src
             t_dst = g_src
             perm.append((s_src * n_tm + t_src, s_dst * n_tm + t_dst))
-    moved = lax.ppermute(piece, ("svc", "tm"), perm)
-    row_chunks = gather_by_all_to_all(piece, "tm", n_tm)
+    moved = lax.ppermute(piece, ("svc",) + TM, perm)
+    near = lax.axis_size("x")
+    own_group = gather_by_all_to_all(piece, "x", near)
+    pairs = [(a * n_tm + b, a * n_tm + (b ^ near)) for a in range(n_svc) for b in range(n_tm)]
+    received = lax.ppermute(own_group, ("svc",) + TM, pairs)
+    upper = (time_index & near) != 0
+    row_chunks = jnp.where(
+        upper,
+        jnp.concatenate([received, own_group], axis=0),
+        jnp.concatenate([own_group, received], axis=0),
+    )
     col_chunks = gather_by_all_to_all(moved, "svc", n_svc)
     bands_row = row_chunks.reshape(BANDS, 2, row_count, BINS)
     row_spec = jnp.transpose(bands_row, (0, 2, 1, 3)).reshape(BANDS, row_count, 2 * BINS)
@@ -72,11 +81,17 @@
     return all_bands(row_spec, col_spec)
 
 
+TM = ("far", "x")
+
+
 def solution(mesh):
+    n_svc, n_tm = mesh.shape["svc"], mesh.shape["tm"]
+    n_x = 4 if n_tm % 4 == 0 else n_tm
+    split = jax.sharding.Mesh(mesh.devices.reshape(n_svc, n_tm // n_x, n_x), ("svc",) + TM)
     return jax.shard_map(
         body,
-        mesh=mesh,
-        in_specs=(P("svc", "tm"), P()),
-        out_specs=(P(None, None, "svc", "tm"), P(None, "svc", "tm")),
+        mesh=split,
+        in_specs=(P("svc", TM), P()),
+        out_specs=(P(None, None, "svc", TM), P(None, "svc", TM)),
         check_vma=False,
     )

time: 71 us -> 70.3 us (level)
  waiting for transfers between devices: 22.7 us -> 20 us
  starting transfers between devices: 20.7 us -> 23.3 us
    all_to_all x2, waiting for transfers between devices: 22.7 us -> 15.1 us  [gather_by_all_to_all(): lax.all_to_all(jnp.broadcast_to(x, (size,) + x.shape[1:]), axis, 0, 0, ti...]
    ppermute x1 -> x2, waiting for transfers between devices: 0.01 us -> 4.91 us  [the longest x1 4.91 us: body(): received = lax.ppermute(own_group, ('svc',) + TM, pairs)]
    all_to_all x2, starting transfers between devices: 20 us -> 22.4 us  [gather_by_all_to_all(): lax.all_to_all(jnp.broadcast_to(x, (size,) + x.shape[1:]), axis, 0, 0, ti...]
  transfers between devices with their start and end apart: 3 -> 4, of which waited for: 2 -> 3; matrix products, arithmetic and copies ran while one was open for 0% -> 0% of each run, Pallas kernels for 0% -> 0%
where the time goes in v13:
time: 70.3 us; the launch traced here: 69.7 us
  starting transfers between devices  23.3 us (33%)
  waiting for transfers between devices  20 us (28%)
  blocking collectives  15.1 us (21%)
  other arithmetic  4.78 us (7%)
  matrix products  3.56 us (5%)
  local copies, waits for them, and re-layouts  2.28 us (3%)
  between operations  0.77 us (1%)
    all_to_all x2, starting transfers between devices, gather_by_all_to_all(): lax.all_to_all(jnp.broadcast_to(x, (size,) + x.shape[1:]), axis, 0, 0, ti...  22.4 us
    all_to_all x1, blocking collectives, body(): partials = lax.all_to_all(partial_value, TM, 0, 0, tiled=True)  15.1 us
    all_to_all x2, waiting for transfers between devices, gather_by_all_to_all(): lax.all_to_all(jnp.broadcast_to(x, (size,) + x.shape[1:]), axis, 0, 0, ti...  15.1 us
    ppermute x1, waiting for transfers between devices, body(): received = lax.ppermute(own_group, ('svc',) + TM, pairs)  4.91 us
    dot_general x1, matrix products, all_bands(): jnp.einsum('bpik,bjk->bpij', lhs, col_spec, preferred_element_type=jnp.fl...  3.31 us
    div x1, other arithmetic, all_bands(): (real_part * real_part + imag_part * imag_part) / ((row_power[:, :, None]...  2.5 us
    broadcast_in_dim x2, local copies, waits for them, and re-layouts, gather_by_all_to_all(): jnp.broadcast_to(x, (size,) + x.shape[1:])  1.49 us
  transfers between devices with their start and end apart: 4, of which 3 were waited for; matrix products, arithmetic and copies ran while one was open for 0% of the time, Pallas kernels for 0%

profile of v13, /device:TPU:1, one launch (start us, length us, event | category | flops | bytes accessed | tf_op | source)
XLA Modules:
  0.0 69.7 jit_solution(9073122868022818400)
XLA Ops:
  0.6 0.0 copy-start
  0.7 0.8 %iota_add_fusion = s32[4,32]{1,0:T(4,128)S(1)} fusion(s32[4]{0:T(128)} %param.3), kind=kLoop, calls=%fused_computation.30 | loop fusion | flops 128 | bytes 528 | tf_op jit(solution)/shard_map/add | solution.py:16
  1.4 1.2 %multiply_convert_fusion.1 = (bf16[512,4,1,32]{0,3,2,1:T(8,128)(2,1)S(1)}, bf16[512,4,1,32]{0,3,2,1:T(8,128)(2,1)S(1)}) fusion(s32[4,32]{1,0:T(4,128)S(1)} %iota_add_fusion, s32[512]{0:T(512)S(1)} %iota_add_fusion.1), kind=kLoop, calls=%fused_computation.24 | loop fusion | flops 1245184 | bytes 264704 | tf_op jit(solution)/shard_map/convert
  2.7 0.0 copy-done
  2.7 0.3 convolution_bitcast_fusion
  3.0 15.1 %all_to_all.15 = f32[8,256,32]{1,2,0:T(8,128)S(1)} all-to-all(f32[8,256,32]{1,2,0:T(8,128)S(1)} %convolution_bitcast_fusion), channel_id=1, replica_groups=mesh['svc'=32,'far'=2,'x'=4] {'far','x'}, dimensions={0} | all-to-all | bytes 524288 | tf_op jit(solution)/shard_map/all_to_all | solution.py:56
  18.1 0.6 broadcast_in_dim.6
  18.7 3.3 %all-to-all-start.1 = ((bf16[4,256,32]{1,2,0:T(8,128)(2,1)}), bf16[4,256,32]{1,2,0:T(8,128)(2,1)S(1)}, u32[]{:S(2)}, u32[]{:S(2)}) async-start(bf16[4,256,32]{1,2,0:T(8,128)(2,1)} %broadcast_in_dim.6), calls=%async_computation.1 | async-start | bytes 131072 | tf_op jit(solution)/shard_map/all_to_all | solution.py:39
  22.0 0.7 collective-permute-start.1
  22.7 0.0 collective-permute-done.1
  22.7 3.8 %all-to-all-done.1 = bf16[4,256,32]{1,2,0:T(8,128)(2,1)S(1)} async-done(((bf16[4,256,32]{1,2,0:T(8,128)(2,1)}), bf16[4,256,32]{1,2,0:T(8,128)(2,1)S(1)}, u32[]{:S(2)}, u32[]{:S(2)}) %all-to-all-start.1) | async-done | bytes 65568 | tf_op jit(solution)/shard_map/all_to_all | solution.py:39
  26.4 0.9 %broadcast_in_dim.8 = bf16[32,256,32]{1,2,0:T(8,128)(2,1)} broadcast(bf16[256,32]{0,1:T(8,128)(2,1)S(1)} %bitcast.43), dimensions={1,2} | broadcast | bytes 540672 | tf_op jit(solution)/shard_map/broadcast_in_dim | solution.py:39
  27.3 19.1 %all-to-all-start.2 = ((bf16[32,256,32]{1,2,0:T(8,128)(2,1)}), bf16[32,256,32]{1,2,0:T(8,128)(2,1)S(1)}, u32[]{:S(2)}, u32[]{:S(2)}) async-start(bf16[32,256,32]{1,2,0:T(8,128)(2,1)} %broadcast_in_dim.8), calls=%async_computation.2 | async-start | bytes 1048576 | tf_op jit(solution)/shard_map/all_to_all | solution.py:39
  46.4 0.3 collective-permute-start
  46.6 4.9 %collective-permute-done = bf16[4,256,32]{1,2,0:T(8,128)(2,1)S(1)} collective-permute-done((bf16[4,256,32]{1,2,0:T(8,128)(2,1)S(1)}, bf16[4,256,32]{1,2,0:T(8,128)(2,1)S(1)}, u32[]{:S(2)}, u32[]{:S(2)}) %collective-permute-start) | collective-permute-done | bytes 65568 | tf_op jit(solution)/shard_map/ppermute | solution.py:69
  51.7 11.3 %all-to-all-done.2 = bf16[32,256,32]{1,2,0:T(8,128)(2,1)S(1)} async-done(((bf16[32,256,32]{1,2,0:T(8,128)(2,1)}), bf16[32,256,32]{1,2,0:T(8,128)(2,1)S(1)}, u32[]{:S(2)}, u32[]{:S(2)}) %all-to-all-start.2) | async-done | bytes 524320 | tf_op jit(solution)/shard_map/all_to_all | solution.py:39
  62.9 0.1 multiply_reduce_fusion
  63.1 0.4 copy.5
  63.5 0.4 reshape.135
  63.9 3.3 %fusion.13 = (bf16[4,2,256,1024]{3,2,1,0:T(8,128)(2,1)}, f32[4,2,256,1024]{3,2,1,0:T(8,128)S(1)}) fusion(bf16[4,1024,64,1]{1,2,0,3:T(8,128)(2,1)S(1)} %reshape.135, bf16[4,1,256,64]{2,3,1,0:T(8,128)(2,1)S(1)} %maximum_bitcast_fusion, bf16[4,1,256,64]{2,3,1,0:T(8,128)(2,1)S(1)} %bitcast.39), kind=kOutput, calls=%fused_computation.34 | convolution fusion | flops 272760832 | bytes 13369344 | tf_op jit(solution)/shard_map/bpik,bjk->bpij/dot_general | solution.py:27
  67.2 2.5 %fusion.2 = f32[4,256,1024]{2,1,0:T(8,128)} fusion(f32[4,2,256,1024]{3,2,1,0:T(8,128)S(1)} %get-tuple-element.7, f32[4,1024]{1,0:T(4,128)S(1)} %bitcast.41, f32[4,256]{1,0:T(4,128)S(1)} %multiply_add_fusion), kind=kLoop, calls=%fused_computation.3 | loop fusion | flops 5242880 | bytes 12603392 | tf_op jit(solution)/shard_map/div | solution.py:32
  (10 shorter events, 0.1 us)
Async XLA Ops:
  0.6 2.1 %copy-start = (bf16[256,512]{1,0:T(8,128)(2,1)S(1)}, bf16[256,512]{1,0:T(8,128)(2,1)}, u32[]{:S(2)}) copy-start(bf16[256,512]{1,0:T(8,128)(2,1)} %param.2) | copy-start | bytes 786436
  18.7 7.7 %all-to-all-start.1 = ((bf16[4,256,32]{1,2,0:T(8,128)(2,1)}), bf16[4,256,32]{1,2,0:T(8,128)(2,1)S(1)}, u32[]{:S(2)}, u32[]{:S(2)}) async-start(bf16[4,256,32]{1,2,0:T(8,128)(2,1)} %broadcast_in_dim.6), calls=%async_computation.1 | async-start | bytes 131072 | tf_op jit(solution)/shard_map/all_to_all | solution.py:39
  22.0 0.7 collective-permute-start.1
  27.3 35.7 %all-to-all-start.2 = ((bf16[32,256,32]{1,2,0:T(8,128)(2,1)}), bf16[32,256,32]{1,2,0:T(8,128)(2,1)S(1)}, u32[]{:S(2)}, u32[]{:S(2)}) async-start(bf16[32,256,32]{1,2,0:T(8,128)(2,1)} %broadcast_in_dim.8), calls=%async_computation.2 | async-start | bytes 1048576 | tf_op jit(solution)/shard_map/all_to_all | solution.py:39
  46.4 5.2 %collective-permute-start = (bf16[4,256,32]{1,2,0:T(8,128)(2,1)S(1)}, bf16[4,256,32]{1,2,0:T(8,128)(2,1)S(1)}, u32[]{:S(2)}, u32[]{:S(2)}) collective-permute-start(bf16[4,256,32]{1,2,0:T(8,128)(2,1)S(1)} %all-to-all-done.1), channel_id=1, source_target_pairs={{0,4},{1,5},{2,6},{3,7},{4,0},{5,1},{6,2},{7,3},{8,12},{9,13},{10,... | collective-permute-start | bytes 196616 | tf_op jit(solution)/shard_map/ppermute | solution.py:69

commit v14 on v2

--- a/solution.py
+++ b/solution.py
@@ -55,16 +55,12 @@
     )
     partials = lax.all_to_all(partial_value, "tm", 0, 0, tiled=True)
     piece = jnp.sum(partials, axis=0, keepdims=True).astype(jnp.bfloat16)
-    perm = []
-    for s_src in range(n_svc):
-        g_src, r_src = divmod(s_src, owners)
-        for t_src in range(n_tm):
-            s_dst = t_src * owners + r_src
-            t_dst = g_src
-            perm.append((s_src * n_tm + t_src, s_dst * n_tm + t_dst))
-    moved = lax.ppermute(piece, ("svc", "tm"), perm)
-    row_chunks = gather_by_all_to_all(piece, "tm", n_tm)
-    col_chunks = gather_by_all_to_all(moved, "svc", n_svc)
+    every_block = gather_by_all_to_all(piece, "svc", n_svc)
+    panel = every_block.reshape(n_tm, owners, row_count, chunk)
+    own = jnp.broadcast_to(piece[None], (n_tm, 1, row_count, chunk))
+    received = lax.all_to_all(jnp.concatenate([panel, own], axis=1), "tm", 0, 0, tiled=True)
+    row_chunks = received[:, owners]
+    col_chunks = received[:, :owners].reshape(n_svc, row_count, chunk)
     bands_row = row_chunks.reshape(BANDS, 2, row_count, BINS)
     row_spec = jnp.transpose(bands_row, (0, 2, 1, 3)).reshape(BANDS, row_count, 2 * BINS)
     bands_col = col_chunks.reshape(BANDS, 2, owners, row_count, BINS)

time: 71 us -> 68 us (0.958)
  the two profiles are of different devices: /device:TPU:1 before, /device:TPU:32 now
where the time goes in v14:
time: 68 us; the launch traced here: 67.8 us
  blocking collectives  57.4 us (84%)
  other arithmetic  5.1 us (7%)
  matrix products  3.58 us (5%)
  local copies, waits for them, and re-layouts  0.9 us (1%)
  between operations  0.77 us (1%)
    all_to_all x1, blocking collectives, gather_by_all_to_all(): lax.all_to_all(jnp.broadcast_to(x, (size,) + x.shape[1:]), axis, 0, 0, ti...  26.4 us
    all_to_all x1, blocking collectives, body(): lax.all_to_all(jnp.concatenate([panel, own], axis=1), 'tm', 0, 0, tiled=T...  15.5 us
    all_to_all x1, blocking collectives, body(): partials = lax.all_to_all(partial_value, 'tm', 0, 0, tiled=True)  15.5 us
    dot_general x1, matrix products, all_bands(): jnp.einsum('bpik,bjk->bpij', lhs, col_spec, preferred_element_type=jnp.fl...  3.31 us
    div x1, other arithmetic, all_bands(): (real_part * real_part + imag_part * imag_part) / ((row_power[:, :, None]...  2.49 us

profile of v14, /device:TPU:32, one launch (start us, length us, event | category | flops | bytes accessed | tf_op | source)
XLA Modules:
  0.0 67.8 jit_solution(4884840629865783296)
XLA Ops:
  0.6 0.0 copy-start
  0.7 0.8 %iota_add_fusion = s32[4,32]{1,0:T(4,128)S(1)} fusion(s32[4]{0:T(128)} %param.3), kind=kLoop, calls=%fused_computation.31 | loop fusion | flops 128 | bytes 528 | tf_op jit(solution)/shard_map/add | solution.py:16
  1.4 1.2 %multiply_convert_fusion.1 = (bf16[512,4,1,32]{0,3,2,1:T(8,128)(2,1)S(1)}, bf16[512,4,1,32]{0,3,2,1:T(8,128)(2,1)S(1)}) fusion(s32[4,32]{1,0:T(4,128)S(1)} %iota_add_fusion, s32[512]{0:T(512)S(1)} %iota_add_fusion.1), kind=kLoop, calls=%fused_computation.26 | loop fusion | flops 1245184 | bytes 264704 | tf_op jit(solution)/shard_map/convert
  2.7 0.0 copy-done
  2.7 0.3 convolution_bitcast_fusion
  3.0 15.5 %all_to_all.15 = f32[8,256,32]{1,2,0:T(8,128)S(1)} all-to-all(f32[8,256,32]{1,2,0:T(8,128)S(1)} %convolution_bitcast_fusion), channel_id=1, replica_groups=mesh['svc'=32,'tm'=8] {'tm'}, dimensions={0} | all-to-all | bytes 524288 | tf_op jit(solution)/shard_map/all_to_all | solution.py:56
  18.5 0.1 broadcast_in_dim.4
  18.6 26.4 %all_to_all.16 = bf16[32,256,32]{1,2,0:T(8,128)(2,1)S(1)} all-to-all(bf16[32,256,32]{1,2,0:T(8,128)(2,1)S(1)} %broadcast_in_dim.4), channel_id=1, replica_groups=mesh['svc'=32,'tm'=8] {'svc'}, dimensions={0} | all-to-all | bytes 1048576 | tf_op jit(solution)/shard_map/all_to_all | solution.py:39
  45.0 0.1 pad_maximum_fusion
  45.0 15.5 %all_to_all.17 = bf16[8,5,256,32]{2,3,1,0:T(8,128)(2,1)S(1)} all-to-all(bf16[8,5,256,32]{2,3,1,0:T(8,128)(2,1)S(1)} %pad_maximum_fusion), channel_id=1, replica_groups=mesh['svc'=32,'tm'=8] {'tm'}, dimensions={0} | all-to-all | bytes 1310720 | tf_op jit(solution)/shard_map/all_to_all | solution.py:61
  60.6 0.4 multiply_reduce_fusion
  61.0 0.4 copy.11
  61.5 0.4 reshape.130
  62.0 3.3 %fusion.13 = (bf16[4,2,256,1024]{3,2,1,0:T(8,128)(2,1)}, f32[4,2,256,1024]{3,2,1,0:T(8,128)S(1)}) fusion(bf16[4,1024,64,1]{1,2,0,3:T(8,128)(2,1)S(1)} %reshape.130, bf16[4,1,256,64]{2,3,1,0:T(8,128)(2,1)S(1)} %maximum_bitcast_fusion, bf16[4,1,256,64]{2,3,1,0:T(8,128)(2,1)S(1)} %bitcast.41), kind=kOutput, calls=%fused_computation.35 | convolution fusion | flops 272760832 | bytes 13369344 | tf_op jit(solution)/shard_map/bpik,bjk->bpij/dot_general | solution.py:27
  65.3 2.5 %fusion.2 = f32[4,256,1024]{2,1,0:T(8,128)} fusion(f32[4,2,256,1024]{3,2,1,0:T(8,128)S(1)} %get-tuple-element.7, f32[4,1024]{1,0:T(4,128)S(1)} %bitcast.45, f32[4,256]{1,0:T(4,128)S(1)} %multiply_add_fusion), kind=kLoop, calls=%fused_computation.3 | loop fusion | flops 5242880 | bytes 12603392 | tf_op jit(solution)/shard_map/div | solution.py:32
  (12 shorter events, 0.2 us)
Async XLA Ops:
  0.6 2.1 %copy-start = (bf16[256,512]{1,0:T(8,128)(2,1)S(1)}, bf16[256,512]{1,0:T(8,128)(2,1)}, u32[]{:S(2)}) copy-start(bf16[256,512]{1,0:T(8,128)(2,1)} %param.2) | copy-start | bytes 786436

commit v15 on v10

--- a/solution.py
+++ b/solution.py
@@ -64,17 +64,17 @@
             perm.append((s_src * n_tm + t_src, s_dst * n_tm + t_dst))
     moved = lax.ppermute(piece, ("svc", "tm"), perm)
     row_chunks = piece
-    distance = 1
-    while distance < n_tm:
+    distance = n_tm // 2
+    while distance >= 1:
         pairs = [(a * n_tm + b, a * n_tm + (b ^ distance)) for a in range(n_svc) for b in range(n_tm)]
         received = lax.ppermute(row_chunks, ("svc", "tm"), pairs)
         upper = (time_index & distance) != 0
         row_chunks = jnp.where(
             upper,
-            jnp.concatenate([received, row_chunks], axis=0),
-            jnp.concatenate([row_chunks, received], axis=0),
-        )
-        distance *= 2
+            jnp.stack([received, row_chunks], axis=1),
+            jnp.stack([row_chunks, received], axis=1),
+        ).reshape((2 * row_chunks.shape[0],) + piece.shape[1:])
+        distance //= 2
     col_chunks = gather_by_all_to_all(moved, "svc", n_svc)
     bands_row = row_chunks.reshape(BANDS, 2, row_count, BINS)
     row_spec = jnp.transpose(bands_row, (0, 2, 1, 3)).reshape(BANDS, row_count, 2 * BINS)

time: 67 us -> 66.1 us (0.987)
  waiting for transfers between devices: 17.6 us -> 16.2 us
    all_to_all x1, starting transfers between devices: 12.3 us -> 19.3 us  [gather_by_all_to_all(): lax.all_to_all(jnp.broadcast_to(x, (size,) + x.shape[1:]), axis, 0, 0, ti...]
    ppermute x3, starting transfers between devices: 10.3 us -> 3.7 us  [body(): received = lax.ppermute(row_chunks, ('svc', 'tm'), pairs)]
    all_to_all x1, waiting for transfers between devices: 11.3 us -> 8.56 us  [gather_by_all_to_all(): lax.all_to_all(jnp.broadcast_to(x, (size,) + x.shape[1:]), axis, 0, 0, ti...]
    ppermute x3, waiting for transfers between devices: 6.29 us -> 7.64 us  [body(): received = lax.ppermute(row_chunks, ('svc', 'tm'), pairs)]
where the time goes in v15:
time: 66.1 us; the launch traced here: 65.8 us
  starting transfers between devices  23.7 us (36%)
  waiting for transfers between devices  16.2 us (25%)
  blocking collectives  15.1 us (23%)
  other arithmetic  4.81 us (7%)
  matrix products  3.57 us (5%)
  local copies, waits for them, and re-layouts  1.65 us (2%)
  between operations  0.8 us (1%)
    all_to_all x1, starting transfers between devices, gather_by_all_to_all(): lax.all_to_all(jnp.broadcast_to(x, (size,) + x.shape[1:]), axis, 0, 0, ti...  19.3 us
    all_to_all x1, blocking collectives, body(): partials = lax.all_to_all(partial_value, 'tm', 0, 0, tiled=True)  15.1 us
    all_to_all x1, waiting for transfers between devices, gather_by_all_to_all(): lax.all_to_all(jnp.broadcast_to(x, (size,) + x.shape[1:]), axis, 0, 0, ti...  8.56 us
    ppermute x3, waiting for transfers between devices, body(): received = lax.ppermute(row_chunks, ('svc', 'tm'), pairs)  7.64 us
    ppermute x3, starting transfers between devices, body(): received = lax.ppermute(row_chunks, ('svc', 'tm'), pairs)  3.7 us
    dot_general x1, matrix products, all_bands(): jnp.einsum('bpik,bjk->bpij', lhs, col_spec, preferred_element_type=jnp.fl...  3.31 us
    div x1, other arithmetic, all_bands(): (real_part * real_part + imag_part * imag_part) / ((row_power[:, :, None]...  2.5 us
  transfers between devices with their start and end apart: 5, of which 3 were waited for; matrix products, arithmetic and copies ran while one was open for 1% of the time, Pallas kernels for 0%

profile of v15, /device:TPU:1, one launch (start us, length us, event | category | flops | bytes accessed | tf_op | source)
XLA Modules:
  0.0 65.8 jit_solution(14710396119510545971)
XLA Ops:
  0.6 0.0 copy-start
  0.7 0.8 %iota_add_fusion = s32[4,32]{1,0:T(4,128)S(1)} fusion(s32[4]{0:T(128)} %param.3), kind=kLoop, calls=%fused_computation.35 | loop fusion | flops 128 | bytes 528 | tf_op jit(solution)/shard_map/add | solution.py:16
  1.4 1.2 %multiply_convert_fusion.1 = (bf16[512,4,1,32]{0,3,2,1:T(8,128)(2,1)S(1)}, bf16[512,4,1,32]{0,3,2,1:T(8,128)(2,1)S(1)}) fusion(s32[4,32]{1,0:T(4,128)S(1)} %iota_add_fusion, s32[512]{0:T(512)S(1)} %iota_add_fusion.1), kind=kLoop, calls=%fused_computation.24 | loop fusion | flops 1245184 | bytes 264704 | tf_op jit(solution)/shard_map/convert
  2.7 0.0 copy-done
  2.7 0.3 convolution_bitcast_fusion
  3.0 15.1 %all_to_all.10 = f32[8,256,32]{1,2,0:T(8,128)S(1)} all-to-all(f32[8,256,32]{1,2,0:T(8,128)S(1)} %convolution_bitcast_fusion), channel_id=1, replica_groups=mesh['svc'=32,'tm'=8] {'tm'}, dimensions={0} | all-to-all | bytes 524288 | tf_op jit(solution)/shard_map/all_to_all | solution.py:56
  18.1 0.7 %collective-permute-start.3 = (bf16[1,256,32]{1,2,0:T(8,128)(2,1)S(1)}, bf16[1,256,32]{1,2,0:T(8,128)(2,1)S(1)}, u32[]{:S(2)}, u32[]{:S(2)}) collective-permute-start(bf16[1,256,32]{1,2,0:T(8,128)(2,1)S(1)} %bitcast.51), channel_id=1, source_target_pairs={{0,0},{1,32},{2,64},{3,96},{4,128},{5,160},{6,192},{7,224},{8,8},{... | collective-permute-start | bytes 49160 | tf_op jit(solution)/shard_map/ppermute | solution.py:65
  18.7 3.5 %collective-permute-start = (bf16[1,256,32]{1,2,0:T(8,128)(2,1)S(1)}, bf16[1,256,32]{1,2,0:T(8,128)(2,1)S(1)}, u32[]{:S(2)}, u32[]{:S(2)}) collective-permute-start(bf16[1,256,32]{1,2,0:T(8,128)(2,1)S(1)} %bitcast.52), channel_id=1, source_target_pairs={{0,4},{1,5},{2,6},{3,7},{4,0},{5,1},{6,2},{7,3},{8,12},{9,13},{10,... | collective-permute-start | bytes 49160 | tf_op jit(solution)/shard_map/ppermute | solution.py:70
  22.3 0.0 collective-permute-done.3
  22.3 0.9 %broadcast_in_dim.5 = bf16[32,256,32]{1,2,0:T(8,128)(2,1)} broadcast(bf16[256,32]{0,1:T(8,128)(2,1)S(1)} %bitcast.59), dimensions={1,2} | broadcast | bytes 540672 | tf_op jit(solution)/shard_map/broadcast_in_dim | solution.py:39
  23.1 19.3 %all-to-all-start.1 = ((bf16[32,256,32]{1,2,0:T(8,128)(2,1)}), bf16[32,256,32]{1,2,0:T(8,128)(2,1)S(1)}, u32[]{:S(2)}, u32[]{:S(2)}) async-start(bf16[32,256,32]{1,2,0:T(8,128)(2,1)} %broadcast_in_dim.5), calls=%async_computation.1 | async-start | bytes 1048576 | tf_op jit(solution)/shard_map/all_to_all | solution.py:39
  42.4 0.0 collective-permute-done
  42.5 0.1 collective-permute-start.1
  42.6 4.2 %collective-permute-done.1 = bf16[2,256,32]{1,2,0:T(8,128)(2,1)S(1)} collective-permute-done((bf16[2,256,32]{1,2,0:T(8,128)(2,1)S(1)}, bf16[2,256,32]{1,2,0:T(8,128)(2,1)S(1)}, u32[]{:S(2)}, u32[]{:S(2)}) %collective-permute-start.1) | collective-permute-done | bytes 32800 | tf_op jit(solution)/shard_map/ppermute | solution.py:70
  46.9 0.1 collective-permute-start.2
  47.0 3.4 %collective-permute-done.2 = bf16[4,256,32]{1,2,0:T(8,128)(2,1)S(1)} collective-permute-done((bf16[4,256,32]{1,2,0:T(8,128)(2,1)S(1)}, bf16[4,256,32]{1,2,0:T(8,128)(2,1)S(1)}, u32[]{:S(2)}, u32[]{:S(2)}) %collective-permute-start.2) | collective-permute-done | bytes 65568 | tf_op jit(solution)/shard_map/ppermute | solution.py:70
  50.4 0.1 multiply_reduce_fusion.1
  50.5 8.6 %all-to-all-done.1 = bf16[32,256,32]{1,2,0:T(8,128)(2,1)S(1)} async-done(((bf16[32,256,32]{1,2,0:T(8,128)(2,1)}), bf16[32,256,32]{1,2,0:T(8,128)(2,1)S(1)}, u32[]{:S(2)}, u32[]{:S(2)}) %all-to-all-start.1) | async-done | bytes 524320 | tf_op jit(solution)/shard_map/all_to_all | solution.py:39
  59.0 0.1 multiply_reduce_fusion
  59.2 0.4 copy.7
  59.6 0.4 reshape.232
  60.0 3.3 %fusion.13 = (bf16[4,2,256,1024]{3,2,1,0:T(8,128)(2,1)}, f32[4,2,256,1024]{3,2,1,0:T(8,128)S(1)}) fusion(bf16[4,1024,64,1]{1,2,0,3:T(8,128)(2,1)S(1)} %reshape.232, bf16[4,1,256,64]{2,3,1,0:T(8,128)(2,1)S(1)} %maximum_bitcast_fusion, bf16[4,1,256,64]{2,3,1,0:T(8,128)(2,1)S(1)} %bitcast.47), kind=kOutput, calls=%fused_computation.39 | convolution fusion | flops 272760832 | bytes 13369344 | tf_op jit(solution)/shard_map/bpik,bjk->bpij/dot_general | solution.py:27
  63.3 2.5 %fusion.2 = f32[4,256,1024]{2,1,0:T(8,128)} fusion(f32[4,2,256,1024]{3,2,1,0:T(8,128)S(1)} %get-tuple-element.9, f32[4,1024]{1,0:T(4,128)S(1)} %bitcast.55, f32[4,256]{1,0:T(4,128)S(1)} %multiply_add_fusion), kind=kLoop, calls=%fused_computation.3 | loop fusion | flops 5242880 | bytes 12603392 | tf_op jit(solution)/shard_map/div | solution.py:32
  (12 shorter events, 0.1 us)
Async XLA Ops:
  0.6 2.1 %copy-start = (bf16[256,512]{1,0:T(8,128)(2,1)S(1)}, bf16[256,512]{1,0:T(8,128)(2,1)}, u32[]{:S(2)}) copy-start(bf16[256,512]{1,0:T(8,128)(2,1)} %param.2) | copy-start | bytes 786436
  18.1 4.2 %collective-permute-start.3 = (bf16[1,256,32]{1,2,0:T(8,128)(2,1)S(1)}, bf16[1,256,32]{1,2,0:T(8,128)(2,1)S(1)}, u32[]{:S(2)}, u32[]{:S(2)}) collective-permute-start(bf16[1,256,32]{1,2,0:T(8,128)(2,1)S(1)} %bitcast.51), channel_id=1, source_target_pairs={{0,0},{1,32},{2,64},{3,96},{4,128},{5,160},{6,192},{7,224},{8,8},{... | collective-permute-start | bytes 49160 | tf_op jit(solution)/shard_map/ppermute | solution.py:65
  18.7 23.7 %collective-permute-start = (bf16[1,256,32]{1,2,0:T(8,128)(2,1)S(1)}, bf16[1,256,32]{1,2,0:T(8,128)(2,1)S(1)}, u32[]{:S(2)}, u32[]{:S(2)}) collective-permute-start(bf16[1,256,32]{1,2,0:T(8,128)(2,1)S(1)} %bitcast.52), channel_id=1, source_target_pairs={{0,4},{1,5},{2,6},{3,7},{4,0},{5,1},{6,2},{7,3},{8,12},{9,13},{10,... | collective-permute-start | bytes 49160 | tf_op jit(solution)/shard_map/ppermute | solution.py:70
  23.1 35.9 %all-to-all-start.1 = ((bf16[32,256,32]{1,2,0:T(8,128)(2,1)}), bf16[32,256,32]{1,2,0:T(8,128)(2,1)S(1)}, u32[]{:S(2)}, u32[]{:S(2)}) async-start(bf16[32,256,32]{1,2,0:T(8,128)(2,1)} %broadcast_in_dim.5), calls=%async_computation.1 | async-start | bytes 1048576 | tf_op jit(solution)/shard_map/all_to_all | solution.py:39
  42.5 4.4 %collective-permute-start.1 = (bf16[2,256,32]{1,2,0:T(8,128)(2,1)S(1)}, bf16[2,256,32]{1,2,0:T(8,128)(2,1)S(1)}, u32[]{:S(2)}, u32[]{:S(2)}) collective-permute-start(bf16[2,256,32]{1,2,0:T(8,128)(2,1)S(1)} %maximum_select_fusion.2), channel_id=1, source_target_pairs={{0,2},{1,3},{2,0},{3,1},{4,6},{5,7},{6,4},{7,5},{8,10},{9,11},{10,... | collective-permute-start | bytes 98312 | tf_op jit(solution)/shard_map/ppermute | solution.py:70
  46.9 3.5 %collective-permute-start.2 = (bf16[4,256,32]{1,2,0:T(8,128)(2,1)S(1)}, bf16[4,256,32]{1,2,0:T(8,128)(2,1)S(1)}, u32[]{:S(2)}, u32[]{:S(2)}) collective-permute-start(bf16[4,256,32]{1,2,0:T(8,128)(2,1)S(1)} %bitcast.49), channel_id=1, source_target_pairs={{0,1},{1,0},{2,3},{3,2},{4,5},{5,4},{6,7},{7,6},{8,9},{9,8},{10,11... | collective-permute-start | bytes 196616 | tf_op jit(solution)/shard_map/ppermute | solution.py:70

commit v16 on v15

--- a/solution.py
+++ b/solution.py
@@ -53,8 +53,11 @@
     partial_value = jnp.einsum(
         "nt,tcb->cnb", metrics, dft_table, preferred_element_type=jnp.float32
     )
-    partials = lax.all_to_all(partial_value, "tm", 0, 0, tiled=True)
-    piece = jnp.sum(partials, axis=0, keepdims=True).astype(jnp.bfloat16)
+    far = n_tm // 2
+    pairs_of = jnp.swapaxes(partial_value.reshape(2, far, row_count, chunk), 0, 1)
+    partials = lax.all_to_all(jnp.concatenate([pairs_of, pairs_of], axis=0), "tm", 0, 0, tiled=True)
+    own_pair = jnp.sum(partials, axis=0).astype(jnp.bfloat16)
+    piece = lax.dynamic_slice_in_dim(own_pair, time_index // far, 1, 0)
     perm = []
     for s_src in range(n_svc):
         g_src, r_src = divmod(s_src, owners)
@@ -63,8 +66,8 @@
             t_dst = g_src
             perm.append((s_src * n_tm + t_src, s_dst * n_tm + t_dst))
     moved = lax.ppermute(piece, ("svc", "tm"), perm)
-    row_chunks = piece
-    distance = n_tm // 2
+    row_chunks = own_pair
+    distance = far // 2
     while distance >= 1:
         pairs = [(a * n_tm + b, a * n_tm + (b ^ distance)) for a in range(n_svc) for b in range(n_tm)]
         received = lax.ppermute(row_chunks, ("svc", "tm"), pairs)

time: 66.1 us -> 70 us (1.059)
  blocking collectives: 15.1 us -> 0 us
  waiting for transfers between devices: 16.2 us -> 27.9 us
  starting transfers between devices: 23.7 us -> 30.1 us
  other arithmetic: 4.81 us -> 5.65 us
    all_to_all x1 -> x0, blocking collectives: 15.1 us -> none  [body(): partials = lax.all_to_all(partial_value, 'tm', 0, 0, tiled=True)]
    all_to_all x0 -> x1, waiting for transfers between devices: none -> 11.7 us  [body(): lax.all_to_all(jnp.concatenate([pairs_of, pairs_of], axis=0), 'tm', 0, 0,...]
    all_to_all x0 -> x1, starting transfers between devices: none -> 7.48 us  [body(): lax.all_to_all(jnp.concatenate([pairs_of, pairs_of], axis=0), 'tm', 0, 0,...]
    ppermute x3 -> x2, starting transfers between devices: 3.7 us -> 0.19 us  [body(): received = lax.ppermute(row_chunks, ('svc', 'tm'), pairs)]
    all_to_all x1, starting transfers between devices: 19.3 us -> 21.7 us  [gather_by_all_to_all(): lax.all_to_all(jnp.broadcast_to(x, (size,) + x.shape[1:]), axis, 0, 0, ti...]
    concatenate x0 -> x1, other arithmetic: none -> 0.85 us  [body(): jnp.concatenate([pairs_of, pairs_of], axis=0)]
    ppermute x3 -> x2, waiting for transfers between devices: 7.64 us -> 7.64 us  [body(): received = lax.ppermute(row_chunks, ('svc', 'tm'), pairs)]
  transfers between devices with their start and end apart: 5 -> 5, of which waited for: 3 -> 4; matrix products, arithmetic and copies ran while one was open for 1% -> 0% of each run, Pallas kernels for 0% -> 0%
where the time goes in v16:
time: 70 us; the launch traced here: 69.7 us
  starting transfers between devices  30.1 us (43%)
  waiting for transfers between devices  27.9 us (40%)
  other arithmetic  5.65 us (8%)
  matrix products  3.57 us (5%)
  local copies, waits for them, and re-layouts  1.68 us (2%)
  between operations  0.8 us (1%)
    all_to_all x1, starting transfers between devices, gather_by_all_to_all(): lax.all_to_all(jnp.broadcast_to(x, (size,) + x.shape[1:]), axis, 0, 0, ti...  21.7 us
    all_to_all x1, waiting for transfers between devices, body(): lax.all_to_all(jnp.concatenate([pairs_of, pairs_of], axis=0), 'tm', 0, 0,...  11.7 us
    all_to_all x1, waiting for transfers between devices, gather_by_all_to_all(): lax.all_to_all(jnp.broadcast_to(x, (size,) + x.shape[1:]), axis, 0, 0, ti...  8.58 us
    ppermute x2, waiting for transfers between devices, body(): received = lax.ppermute(row_chunks, ('svc', 'tm'), pairs)  7.64 us
    all_to_all x1, starting transfers between devices, body(): lax.all_to_all(jnp.concatenate([pairs_of, pairs_of], axis=0), 'tm', 0, 0,...  7.48 us
    dot_general x1, matrix products, all_bands(): jnp.einsum('bpik,bjk->bpij', lhs, col_spec, preferred_element_type=jnp.fl...  3.3 us
    div x1, other arithmetic, all_bands(): (real_part * real_part + imag_part * imag_part) / ((row_power[:, :, None]...  2.5 us
  transfers between devices with their start and end apart: 5, of which 4 were waited for; matrix products, arithmetic and copies ran while one was open for 0% of the time, Pallas kernels for 0%

profile of v16, /device:TPU:1, one launch (start us, length us, event | category | flops | bytes accessed | tf_op | source)
XLA Modules:
  0.0 69.7 jit_solution(13309087812078002707)
XLA Ops:
  0.6 0.0 copy-start
  0.7 0.8 %iota_add_fusion = s32[4,32]{1,0:T(4,128)S(1)} fusion(s32[4]{0:T(128)} %param.3), kind=kLoop, calls=%fused_computation.33 | loop fusion | flops 128 | bytes 528 | tf_op jit(solution)/shard_map/add | solution.py:16
  1.4 1.2 %multiply_convert_fusion.1 = (bf16[512,4,1,32]{0,3,2,1:T(8,128)(2,1)S(1)}, bf16[512,4,1,32]{0,3,2,1:T(8,128)(2,1)S(1)}) fusion(s32[4,32]{1,0:T(4,128)S(1)} %iota_add_fusion, s32[512]{0:T(512)S(1)} %iota_add_fusion.1), kind=kLoop, calls=%fused_computation.26 | loop fusion | flops 1245184 | bytes 264704 | tf_op jit(solution)/shard_map/convert
  2.7 0.0 copy-done
  2.7 0.3 fusion.10
  3.0 0.8 %pad_maximum_fusion = f32[8,2,256,32]{2,3,1,0:T(8,128)} fusion(f32[4,2,256,32]{2,3,1,0:T(8,128)S(1)} %bitcast.48), kind=kLoop, calls=%fused_computation.7 | loop fusion | flops 131072 | bytes 786432 | tf_op jit(solution)/shard_map/concatenate | solution.py:58
  3.8 7.5 %all-to-all-start = ((f32[8,2,256,32]{2,3,1,0:T(8,128)}), f32[8,2,256,32]{2,3,1,0:T(8,128)S(1)}, u32[]{:S(2)}, u32[]{:S(2)}) async-start(f32[8,2,256,32]{2,3,1,0:T(8,128)} %pad_maximum_fusion), calls=%async_computation | async-start | bytes 1048576 | tf_op jit(solution)/shard_map/all_to_all | solution.py:58
  11.3 11.7 %all-to-all-done = f32[8,2,256,32]{2,3,1,0:T(8,128)S(1)} async-done(((f32[8,2,256,32]{2,3,1,0:T(8,128)}), f32[8,2,256,32]{2,3,1,0:T(8,128)S(1)}, u32[]{:S(2)}, u32[]{:S(2)}) %all-to-all-start) | async-done | bytes 524320 | tf_op jit(solution)/shard_map/all_to_all | solution.py:58
  23.1 0.7 collective-permute-start.2
  23.7 0.0 collective-permute-done.2
  23.8 0.9 %broadcast_in_dim.5 = bf16[32,256,32]{1,2,0:T(8,128)(2,1)} broadcast(bf16[256,32]{0,1:T(8,128)(2,1)S(1)} %bitcast.55), dimensions={1,2} | broadcast | bytes 540672 | tf_op jit(solution)/shard_map/broadcast_in_dim | solution.py:39
  24.6 21.7 %all-to-all-start.1 = ((bf16[32,256,32]{1,2,0:T(8,128)(2,1)}), bf16[32,256,32]{1,2,0:T(8,128)(2,1)S(1)}, u32[]{:S(2)}, u32[]{:S(2)}) async-start(bf16[32,256,32]{1,2,0:T(8,128)(2,1)} %broadcast_in_dim.5), calls=%async_computation.1 | async-start | bytes 1048576 | tf_op jit(solution)/shard_map/all_to_all | solution.py:39
  46.4 0.1 collective-permute-start
  46.5 4.3 %collective-permute-done = bf16[2,256,32]{1,2,0:T(8,128)(2,1)S(1)} collective-permute-done((bf16[2,256,32]{1,2,0:T(8,128)(2,1)S(1)}, bf16[2,256,32]{1,2,0:T(8,128)(2,1)S(1)}, u32[]{:S(2)}, u32[]{:S(2)}) %collective-permute-start) | collective-permute-done | bytes 32800 | tf_op jit(solution)/shard_map/ppermute | solution.py:73
  50.7 0.1 collective-permute-start.1
  50.8 3.4 %collective-permute-done.1 = bf16[4,256,32]{1,2,0:T(8,128)(2,1)S(1)} collective-permute-done((bf16[4,256,32]{1,2,0:T(8,128)(2,1)S(1)}, bf16[4,256,32]{1,2,0:T(8,128)(2,1)S(1)}, u32[]{:S(2)}, u32[]{:S(2)}) %collective-permute-start.1) | collective-permute-done | bytes 65568 | tf_op jit(solution)/shard_map/ppermute | solution.py:73
  54.2 0.1 multiply_reduce_fusion.1
  54.3 8.6 %all-to-all-done.1 = bf16[32,256,32]{1,2,0:T(8,128)(2,1)S(1)} async-done(((bf16[32,256,32]{1,2,0:T(8,128)(2,1)}), bf16[32,256,32]{1,2,0:T(8,128)(2,1)S(1)}, u32[]{:S(2)}, u32[]{:S(2)}) %all-to-all-start.1) | async-done | bytes 524320 | tf_op jit(solution)/shard_map/all_to_all | solution.py:39
  62.9 0.1 multiply_reduce_fusion
  63.1 0.4 copy.11
  63.5 0.4 reshape.157
  63.9 3.3 %fusion.14 = (bf16[4,2,256,1024]{3,2,1,0:T(8,128)(2,1)}, f32[4,2,256,1024]{3,2,1,0:T(8,128)S(1)}) fusion(bf16[4,1024,64,1]{1,2,0,3:T(8,128)(2,1)S(1)} %reshape.157, bf16[4,1,256,64]{2,3,1,0:T(8,128)(2,1)S(1)} %maximum_bitcast_fusion, bf16[4,1,256,64]{2,3,1,0:T(8,128)(2,1)S(1)} %bitcast.45), kind=kOutput, calls=%fused_computation.38 | convolution fusion | flops 272760832 | bytes 13369344 | tf_op jit(solution)/shard_map/bpik,bjk->bpij/dot_general | solution.py:27
  67.2 2.5 %fusion.2 = f32[4,256,1024]{2,1,0:T(8,128)} fusion(f32[4,2,256,1024]{3,2,1,0:T(8,128)S(1)} %get-tuple-element.9, f32[4,1024]{1,0:T(4,128)S(1)} %bitcast.52, f32[4,256]{1,0:T(4,128)S(1)} %multiply_add_fusion), kind=kLoop, calls=%fused_computation.3 | loop fusion | flops 5242880 | bytes 12603392 | tf_op jit(solution)/shard_map/div | solution.py:32
  (12 shorter events, 0.2 us)
Async XLA Ops:
  0.6 2.1 %copy-start = (bf16[256,512]{1,0:T(8,128)(2,1)S(1)}, bf16[256,512]{1,0:T(8,128)(2,1)}, u32[]{:S(2)}) copy-start(bf16[256,512]{1,0:T(8,128)(2,1)} %param.2) | copy-start | bytes 786436
  3.8 19.2 %all-to-all-start = ((f32[8,2,256,32]{2,3,1,0:T(8,128)}), f32[8,2,256,32]{2,3,1,0:T(8,128)S(1)}, u32[]{:S(2)}, u32[]{:S(2)}) async-start(f32[8,2,256,32]{2,3,1,0:T(8,128)} %pad_maximum_fusion), calls=%async_computation | async-start | bytes 1048576 | tf_op jit(solution)/shard_map/all_to_all | solution.py:58
  23.1 0.7 collective-permute-start.2
  24.6 38.3 %all-to-all-start.1 = ((bf16[32,256,32]{1,2,0:T(8,128)(2,1)}), bf16[32,256,32]{1,2,0:T(8,128)(2,1)S(1)}, u32[]{:S(2)}, u32[]{:S(2)}) async-start(bf16[32,256,32]{1,2,0:T(8,128)(2,1)} %broadcast_in_dim.5), calls=%async_computation.1 | async-start | bytes 1048576 | tf_op jit(solution)/shard_map/all_to_all | solution.py:39
  46.4 4.4 %collective-permute-start = (bf16[2,256,32]{1,2,0:T(8,128)(2,1)S(1)}, bf16[2,256,32]{1,2,0:T(8,128)(2,1)S(1)}, u32[]{:S(2)}, u32[]{:S(2)}) collective-permute-start(bf16[2,256,32]{1,2,0:T(8,128)(2,1)S(1)} %reduce_sum.27), channel_id=1, source_target_pairs={{0,2},{1,3},{2,0},{3,1},{4,6},{5,7},{6,4},{7,5},{8,10},{9,11},{10,... | collective-permute-start | bytes 98312 | tf_op jit(solution)/shard_map/ppermute | solution.py:73
  50.7 3.5 %collective-permute-start.1 = (bf16[4,256,32]{1,2,0:T(8,128)(2,1)S(1)}, bf16[4,256,32]{1,2,0:T(8,128)(2,1)S(1)}, u32[]{:S(2)}, u32[]{:S(2)}) collective-permute-start(bf16[4,256,32]{1,2,0:T(8,128)(2,1)S(1)} %bitcast.49), channel_id=1, source_target_pairs={{0,1},{1,0},{2,3},{3,2},{4,5},{5,4},{6,7},{7,6},{8,9},{9,8},{10,11... | collective-permute-start | bytes 196616 | tf_op jit(solution)/shard_map/ppermute | solution.py:73
